TPU v7x, 768 devices: a whole 4x8x12 slice. The times are simulated.
768 devices in a mesh: section: 48 (over z, x), ctx: 16 (over y, core).
Axes of the slice: x: 4, y: 8, z: 12, core: 2. Of those that a mesh axis runs over, the one named last changes fastest.
Arguments:
- residual_flow: float32 [48, 2048, 2048], P('section', 'ctx'), may hold values from -18 to 18
- tiers_each_segment: int32 [48], P('section'), may hold values from 0 to 1, as said below
- resident_tile_order: int32 [32], replicated, may hold values from 0 to 31, each once
- normalizer_weight_entries: float32 [48, 1, 2048], P('section'), may hold values from 0.1 to 1.9
- lookup_map_weights: bfloat16 [48, 1, 2048, 512], P('section'), may hold values from -2 to 2
- content_map_weights: bfloat16 [48, 1, 2048, 512], P('section'), may hold values from -0.125 to 0.125
- softmax_warmth: float32 [48, 1, 16], P('section'), may hold values from 2 to 320
- attention_result_weight: float32 [48, 1, 2048], P('section'), may hold values from 0.5 to 2
Outputs:
- passed: float32 [48, 2048, 2048], P('section', 'ctx')
Inputs may be any that keep to these rules, and one draw needn't show every extreme that they name: `tiers_each_segment`: some section applies 1 layer and some none.
All inputs are finite; a program needn't handle non-finite values.
Results may differ from a plain program's by a relative error of at most 0.013.
Values may be sent and summed in bfloat16 or wider, within the bound.
No kernel may reach another device: no remote copies, remote signals or barrier semaphores. Data moves between devices by JAX's collectives and lax.ppermute only.
A program may use at most 64 MiB of HBM per device.

v0:
```python
from functools import partial

import jax
import jax.numpy as jnp
from jax import lax
from jax.sharding import PartitionSpec as P

H = 16
KEY_VALUE_HEADS = 4
ATTN_UNIT_WIDTH = 128


def passed_along(block, axis, distance):
    devices = range(lax.axis_size(axis))
    route = [((i - distance) % len(devices), i) for i in devices]
    return lax.ppermute(block, axis, route)


def head_norm(values):
    return values * lax.rsqrt(jnp.mean(values * values, axis=-1, keepdims=True) + 1e-05)


def row_positions(row_start, row_count, resident_tile_order, tok_rows):
    row_ids = row_start + jnp.arange(row_count, dtype=jnp.int32)
    half_rows = tok_rows // 2
    slot_ids = row_ids // tok_rows * 2 + row_ids % tok_rows // half_rows
    lookup = (
        slot_ids[:, None] == jnp.arange(resident_tile_order.shape[0], dtype=jnp.int32)[None, :]
    ).astype(jnp.int32)
    return jnp.sum(lookup * resident_tile_order[None, :], axis=1) * half_rows + row_ids % half_rows


def attend_block(
    running, pieces, row_start, queries, logit_multiplier, query_pos, resident_tile_order, tok_rows
):
    running_max, running_sum, running_acc = running
    key_piece, value_piece = pieces
    piece_rows = key_piece.shape[0]
    kv_heads = queries.shape[0]
    key_pos = row_positions(row_start, piece_rows, resident_tile_order, tok_rows)
    allowed = (key_pos[None, :] <= query_pos[:, None])[None, None, :, :]
    scores = (
        jnp.einsum(
            "cgqe,sce->cgqs",
            queries,
            key_piece.reshape(piece_rows, kv_heads, -1),
            preferred_element_type=jnp.float32,
        )
        * logit_multiplier
    )
    scores = jnp.where(allowed, scores, -1e30)
    new_max = jnp.maximum(running_max, jnp.max(scores, axis=-1))
    weights = jnp.where(allowed, jnp.exp(scores - new_max[..., None]), 0.0)
    new_sum = jnp.sum(weights, axis=-1)
    new_acc = jnp.einsum(
        "cgqs,sce->cgqe",
        weights.astype(jnp.bfloat16),
        value_piece.reshape(piece_rows, kv_heads, -1),
        preferred_element_type=jnp.float32,
    )
    return (new_max, new_sum, new_acc)


def local(
    residual_flow,
    tiers_each_segment,
    resident_tile_order,
    normalizer_weight_entries,
    lookup_map_weights,
    content_map_weights,
    softmax_warmth,
    attention_result_weight,
):
    tok_rows = residual_flow.shape[1]
    query_groups = H // KEY_VALUE_HEADS
    residual = residual_flow[0]
    query_pos = row_positions(
        lax.axis_index("ctx") * tok_rows, tok_rows, resident_tile_order, tok_rows
    )
    normed = (
        residual
        * lax.rsqrt(jnp.mean(residual * residual, axis=-1, keepdims=True) + 1e-05)
        * normalizer_weight_entries[0, 0]
    ).astype(jnp.bfloat16)
    keys_raw = jnp.dot(normed, lookup_map_weights[0, 0], preferred_element_type=jnp.float32)
    key_unit = (
        head_norm(keys_raw.reshape(tok_rows, KEY_VALUE_HEADS, ATTN_UNIT_WIDTH))
        .astype(jnp.bfloat16)
        .reshape(tok_rows, KEY_VALUE_HEADS * ATTN_UNIT_WIDTH)
    )
    values = jnp.dot(normed, content_map_weights[0, 0], preferred_element_type=jnp.float32).astype(
        jnp.bfloat16
    )
    queries = head_norm(
        normed.astype(jnp.float32).reshape(tok_rows, KEY_VALUE_HEADS, query_groups, ATTN_UNIT_WIDTH)
    ).astype(jnp.bfloat16)
    queries = jnp.transpose(queries, (1, 2, 0, 3))
    logit_multiplier = (softmax_warmth[0, 0] / ATTN_UNIT_WIDTH).reshape(
        KEY_VALUE_HEADS, query_groups, 1, 1
    )
    folder = partial(
        attend_block,
        queries=queries,
        logit_multiplier=logit_multiplier,
        query_pos=query_pos,
        resident_tile_order=resident_tile_order,
        tok_rows=tok_rows,
    )
    initial = (
        jnp.full((KEY_VALUE_HEADS, query_groups, tok_rows), -1e30, jnp.float32),
        jnp.zeros((KEY_VALUE_HEADS, query_groups, tok_rows), jnp.float32),
        jnp.zeros((KEY_VALUE_HEADS, query_groups, tok_rows, ATTN_UNIT_WIDTH), jnp.float32),
    )
    running = folder(
        initial,
        (
            lax.all_gather(key_unit, "ctx", axis=0, tiled=True),
            lax.all_gather(values, "ctx", axis=0, tiled=True),
        ),
        jnp.int32(0),
    )
    mixed_out = running[2] / running[1][..., None]
    mixed_rows = jnp.transpose(mixed_out, (2, 0, 1, 3)).reshape(
        tok_rows, KEY_VALUE_HEADS * query_groups * ATTN_UNIT_WIDTH
    )
    updated = residual + attention_result_weight[0, 0] * mixed_rows
    residual = jnp.where(0 < tiers_each_segment[0], updated, residual)
    return passed_along(residual[None], "section", 1)


def solution(mesh):
    in_specs = (
        P("section", "ctx", None),
        P("section"),
        P(),
        P("section", None, None),
        P("section", None, None, None),
        P("section", None, None, None),
        P("section", None, None),
        P("section", None, None),
    )
    out_specs = P("section", "ctx", None)
    return jax.shard_map(local, mesh=mesh, in_specs=in_specs, out_specs=out_specs, check_vma=False)
```

profile of v0, /device:TPU:1, one launch (start us, length us, event | category | flops | bytes accessed | tf_op | source)
XLA Modules:
  0.0 173.3 jit_solution(15887718447238768419)
XLA Ops:
  6.5 0.0 copy-start
  6.5 0.0 all-gather.3.cloned.1.call-start
  6.5 1.5 multiply_reduce_fusion
  8.1 4.0 %copy.25 = bf16[512,2048]{1,0:T(8,128)(2,1)} copy(bf16[512,2048]{0,1:T(8,128)(2,1)} %bitcast.47) | data formatting | bytes 4194304 | tf_op jit(solution)/shard_map/dot_general | solution.py:85
  12.1 2.7 %multiply_reduce_fusion.1 = (f32[128,4]{0,1:T(4,128)S(1)}, f32[128,4,128]{0,2,1:T(8,128)S(1)}) fusion(bf16[4,128,2048]{2,1,0:T(8,128)(2,1)} %bitcast.46, f32[2048]{0:T(1024)} %bitcast.52, f32[1,128,2048]{2,1,0:T(8,128)} %param.8, f32[128]{0:T(128)S(1)} %add_rsqrt_fusion.2), kind=kOutput, calls=%fused_computation.30 | convolution fusion | flops 269352448 | bytes 3418624 | tf_op jit(solution)/shard_map/dot_general | solution.py:85
  14.8 0.7 multiply_convert_fusion.1
  15.5 0.0 all-gather.3.cloned.1.call-update
  15.5 0.0 all-gather.5.cloned.1.call-start
  15.6 0.0 copy-done
  15.6 2.4 %fusion.11 = bf16[128,512]{1,0:T(8,128)(2,1)} fusion(bf16[1,1,2048,512]{3,2,1,0:T(8,128)(2,1)S(1)} %copy-done, f32[1,128,2048]{2,1,0:T(8,128)} %param.8, f32[2048]{0:T(1024)} %bitcast.53, f32[128]{0:T(128)S(1)} %add_rsqrt_fusion.2), kind=kOutput, calls=%fused_computation.13 | convolution fusion | flops 269287424 | bytes 3285504 | tf_op jit(solution)/shard_map/dot_general | solution.py:91
  18.0 0.0 all-gather.5.cloned.1.call-update
  18.0 1.9 %squeeze.11 = f32[128,4,4,128]{3,2,1,0:T(4,128)S(1)} reshape(f32[1,128,2048]{2,1,0:T(8,128)} %param.8) | data formatting | bytes 2097152 | tf_op jit(solution)/shard_map/squeeze | solution.py:76
  20.0 0.7 multiply_reduce_fusion.2
  20.6 0.1 div.95
  21.4 0.7 select_reduce_fusion.1
  22.1 0.8 select_reduce_fusion
  22.9 1.1 fusion.14
  24.1 0.2 broadcast_compare_fusion
  24.3 45.5 %all-gather.3.cloned.1.call-done = bf16[2048,512]{0,1:T(8,128)(2,1)} async-done(((bf16[128,512]{0,1:T(8,128)(2,1)}), bf16[2048,512]{0,1:T(8,128)(2,1)}) %all-gather.3.cloned.1.call-update) | async-done | bytes 2097168 | tf_op jit(solution)/shard_map/all_gather | solution.py:117
  69.8 4.7 %fusion = (f32[4,4,128]{2,1,0:T(4,128)S(1)}, f32[4,4,128,2048]{3,2,1,0:T(8,128)S(1)}) fusion(f32[4,4]{1,0:T(4,128)S(1)} %div.95, pred[128,2048]{1,0:T(8,128)(4,1)S(1)} %broadcast_compare_fusion, bf16[2048,4,128,1]{0,2,3,1:T(8,128)(2,1)} %bitcast.49, f32[128,4,4]{0,2,1:T(4,128)S(1)} %add_rsqrt_fusion, f32[4,4,128]{2,1,0:T(4,128)} %bitcast.55, ...), kind=kOutput, calls=%fused_computation.2 | convolution fusion | flops 1087895552 | bytes 20210240 | tf_op jit(solution)/shard_map/cgqe,sce->cgqs/dot_general | solution.py:43
  74.5 0.0 copy-start.1
  74.5 5.7 %copy-done.1 = f32[4,4,128,2048]{3,2,1,0:T(8,128)} copy-done((f32[4,4,128,2048]{3,2,1,0:T(8,128)}, f32[4,4,128,2048]{3,2,1,0:T(8,128)S(1)}, u32[]{:S(2)}) %copy-start.1) | copy-done | bytes 16777240
  80.2 5.1 %fusion.1 = f32[4,4,128]{2,1,0:T(4,128)S(1)} fusion(f32[4,4,128,2048]{3,2,1,0:T(8,128)S(1)} %get-tuple-element.8, f32[4,4,128]{2,1,0:T(4,128)S(1)} %broadcast_maximum_fusion, f32[4,4]{1,0:T(4,128)S(1)} %div.95, pred[128,2048]{1,0:T(8,128)(4,1)S(1)} %broadcast_compare_fusion), kind=kLoop, calls=%fused_computation.3 | loop fusion | flops 20969472 | bytes 17055808 | tf_op jit(solution)/shard_map/reduce_sum | solution.py:54
  85.3 30.9 %all-gather.5.cloned.1.call-done = bf16[2048,512]{1,0:T(8,128)(2,1)} async-done(((bf16[128,512]{1,0:T(8,128)(2,1)}), bf16[2048,512]{1,0:T(8,128)(2,1)}) %all-gather.5.cloned.1.call-update) | async-done | bytes 2097168 | tf_op jit(solution)/shard_map/all_gather | solution.py:118
  116.2 3.9 %copy.28 = bf16[2048,512]{0,1:T(8,128)(2,1)} copy(bf16[2048,512]{1,0:T(8,128)(2,1)} %all-gather.5.cloned.1.call-done) | data formatting | bytes 4194304 | tf_op jit(solution)/shard_map/reshape | solution.py:58
  120.1 0.0 copy-start.2
  120.1 0.0 copy-start.3
  120.1 9.4 %fusion.18 = f32[128,4,4,128]{0,3,2,1:T(8,128)} fusion(bf16[2048,4,128,1]{0,2,3,1:T(8,128)(2,1)} %bitcast.48, f32[4,4,128,2048]{3,2,1,0:T(8,128)} %copy-done.1, f32[4,4,128]{2,1,0:T(4,128)S(1)} %broadcast_maximum_fusion, f32[4,4]{1,0:T(4,128)S(1)} %div.95, pred[128,2048]{1,0:T(8,128)(4,1)S(1)} %broadcast_compare_fusion, f32[128,4,4]{0,2,1:T(4,128)S(1)} %bitcast.57), kind=kOutput, calls=%fused_computation.21 | convolution fusion | flops 1094975488 | bytes 20201536 | tf_op jit(solution)/shard_map/cgqs,sce->cgqe/dot_general | solution.py:55
  129.6 2.5 %copy.22 = f32[1,128,2048]{2,1,0:T(8,128)} copy(f32[1,128,2048]{1,2,0:T(8,128)} %bitcast.50) | data formatting | bytes 2097152 | tf_op jit(solution)/shard_map/reshape | solution.py:123
  132.1 0.0 copy-done.2
  132.1 0.0 copy-done.3
  132.1 1.4 add_select_fusion
  133.5 3.3 %collective-permute-start = (f32[1,128,2048]{2,1,0:T(8,128)S(1)}, f32[1,128,2048]{2,1,0:T(8,128)S(1)}, u32[]{:S(2)}, u32[]{:S(2)}) collective-permute-start(f32[1,128,2048]{2,1,0:T(8,128)S(1)} %add_select_fusion), channel_id=1, source_target_pairs={{752,0},{0,16},{16,32},{32,48},{48,64},{64,80},{80,96},{96,112},{1... | collective-permute-start | bytes 3145736 | tf_op jit(solution)/shard_map/ppermute | solution.py:16
  136.8 28.7 %collective-permute-done = f32[1,128,2048]{2,1,0:T(8,128)S(1)} collective-permute-done((f32[1,128,2048]{2,1,0:T(8,128)S(1)}, f32[1,128,2048]{2,1,0:T(8,128)S(1)}, u32[]{:S(2)}, u32[]{:S(2)}) %collective-permute-start) | collective-permute-done | bytes 1048608 | tf_op jit(solution)/shard_map/ppermute | solution.py:16
  165.5 1.0 copy.43
  (8 shorter events, 0.1 us)
Async XLA Ops:
  6.5 9.0 %copy-start = (bf16[1,1,2048,512]{3,2,1,0:T(8,128)(2,1)S(1)}, bf16[1,1,2048,512]{3,2,1,0:T(8,128)(2,1)}, u32[]{:S(2)}) copy-start(bf16[1,1,2048,512]{3,2,1,0:T(8,128)(2,1)} %param.13) | copy-start | bytes 6291460
  6.5 63.2 %all-gather.3.cloned.1.call-start = ((), (), s32[]{:S(2)}) async-start(), calls=%async_computation | async-start | bytes 2228224 | tf_op jit(solution)/shard_map/all_gather | solution.py:117
  15.5 100.7 %all-gather.5.cloned.1.call-start = ((), (), s32[]{:S(2)}) async-start(), calls=%async_computation.1 | async-start | bytes 2228224 | tf_op jit(solution)/shard_map/all_gather | solution.py:118
  74.5 5.7 %copy-start.1 = (f32[4,4,128,2048]{3,2,1,0:T(8,128)}, f32[4,4,128,2048]{3,2,1,0:T(8,128)S(1)}, u32[]{:S(2)}) copy-start(f32[4,4,128,2048]{3,2,1,0:T(8,128)S(1)} %get-tuple-element.8) | copy-start | bytes 50331652
  120.1 12.0 %copy-start.2 = (f32[1,128,2048]{2,1,0:T(8,128)S(1)}, f32[1,128,2048]{2,1,0:T(8,128)}, u32[]{:S(2)}) copy-start(f32[1,128,2048]{2,1,0:T(8,128)} %param.8) | copy-start | bytes 3145732
  120.1 12.0 %copy-start.3 = (f32[1,1,2048]{2,1,0:T(1,128)S(1)}, f32[1,1,2048]{2,1,0:T(1,128)}, u32[]{:S(2)}) copy-start(f32[1,1,2048]{2,1,0:T(1,128)} %param.15) | copy-start | bytes 24580
  133.5 32.0 %collective-permute-start = (f32[1,128,2048]{2,1,0:T(8,128)S(1)}, f32[1,128,2048]{2,1,0:T(8,128)S(1)}, u32[]{:S(2)}, u32[]{:S(2)}) collective-permute-start(f32[1,128,2048]{2,1,0:T(8,128)S(1)} %add_select_fusion), channel_id=1, source_target_pairs={{752,0},{0,16},{16,32},{32,48},{48,64},{64,80},{80,96},{96,112},{1... | collective-permute-start | bytes 3145736 | tf_op jit(solution)/shard_map/ppermute | solution.py:16
Sparse Core Ops, SparseCore 0:
  15.6 54.0 all-gather.2
  72.2 43.9 all-gather.4
where the time goes:
time: 174 us; the launch traced here: 173 us
  waiting for transfers between devices  105 us (60%)
  matrix products  19.3 us (11%)
  local copies, waits for them, and re-layouts  19.2 us (11%)
  between operations  14.2 us (8%)
  other arithmetic  12.2 us (7%)
  starting transfers between devices  3.3 us (2%)
    all_gather x1, waiting for transfers between devices, local(): lax.all_gather(key_unit, 'ctx', axis=0, tiled=True)  45.5 us
    all_gather x1, waiting for transfers between devices, local(): lax.all_gather(values, 'ctx', axis=0, tiled=True)  30.9 us
    ppermute x1, waiting for transfers between devices, passed_along(): return lax.ppermute(block, axis, route)  28.7 us
    dot_general x1, matrix products, attend_block(): jnp.einsum('cgqs,sce->cgqe', weights.astype(jnp.bfloat16), value_piece.re...  9.43 us
    unnamed x9, local copies, waits for them, and re-layouts  6.67 us
    reduce_sum x1, other arithmetic, attend_block(): new_sum = jnp.sum(weights, axis=-1)  5.06 us
    dot_general x1, matrix products, attend_block(): jnp.einsum('cgqe,sce->cgqs', queries, key_piece.reshape(piece_rows, kv_he...  4.74 us
    dot_general x1, local copies, waits for them, and re-layouts, local(): jnp.dot(normed, lookup_map_weights[0, 0], preferred_element_type=jnp.floa...  3.99 us
  transfers between devices with their start and end apart: 3, of which 3 were waited for; matrix products, arithmetic and copies ran while one was open for 10% of the time, Pallas kernels for 0%

commit v1 on v0

--- a/solution.py
+++ b/solution.py
@@ -1,5 +1,3 @@
-from functools import partial
-
 import jax
 import jax.numpy as jnp
 from jax import lax
@@ -30,32 +28,27 @@
     return jnp.sum(lookup * resident_tile_order[None, :], axis=1) * half_rows + row_ids % half_rows
 
 
-def attend_block(
-    running, pieces, row_start, queries, logit_multiplier, query_pos, resident_tile_order, tok_rows
-):
+def attend_block(running, block, key_pos, queries, logit_multiplier, query_pos):
     running_max, running_sum, running_acc = running
-    key_piece, value_piece = pieces
-    piece_rows = key_piece.shape[0]
+    rows = block.shape[0]
     kv_heads = queries.shape[0]
-    key_pos = row_positions(row_start, piece_rows, resident_tile_order, tok_rows)
+    kvd = block.shape[1] // 2
+    key_piece = block[:, :kvd].reshape(rows, kv_heads, -1)
+    value_piece = block[:, kvd:].reshape(rows, kv_heads, -1)
     allowed = (key_pos[None, :] <= query_pos[:, None])[None, None, :, :]
     scores = (
-        jnp.einsum(
-            "cgqe,sce->cgqs",
-            queries,
-            key_piece.reshape(piece_rows, kv_heads, -1),
-            preferred_element_type=jnp.float32,
-        )
+        jnp.einsum("cgqe,sce->cgqs", queries, key_piece, preferred_element_type=jnp.float32)
         * logit_multiplier
     )
     scores = jnp.where(allowed, scores, -1e30)
     new_max = jnp.maximum(running_max, jnp.max(scores, axis=-1))
     weights = jnp.where(allowed, jnp.exp(scores - new_max[..., None]), 0.0)
-    new_sum = jnp.sum(weights, axis=-1)
-    new_acc = jnp.einsum(
+    scale = jnp.exp(running_max - new_max)
+    new_sum = running_sum * scale + jnp.sum(weights, axis=-1)
+    new_acc = running_acc * scale[..., None] + jnp.einsum(
         "cgqs,sce->cgqe",
         weights.astype(jnp.bfloat16),
-        value_piece.reshape(piece_rows, kv_heads, -1),
+        value_piece,
         preferred_element_type=jnp.float32,
     )
     return (new_max, new_sum, new_acc)
@@ -73,10 +66,14 @@
 ):
     tok_rows = residual_flow.shape[1]
     query_groups = H // KEY_VALUE_HEADS
+    n_ctx = lax.axis_size("ctx")
+    n_ring = n_ctx // 2
+    me = lax.axis_index("ctx")
+    chip = me // 2
+    core = me % 2
+    step_dir = 1 - 2 * core
     residual = residual_flow[0]
-    query_pos = row_positions(
-        lax.axis_index("ctx") * tok_rows, tok_rows, resident_tile_order, tok_rows
-    )
+    query_pos = row_positions(me * tok_rows, tok_rows, resident_tile_order, tok_rows)
     normed = (
         residual
         * lax.rsqrt(jnp.mean(residual * residual, axis=-1, keepdims=True) + 1e-05)
@@ -98,27 +95,42 @@
     logit_multiplier = (softmax_warmth[0, 0] / ATTN_UNIT_WIDTH).reshape(
         KEY_VALUE_HEADS, query_groups, 1, 1
     )
-    folder = partial(
-        attend_block,
-        queries=queries,
-        logit_multiplier=logit_multiplier,
-        query_pos=query_pos,
-        resident_tile_order=resident_tile_order,
-        tok_rows=tok_rows,
-    )
-    initial = (
+    own_block = jnp.concatenate([key_unit, values], axis=1)
+
+    ring_route = [
+        (i, ((i // 2 + (1 if i % 2 == 0 else -1)) % n_ring) * 2 + i % 2) for i in range(n_ctx)
+    ]
+    partner_route = [(i, i ^ 1) for i in range(n_ctx)]
+
+    def origin_pos(origin):
+        return row_positions(origin * tok_rows, tok_rows, resident_tile_order, tok_rows)
+
+    def fold(running, block, origin):
+        return attend_block(
+            running, block, origin_pos(origin), queries, logit_multiplier, query_pos
+        )
+
+    running = (
         jnp.full((KEY_VALUE_HEADS, query_groups, tok_rows), -1e30, jnp.float32),
         jnp.zeros((KEY_VALUE_HEADS, query_groups, tok_rows), jnp.float32),
         jnp.zeros((KEY_VALUE_HEADS, query_groups, tok_rows, ATTN_UNIT_WIDTH), jnp.float32),
     )
-    running = folder(
-        initial,
-        (
-            lax.all_gather(key_unit, "ctx", axis=0, tiled=True),
-            lax.all_gather(values, "ctx", axis=0, tiled=True),
-        ),
-        jnp.int32(0),
-    )
+    ring_block = own_block
+    pending = None
+    for step in range(n_ring):
+        ring_origin = ((chip - step * step_dir) % n_ring) * 2 + core
+        partner_origin = ((chip + step * step_dir) % n_ring) * 2 + (1 - core)
+        partner_block = lax.ppermute(ring_block, "ctx", partner_route)
+        next_block = None
+        if step < n_ring - 1:
+            next_block = lax.ppermute(ring_block, "ctx", ring_route)
+        running = fold(running, ring_block, ring_origin)
+        if pending is not None:
+            running = fold(running, *pending)
+        pending = (partner_block, partner_origin)
+        ring_block = next_block
+    running = fold(running, *pending)
+
     mixed_out = running[2] / running[1][..., None]
     mixed_rows = jnp.transpose(mixed_out, (2, 0, 1, 3)).reshape(
         tok_rows, KEY_VALUE_HEADS * query_groups * ATTN_UNIT_WIDTH

time: 174 us -> 218 us (1.25)
  waiting for transfers between devices: 105 us -> 30.7 us
  local copies, waits for them, and re-layouts: 19.2 us -> 68.4 us
  starting transfers between devices: 3.3 us -> 52.1 us
  matrix products: 19.3 us -> 47.8 us
  between operations: 14.2 us -> 2.32 us
  other arithmetic: 12.2 us -> 15 us
    all_gather x2 -> x0, waiting for transfers between devices: 76.4 us -> none  [the longest x1 45.5 us: local(): lax.all_gather(key_unit, 'ctx', axis=0, tiled=True)]
    ppermute x0 -> x15, starting transfers between devices: none -> 50.1 us  [the longest x7 27.6 us: local(): next_block = lax.ppermute(ring_block, 'ctx', ring_route)]
    dot_general x2 -> x32, matrix products: 14.2 us -> 44.9 us  [the longest x16 38.8 us: attend_block(): jnp.einsum('cgqe,sce->cgqs', queries, key_piece, preferred_element_type=j...]
    reshape x1 -> x32, local copies, waits for them, and re-layouts: 3.95 us -> 33.2 us  [the longest x16 16.7 us: attend_block(): value_piece = block[:, kvd:].reshape(rows, kv_heads, -1)]
    slice x0 -> x15, local copies, waits for them, and re-layouts: none -> 20.9 us  [attend_block(): value_piece = block[:, kvd:].reshape(rows, kv_heads, -1)]
    unnamed x9 -> x157, local copies, waits for them, and re-layouts: 6.67 us -> 5.86 us
    reduce_sum x1 -> x16, other arithmetic: 5.06 us -> 4.6 us  [attend_block(): new_sum = running_sum * scale + jnp.sum(weights, axis=-1)]
  transfers between devices with their start and end apart: 3 -> 16, of which waited for: 3 -> 1; matrix products, arithmetic and copies ran while one was open for 10% -> 26% of each run, Pallas kernels for 0% -> 0%
where the time goes in v1:
time: 218 us; the launch traced here: 216 us
  local copies, waits for them, and re-layouts  68.4 us (31%)
  starting transfers between devices  52.1 us (24%)
  matrix products  47.8 us (22%)
  waiting for transfers between devices  30.7 us (14%)
  other arithmetic  15 us (7%)
  between operations  2.32 us (1%)
    dot_general x16, matrix products, attend_block(): jnp.einsum('cgqe,sce->cgqs', queries, key_piece, preferred_element_type=j...  38.8 us
    ppermute x1, waiting for transfers between devices, passed_along(): return lax.ppermute(block, axis, route)  30.7 us
    ppermute x7, starting transfers between devices, local(): next_block = lax.ppermute(ring_block, 'ctx', ring_route)  27.6 us
    ppermute x8, starting transfers between devices, local(): partner_block = lax.ppermute(ring_block, 'ctx', partner_route)  22.5 us
    slice x15, local copies, waits for them, and re-layouts, attend_block(): value_piece = block[:, kvd:].reshape(rows, kv_heads, -1)  20.9 us
    reshape x16, local copies, waits for them, and re-layouts, attend_block(): value_piece = block[:, kvd:].reshape(rows, kv_heads, -1)  16.7 us
    reshape x15, local copies, waits for them, and re-layouts, attend_block(): key_piece = block[:, :kvd].reshape(rows, kv_heads, -1)  16.5 us
    dot_general x16, matrix products, attend_block(): jnp.einsum('cgqs,sce->cgqe', weights.astype(jnp.bfloat16), value_piece, p...  6.05 us
  transfers between devices with their start and end apart: 16, of which 1 were waited for; matrix products, arithmetic and copies ran while one was open for 26% of the time, Pallas kernels for 0%

profile of v1, /device:TPU:1, one launch (start us, length us, event | category | flops | bytes accessed | tf_op | source)
XLA Modules:
  0.0 216.3 jit_solution(10685403826456940732)
XLA Ops:
  1.6 4.1 %copy.161 = bf16[512,2048]{1,0:T(8,128)(2,1)} copy(bf16[512,2048]{0,1:T(8,128)(2,1)} %bitcast.476) | data formatting | bytes 4194304 | tf_op jit(solution)/shard_map/dot_general | solution.py:82
  5.6 2.4 %multiply_reduce_fusion.1 = (f32[128,4]{0,1:T(4,128)S(1)}, f32[128,4,128]{0,2,1:T(8,128)S(1)}) fusion(bf16[4,128,2048]{2,1,0:T(8,128)(2,1)} %bitcast.475, f32[2048]{0:T(1024)S(1)} %bitcast.509, f32[1,128,2048]{2,1,0:T(8,128)S(1)} %copy-done.1, f32[128]{0:T(128)S(1)} %add_rsqrt_fusion.2), kind=kOutput, calls=%fused_computation.195 | convolution fusion | flops 269352448 | bytes 3418624 | tf_op jit(solution)/shard_map/dot_general | solution.py:82
  9.4 5.9 %collective-permute-start = (bf16[128,1024]{1,0:T(8,128)(2,1)}, bf16[128,1024]{1,0:T(8,128)(2,1)}, u32[]{:S(2)}, u32[]{:S(2)}) collective-permute-start(bf16[128,1024]{1,0:T(8,128)(2,1)} %pad_maximum_fusion), channel_id=1, source_target_pairs={{0,2},{1,15},{2,4},{3,1},{4,6},{5,3},{6,8},{7,5},{8,10},{9,7},{10,... | collective-permute-start | bytes 786440 | tf_op jit(solution)/shard_map/ppermute | solution.py:126
  15.4 8.4 %collective-permute-start.1 = (bf16[128,1024]{1,0:T(8,128)(2,1)}, bf16[128,1024]{1,0:T(8,128)(2,1)}, u32[]{:S(2)}, u32[]{:S(2)}) collective-permute-start(bf16[128,1024]{1,0:T(8,128)(2,1)} %pad_maximum_fusion), channel_id=1, source_target_pairs={{0,1},{1,0},{2,3},{3,2},{4,5},{5,4},{6,7},{7,6},{8,9},{9,8},{10,11... | collective-permute-start | bytes 786440 | tf_op jit(solution)/shard_map/ppermute | solution.py:123
  24.0 1.7 squeeze.11
  35.3 1.9 fusion.271
  37.2 4.8 %collective-permute-start.2 = (bf16[128,1024]{1,0:T(8,128)(2,1)}, bf16[128,1024]{1,0:T(8,128)(2,1)}, u32[]{:S(2)}, u32[]{:S(2)}) collective-permute-start(bf16[128,1024]{1,0:T(8,128)(2,1)} %collective-permute-done), channel_id=1, source_target_pairs={{0,2},{1,15},{2,4},{3,1},{4,6},{5,3},{6,8},{7,5},{8,10},{9,7},{10,... | collective-permute-start | bytes 786440 | tf_op jit(solution)/shard_map/ppermute | solution.py:126
  42.1 1.9 collective-permute-start.3
  44.0 1.9 fusion.272
  48.9 2.8 %fusion.269 = (f32[4,4,128]{2,1,0:T(4,128)}, f32[4,4,128,128]{2,3,1,0:T(8,128)}) fusion(f32[4,4]{1,0:T(4,128)S(1)} %div.342, bf16[4,4,128,128]{3,2,1,0:T(8,128)(2,1)S(1)} %fusion.105, bf16[128,4,128,1]{2,1,0,3:T(4,128)(2,1)} %bitcast.504, pred[128,128]{0,1:T(8,128)(4,1)} %get-tuple-element.94), kind=kOutput, calls=%fused_computation.611 | convolution fusion | flops 67893248 | bytes 1728576 | tf_op jit(solution)/shard_map/cgqe,sce->cgqs/dot_general | solution.py:40
  51.7 2.9 %collective-permute-start.4 = (bf16[128,1024]{1,0:T(8,128)(2,1)}, bf16[128,1024]{1,0:T(8,128)(2,1)}, u32[]{:S(2)}, u32[]{:S(2)}) collective-permute-start(bf16[128,1024]{1,0:T(8,128)(2,1)} %collective-permute-done.2), channel_id=1, source_target_pairs={{0,2},{1,15},{2,4},{3,1},{4,6},{5,3},{6,8},{7,5},{8,10},{9,7},{10,... | collective-permute-start | bytes 786440 | tf_op jit(solution)/shard_map/ppermute | solution.py:126
  54.6 1.9 collective-permute-start.5
  56.5 2.6 %fusion.270 = (f32[4,4,128]{2,1,0:T(4,128)}, f32[4,4,128,128]{2,3,1,0:T(8,128)}) fusion(f32[4,4]{1,0:T(4,128)S(1)} %div.342, bf16[4,4,128,128]{3,2,1,0:T(8,128)(2,1)S(1)} %fusion.105, bf16[128,4,128,1]{2,1,0,3:T(4,128)(2,1)S(1)} %bitcast.497, pred[128,128]{0,1:T(8,128)(4,1)} %get-tuple-element.93), kind=kOutput, calls=%fused_computation.612 | convolution fusion | flops 67893248 | bytes 1728576 | tf_op jit(solution)/shard_map/cgqe,sce->cgqs/dot_general | solution.py:40
  63.4 2.8 %fusion.267 = (f32[4,4,128]{2,1,0:T(4,128)}, f32[4,4,128,128]{2,3,1,0:T(8,128)}) fusion(f32[4,4]{1,0:T(4,128)S(1)} %div.342, bf16[4,4,128,128]{3,2,1,0:T(8,128)(2,1)S(1)} %fusion.105, bf16[128,4,128,1]{2,1,0,3:T(4,128)(2,1)} %bitcast.505, pred[128,128]{0,1:T(8,128)(4,1)} %get-tuple-element.96), kind=kOutput, calls=%fused_computation.609 | convolution fusion | flops 67893248 | bytes 1728576 | tf_op jit(solution)/shard_map/cgqe,sce->cgqs/dot_general | solution.py:40
  66.2 4.4 %collective-permute-start.6 = (bf16[128,1024]{1,0:T(8,128)(2,1)}, bf16[128,1024]{1,0:T(8,128)(2,1)}, u32[]{:S(2)}, u32[]{:S(2)}) collective-permute-start(bf16[128,1024]{1,0:T(8,128)(2,1)} %collective-permute-done.4), channel_id=1, source_target_pairs={{0,2},{1,15},{2,4},{3,1},{4,6},{5,3},{6,8},{7,5},{8,10},{9,7},{10,... | collective-permute-start | bytes 786440 | tf_op jit(solution)/shard_map/ppermute | solution.py:126
  70.5 1.9 collective-permute-start.7
  72.5 2.8 %fusion.268 = (f32[4,4,128]{2,1,0:T(4,128)}, f32[4,4,128,128]{2,3,1,0:T(8,128)}) fusion(f32[4,4]{1,0:T(4,128)S(1)} %div.342, bf16[4,4,128,128]{3,2,1,0:T(8,128)(2,1)S(1)} %fusion.105, bf16[128,4,128,1]{2,1,0,3:T(4,128)(2,1)} %bitcast.498, pred[128,128]{0,1:T(8,128)(4,1)} %get-tuple-element.95), kind=kOutput, calls=%fused_computation.610 | convolution fusion | flops 67893248 | bytes 1728576 | tf_op jit(solution)/shard_map/cgqe,sce->cgqs/dot_general | solution.py:40
  76.5 1.7 fusion.253
  79.8 1.7 fusion.254
  83.0 2.8 %fusion.265 = (f32[4,4,128]{2,1,0:T(4,128)}, f32[4,4,128,128]{2,3,1,0:T(8,128)}) fusion(f32[4,4]{1,0:T(4,128)S(1)} %div.342, bf16[4,4,128,128]{3,2,1,0:T(8,128)(2,1)S(1)} %fusion.105, bf16[128,4,128,1]{2,1,0,3:T(4,128)(2,1)} %bitcast.506, pred[128,128]{0,1:T(8,128)(4,1)} %get-tuple-element.98), kind=kOutput, calls=%fused_computation.607 | convolution fusion | flops 67893248 | bytes 1728576 | tf_op jit(solution)/shard_map/cgqe,sce->cgqs/dot_general | solution.py:40
  85.8 2.9 %collective-permute-start.8 = (bf16[128,1024]{1,0:T(8,128)(2,1)}, bf16[128,1024]{1,0:T(8,128)(2,1)}, u32[]{:S(2)}, u32[]{:S(2)}) collective-permute-start(bf16[128,1024]{1,0:T(8,128)(2,1)} %collective-permute-done.6), channel_id=1, source_target_pairs={{0,2},{1,15},{2,4},{3,1},{4,6},{5,3},{6,8},{7,5},{8,10},{9,7},{10,... | collective-permute-start | bytes 786440 | tf_op jit(solution)/shard_map/ppermute | solution.py:126
  88.7 1.9 collective-permute-start.9
  90.6 2.8 %fusion.266 = (f32[4,4,128]{2,1,0:T(4,128)}, f32[4,4,128,128]{2,3,1,0:T(8,128)}) fusion(f32[4,4]{1,0:T(4,128)S(1)} %div.342, bf16[4,4,128,128]{3,2,1,0:T(8,128)(2,1)S(1)} %fusion.105, bf16[128,4,128,1]{2,1,0,3:T(4,128)(2,1)} %bitcast.499, pred[128,128]{0,1:T(8,128)(4,1)} %get-tuple-element.97), kind=kOutput, calls=%fused_computation.608 | convolution fusion | flops 67893248 | bytes 1728576 | tf_op jit(solution)/shard_map/cgqe,sce->cgqs/dot_general | solution.py:40
  93.4 1.7 copy.185
  95.1 1.7 copy.188
  96.7 1.7 fusion.252
  100.0 1.7 fusion.251
  103.3 2.9 %fusion.264 = (f32[4,4,128]{2,1,0:T(4,128)}, f32[4,4,128,128]{2,3,1,0:T(8,128)}) fusion(f32[4,4]{1,0:T(4,128)S(1)} %div.342, bf16[4,4,128,128]{3,2,1,0:T(8,128)(2,1)S(1)} %fusion.105, bf16[128,4,128,1]{2,1,0,3:T(4,128)(2,1)} %bitcast.501, pred[128,128]{0,1:T(8,128)(4,1)} %get-tuple-element.99), kind=kOutput, calls=%fused_computation.606 | convolution fusion | flops 67893248 | bytes 1728576 | tf_op jit(solution)/shard_map/cgqe,sce->cgqs/dot_general | solution.py:40
  106.2 4.4 %collective-permute-start.10 = (bf16[128,1024]{1,0:T(8,128)(2,1)}, bf16[128,1024]{1,0:T(8,128)(2,1)}, u32[]{:S(2)}, u32[]{:S(2)}) collective-permute-start(bf16[128,1024]{1,0:T(8,128)(2,1)} %collective-permute-done.8), channel_id=1, source_target_pairs={{0,2},{1,15},{2,4},{3,1},{4,6},{5,3},{6,8},{7,5},{8,10},{9,7},{10,... | collective-permute-start | bytes 786440 | tf_op jit(solution)/shard_map/ppermute | solution.py:126
  110.6 1.9 collective-permute-start.11
  112.5 2.8 %fusion.263 = (f32[4,4,128]{2,1,0:T(4,128)}, f32[4,4,128,128]{2,3,1,0:T(8,128)}) fusion(f32[4,4]{1,0:T(4,128)S(1)} %div.342, bf16[4,4,128,128]{3,2,1,0:T(8,128)(2,1)S(1)} %fusion.105, bf16[128,4,128,1]{2,1,0,3:T(4,128)(2,1)} %bitcast.500, pred[128,128]{0,1:T(8,128)(4,1)} %get-tuple-element.100), kind=kOutput, calls=%fused_computation.605 | convolution fusion | flops 67893248 | bytes 1728576 | tf_op jit(solution)/shard_map/cgqe,sce->cgqs/dot_general | solution.py:40
  116.9 1.7 copy.194
  118.6 1.7 fusion.250
  121.9 1.7 fusion.249
  125.2 2.3 %fusion.262 = (f32[4,4,128]{2,1,0:T(4,128)S(1)}, f32[4,4,128,128]{2,3,1,0:T(8,128)}) fusion(f32[4,4]{1,0:T(4,128)S(1)} %div.342, bf16[4,4,128,128]{3,2,1,0:T(8,128)(2,1)S(1)} %fusion.105, bf16[128,4,128,1]{2,1,0,3:T(4,128)(2,1)} %bitcast.502, pred[128,128]{0,1:T(8,128)(4,1)} %get-tuple-element.101), kind=kOutput, calls=%fused_computation.604 | convolution fusion | flops 67893248 | bytes 1728576 | tf_op jit(solution)/shard_map/cgqe,sce->cgqs/dot_general | solution.py:40
  127.5 2.4 %collective-permute-start.13 = (bf16[128,1024]{1,0:T(8,128)(2,1)}, bf16[128,1024]{1,0:T(8,128)(2,1)}, u32[]{:S(2)}, u32[]{:S(2)}) collective-permute-start(bf16[128,1024]{1,0:T(8,128)(2,1)} %collective-permute-done.10), channel_id=1, source_target_pairs={{0,1},{1,0},{2,3},{3,2},{4,5},{5,4},{6,7},{7,6},{8,9},{9,8},{10,11... | collective-permute-start | bytes 786440 | tf_op jit(solution)/shard_map/ppermute | solution.py:123
  129.9 2.2 %fusion.261 = (f32[4,4,128]{2,1,0:T(4,128)S(1)}, f32[4,4,128,128]{2,3,1,0:T(8,128)}) fusion(f32[4,4]{1,0:T(4,128)S(1)} %div.342, bf16[4,4,128,128]{3,2,1,0:T(8,128)(2,1)S(1)} %fusion.105, bf16[128,4,128,1]{2,1,0,3:T(4,128)(2,1)} %bitcast.507, pred[128,128]{0,1:T(8,128)(4,1)} %get-tuple-element.102), kind=kOutput, calls=%fused_computation.603 | convolution fusion | flops 67893248 | bytes 1728576 | tf_op jit(solution)/shard_map/cgqe,sce->cgqs/dot_general | solution.py:40
  132.1 2.4 %collective-permute-start.12 = (bf16[128,1024]{1,0:T(8,128)(2,1)}, bf16[128,1024]{1,0:T(8,128)(2,1)}, u32[]{:S(2)}, u32[]{:S(2)}) collective-permute-start(bf16[128,1024]{1,0:T(8,128)(2,1)} %collective-permute-done.10), channel_id=1, source_target_pairs={{0,2},{1,15},{2,4},{3,1},{4,6},{5,3},{6,8},{7,5},{8,10},{9,7},{10,... | collective-permute-start | bytes 786440 | tf_op jit(solution)/shard_map/ppermute | solution.py:126
  136.9 1.7 copy.200
  138.6 1.7 fusion.247
  141.9 1.7 fusion.248
  146.8 1.7 copy.206
  148.5 2.9 %fusion.275 = (f32[4,4,128]{2,1,0:T(4,128)}, f32[4,4,128,128]{2,3,1,0:T(8,128)}) fusion(f32[4,4]{1,0:T(4,128)S(1)} %div.342, bf16[4,4,128,128]{3,2,1,0:T(8,128)(2,1)S(1)} %fusion.105, bf16[128,4,128,1]{2,1,0,3:T(4,128)(2,1)} %bitcast.494, pred[128,128]{0,1:T(8,128)(4,1)} %get-tuple-element.104), kind=kOutput, calls=%fused_computation.617 | convolution fusion | flops 67893248 | bytes 1728576 | tf_op jit(solution)/shard_map/cgqe,sce->cgqs/dot_general | solution.py:40
  151.3 2.1 collective-permute-start.14
  153.4 2.8 %fusion.276 = (f32[4,4,128]{2,1,0:T(4,128)}, f32[4,4,128,128]{2,3,1,0:T(8,128)}) fusion(f32[4,4]{1,0:T(4,128)S(1)} %div.342, bf16[4,4,128,128]{3,2,1,0:T(8,128)(2,1)S(1)} %fusion.105, bf16[128,4,128,1]{2,1,0,3:T(4,128)(2,1)} %bitcast.495, pred[128,128]{0,1:T(8,128)(4,1)} %get-tuple-element.103), kind=kOutput, calls=%fused_computation.618 | convolution fusion | flops 67893248 | bytes 1728576 | tf_op jit(solution)/shard_map/cgqe,sce->cgqs/dot_general | solution.py:40
  178.7 2.6 %copy.112 = f32[1,128,2048]{2,1,0:T(8,128)} copy(f32[1,128,2048]{1,2,0:T(8,128)} %bitcast.478) | data formatting | bytes 2097152 | tf_op jit(solution)/shard_map/reshape | solution.py:135
  182.7 1.9 collective-permute-start.15
  184.6 30.7 %collective-permute-done.15 = f32[1,128,2048]{2,1,0:T(8,128)S(1)} collective-permute-done((f32[1,128,2048]{2,1,0:T(8,128)S(1)}, f32[1,128,2048]{2,1,0:T(8,128)S(1)}, u32[]{:S(2)}, u32[]{:S(2)}) %collective-permute-start.15) | collective-permute-done | bytes 1048608 | tf_op jit(solution)/shard_map/ppermute | solution.py:14
  (283 shorter events, 62.4 us)
Async XLA Ops:
  0.0 8.2 %copy-start = (bf16[1,1,2048,512]{3,2,1,0:T(8,128)(2,1)S(1)}, bf16[1,1,2048,512]{3,2,1,0:T(8,128)(2,1)}, u32[]{:S(2)}) copy-start(bf16[1,1,2048,512]{3,2,1,0:T(8,128)(2,1)} %param.13) | copy-start | bytes 6291460
  1.5 4.1 %copy-start.1 = (f32[1,128,2048]{2,1,0:T(8,128)S(1)}, f32[1,128,2048]{2,1,0:T(8,128)}, u32[]{:S(2)}) copy-start(f32[1,128,2048]{2,1,0:T(8,128)} %param.8) | copy-start | bytes 3145732
  1.5 4.1 %copy-start.45 = (f32[1,1,2048]{2,1,0:T(1,128)S(1)}, f32[1,1,2048]{2,1,0:T(1,128)}, u32[]{:S(2)}) copy-start(f32[1,1,2048]{2,1,0:T(1,128)} %param.11) | copy-start | bytes 24580
  8.7 17.6 %copy-start.76 = (s32[32]{0:T(128)S(1)}, s32[32]{0:T(128)}, u32[]{:S(2)}) copy-start(s32[32]{0:T(128)} %param.10) | copy-start | bytes 388
  9.4 24.9 %collective-permute-start = (bf16[128,1024]{1,0:T(8,128)(2,1)}, bf16[128,1024]{1,0:T(8,128)(2,1)}, u32[]{:S(2)}, u32[]{:S(2)}) collective-permute-start(bf16[128,1024]{1,0:T(8,128)(2,1)} %pad_maximum_fusion), channel_id=1, source_target_pairs={{0,2},{1,15},{2,4},{3,1},{4,6},{5,3},{6,8},{7,5},{8,10},{9,7},{10,... | collective-permute-start | bytes 786440 | tf_op jit(solution)/shard_map/ppermute | solution.py:126
  15.4 17.9 %collective-permute-start.1 = (bf16[128,1024]{1,0:T(8,128)(2,1)}, bf16[128,1024]{1,0:T(8,128)(2,1)}, u32[]{:S(2)}, u32[]{:S(2)}) collective-permute-start(bf16[128,1024]{1,0:T(8,128)(2,1)} %pad_maximum_fusion), channel_id=1, source_target_pairs={{0,1},{1,0},{2,3},{3,2},{4,5},{5,4},{6,7},{7,6},{8,9},{9,8},{10,11... | collective-permute-start | bytes 786440 | tf_op jit(solution)/shard_map/ppermute | solution.py:123
  24.0 5.8 %copy-start.77 = (f32[1,1,16]{2,1,0:T(1,128)S(1)}, f32[1,1,16]{2,1,0:T(1,128)}, u32[]{:S(2)}) copy-start(f32[1,1,16]{2,1,0:T(1,128)} %param.14) | copy-start | bytes 196
  31.1 2.1 copy-start.42
  31.1 6.1 %copy-start.38 = (pred[128,128]{0,1:T(8,128)(4,1)}, pred[128,128]{0,1:T(8,128)(4,1)S(1)}, u32[]{:S(2)}) copy-start(pred[128,128]{0,1:T(8,128)(4,1)S(1)} %get-tuple-element.91) | copy-start | bytes 49156
  31.1 12.9 %copy-start.40 = (pred[128,128]{0,1:T(8,128)(4,1)}, pred[128,128]{0,1:T(8,128)(4,1)S(1)}, u32[]{:S(2)}) copy-start(pred[128,128]{0,1:T(8,128)(4,1)S(1)} %get-tuple-element.92) | copy-start | bytes 49156
  37.2 10.6 %collective-permute-start.2 = (bf16[128,1024]{1,0:T(8,128)(2,1)}, bf16[128,1024]{1,0:T(8,128)(2,1)}, u32[]{:S(2)}, u32[]{:S(2)}) collective-permute-start(bf16[128,1024]{1,0:T(8,128)(2,1)} %collective-permute-done), channel_id=1, source_target_pairs={{0,2},{1,15},{2,4},{3,1},{4,6},{5,3},{6,8},{7,5},{8,10},{9,7},{10,... | collective-permute-start | bytes 786440 | tf_op jit(solution)/shard_map/ppermute | solution.py:126
  42.1 4.1 %collective-permute-start.3 = (bf16[128,1024]{1,0:T(8,128)(2,1)}, bf16[128,1024]{1,0:T(8,128)(2,1)}, u32[]{:S(2)}, u32[]{:S(2)}) collective-permute-start(bf16[128,1024]{1,0:T(8,128)(2,1)} %collective-permute-done), channel_id=1, source_target_pairs={{0,1},{1,0},{2,3},{3,2},{4,5},{5,4},{6,7},{7,6},{8,9},{9,8},{10,11... | collective-permute-start | bytes 786440 | tf_op jit(solution)/shard_map/ppermute | solution.py:123
  51.7 10.0 %collective-permute-start.4 = (bf16[128,1024]{1,0:T(8,128)(2,1)}, bf16[128,1024]{1,0:T(8,128)(2,1)}, u32[]{:S(2)}, u32[]{:S(2)}) collective-permute-start(bf16[128,1024]{1,0:T(8,128)(2,1)} %collective-permute-done.2), channel_id=1, source_target_pairs={{0,2},{1,15},{2,4},{3,1},{4,6},{5,3},{6,8},{7,5},{8,10},{9,7},{10,... | collective-permute-start | bytes 786440 | tf_op jit(solution)/shard_map/ppermute | solution.py:126
  54.6 4.8 %collective-permute-start.5 = (bf16[128,1024]{1,0:T(8,128)(2,1)}, bf16[128,1024]{1,0:T(8,128)(2,1)}, u32[]{:S(2)}, u32[]{:S(2)}) collective-permute-start(bf16[128,1024]{1,0:T(8,128)(2,1)} %collective-permute-done.2), channel_id=1, source_target_pairs={{0,1},{1,0},{2,3},{3,2},{4,5},{5,4},{6,7},{7,6},{8,9},{9,8},{10,11... | collective-permute-start | bytes 786440 | tf_op jit(solution)/shard_map/ppermute | solution.py:123
  66.2 13.6 %collective-permute-start.6 = (bf16[128,1024]{1,0:T(8,128)(2,1)}, bf16[128,1024]{1,0:T(8,128)(2,1)}, u32[]{:S(2)}, u32[]{:S(2)}) collective-permute-start(bf16[128,1024]{1,0:T(8,128)(2,1)} %collective-permute-done.4), channel_id=1, source_target_pairs={{0,2},{1,15},{2,4},{3,1},{4,6},{5,3},{6,8},{7,5},{8,10},{9,7},{10,... | collective-permute-start | bytes 786440 | tf_op jit(solution)/shard_map/ppermute | solution.py:126
  70.5 5.9 %collective-permute-start.7 = (bf16[128,1024]{1,0:T(8,128)(2,1)}, bf16[128,1024]{1,0:T(8,128)(2,1)}, u32[]{:S(2)}, u32[]{:S(2)}) collective-permute-start(bf16[128,1024]{1,0:T(8,128)(2,1)} %collective-permute-done.4), channel_id=1, source_target_pairs={{0,1},{1,0},{2,3},{3,2},{4,5},{5,4},{6,7},{7,6},{8,9},{9,8},{10,11... | collective-permute-start | bytes 786440 | tf_op jit(solution)/shard_map/ppermute | solution.py:123
  85.8 10.9 %collective-permute-start.8 = (bf16[128,1024]{1,0:T(8,128)(2,1)}, bf16[128,1024]{1,0:T(8,128)(2,1)}, u32[]{:S(2)}, u32[]{:S(2)}) collective-permute-start(bf16[128,1024]{1,0:T(8,128)(2,1)} %collective-permute-done.6), channel_id=1, source_target_pairs={{0,2},{1,15},{2,4},{3,1},{4,6},{5,3},{6,8},{7,5},{8,10},{9,7},{10,... | collective-permute-start | bytes 786440 | tf_op jit(solution)/shard_map/ppermute | solution.py:126
  88.7 11.3 %collective-permute-start.9 = (bf16[128,1024]{1,0:T(8,128)(2,1)}, bf16[128,1024]{1,0:T(8,128)(2,1)}, u32[]{:S(2)}, u32[]{:S(2)}) collective-permute-start(bf16[128,1024]{1,0:T(8,128)(2,1)} %collective-permute-done.6), channel_id=1, source_target_pairs={{0,1},{1,0},{2,3},{3,2},{4,5},{5,4},{6,7},{7,6},{8,9},{9,8},{10,11... | collective-permute-start | bytes 786440 | tf_op jit(solution)/shard_map/ppermute | solution.py:123
  106.2 12.4 %collective-permute-start.10 = (bf16[128,1024]{1,0:T(8,128)(2,1)}, bf16[128,1024]{1,0:T(8,128)(2,1)}, u32[]{:S(2)}, u32[]{:S(2)}) collective-permute-start(bf16[128,1024]{1,0:T(8,128)(2,1)} %collective-permute-done.8), channel_id=1, source_target_pairs={{0,2},{1,15},{2,4},{3,1},{4,6},{5,3},{6,8},{7,5},{8,10},{9,7},{10,... | collective-permute-start | bytes 786440 | tf_op jit(solution)/shard_map/ppermute | solution.py:126
  110.6 11.3 %collective-permute-start.11 = (bf16[128,1024]{1,0:T(8,128)(2,1)}, bf16[128,1024]{1,0:T(8,128)(2,1)}, u32[]{:S(2)}, u32[]{:S(2)}) collective-permute-start(bf16[128,1024]{1,0:T(8,128)(2,1)} %collective-permute-done.8), channel_id=1, source_target_pairs={{0,1},{1,0},{2,3},{3,2},{4,5},{5,4},{6,7},{7,6},{8,9},{9,8},{10,11... | collective-permute-start | bytes 786440 | tf_op jit(solution)/shard_map/ppermute | solution.py:123
  125.2 9.3 %copy-start.46 = (f32[4,4,128]{2,1,0:T(4,128)S(1)}, f32[4,4,128]{2,1,0:T(4,128)}, u32[]{:S(2)}) copy-start(f32[4,4,128]{2,1,0:T(4,128)} %get-tuple-element.131) | copy-start | bytes 24580
  125.2 9.3 %copy-start.48 = (f32[4,4,128]{2,1,0:T(4,128)S(1)}, f32[4,4,128]{2,1,0:T(4,128)}, u32[]{:S(2)}) copy-start(f32[4,4,128]{2,1,0:T(4,128)} %get-tuple-element.127) | copy-start | bytes 24580
  125.2 9.3 %copy-start.50 = (f32[4,4,128]{2,1,0:T(4,128)S(1)}, f32[4,4,128]{2,1,0:T(4,128)}, u32[]{:S(2)}) copy-start(f32[4,4,128]{2,1,0:T(4,128)} %get-tuple-element.123) | copy-start | bytes 24580
  125.2 9.3 %copy-start.52 = (f32[4,4,128]{2,1,0:T(4,128)S(1)}, f32[4,4,128]{2,1,0:T(4,128)}, u32[]{:S(2)}) copy-start(f32[4,4,128]{2,1,0:T(4,128)} %get-tuple-element.119) | copy-start | bytes 24580
  125.2 9.3 %copy-start.54 = (f32[4,4,128]{2,1,0:T(4,128)S(1)}, f32[4,4,128]{2,1,0:T(4,128)}, u32[]{:S(2)}) copy-start(f32[4,4,128]{2,1,0:T(4,128)} %get-tuple-element.115) | copy-start | bytes 24580
  125.2 9.3 %copy-start.61 = (f32[4,4,128]{2,1,0:T(4,128)S(1)}, f32[4,4,128]{2,1,0:T(4,128)}, u32[]{:S(2)}) copy-start(f32[4,4,128]{2,1,0:T(4,128)} %get-tuple-element.129) | copy-start | bytes 24580
  125.2 9.3 %copy-start.62 = (f32[4,4,128]{2,1,0:T(4,128)S(1)}, f32[4,4,128]{2,1,0:T(4,128)}, u32[]{:S(2)}) copy-start(f32[4,4,128]{2,1,0:T(4,128)} %get-tuple-element.125) | copy-start | bytes 24580
  125.2 9.3 %copy-start.63 = (f32[4,4,128]{2,1,0:T(4,128)S(1)}, f32[4,4,128]{2,1,0:T(4,128)}, u32[]{:S(2)}) copy-start(f32[4,4,128]{2,1,0:T(4,128)} %get-tuple-element.121) | copy-start | bytes 24580
  125.2 9.3 %copy-start.64 = (f32[4,4,128]{2,1,0:T(4,128)S(1)}, f32[4,4,128]{2,1,0:T(4,128)}, u32[]{:S(2)}) copy-start(f32[4,4,128]{2,1,0:T(4,128)} %get-tuple-element.117) | copy-start | bytes 24580
  125.2 9.3 %copy-start.65 = (f32[4,4,128]{2,1,0:T(4,128)S(1)}, f32[4,4,128]{2,1,0:T(4,128)}, u32[]{:S(2)}) copy-start(f32[4,4,128]{2,1,0:T(4,128)} %get-tuple-element.113) | copy-start | bytes 24580
  127.5 7.7 %copy-start.56 = (f32[4,4,128]{2,1,0:T(4,128)}, f32[4,4,128]{2,1,0:T(4,128)S(1)}, u32[]{:S(2)}) copy-start(f32[4,4,128]{2,1,0:T(4,128)S(1)} %get-tuple-element.111) | copy-start | bytes 24580
  127.5 11.0 %collective-permute-start.13 = (bf16[128,1024]{1,0:T(8,128)(2,1)}, bf16[128,1024]{1,0:T(8,128)(2,1)}, u32[]{:S(2)}, u32[]{:S(2)}) collective-permute-start(bf16[128,1024]{1,0:T(8,128)(2,1)} %collective-permute-done.10), channel_id=1, source_target_pairs={{0,1},{1,0},{2,3},{3,2},{4,5},{5,4},{6,7},{7,6},{8,9},{9,8},{10,11... | collective-permute-start | bytes 786440 | tf_op jit(solution)/shard_map/ppermute | solution.py:123
  132.1 3.1 %copy-start.66 = (f32[4,4,128]{2,1,0:T(4,128)}, f32[4,4,128]{2,1,0:T(4,128)S(1)}, u32[]{:S(2)}) copy-start(f32[4,4,128]{2,1,0:T(4,128)S(1)} %get-tuple-element.109) | copy-start | bytes 24580
  132.1 9.8 %collective-permute-start.12 = (bf16[128,1024]{1,0:T(8,128)(2,1)}, bf16[128,1024]{1,0:T(8,128)(2,1)}, u32[]{:S(2)}, u32[]{:S(2)}) collective-permute-start(bf16[128,1024]{1,0:T(8,128)(2,1)} %collective-permute-done.10), channel_id=1, source_target_pairs={{0,2},{1,15},{2,4},{3,1},{4,6},{5,3},{6,8},{7,5},{8,10},{9,7},{10,... | collective-permute-start | bytes 786440 | tf_op jit(solution)/shard_map/ppermute | solution.py:126
  151.3 4.9 %collective-permute-start.14 = (bf16[128,1024]{1,0:T(8,128)(2,1)}, bf16[128,1024]{1,0:T(8,128)(2,1)S(1)}, u32[]{:S(2)}, u32[]{:S(2)}) collective-permute-start(bf16[128,1024]{1,0:T(8,128)(2,1)} %collective-permute-done.12), channel_id=1, source_target_pairs={{0,1},{1,0},{2,3},{3,2},{4,5},{5,4},{6,7},{7,6},{8,9},{9,8},{10,11... | collective-permute-start | bytes 786440 | tf_op jit(solution)/shard_map/ppermute | solution.py:123
  160.2 3.9 %copy-start.4 = (f32[4,4,128,128]{2,3,1,0:T(8,128)S(1)}, f32[4,4,128,128]{2,3,1,0:T(8,128)}, u32[]{:S(2)}) copy-start(f32[4,4,128,128]{2,3,1,0:T(8,128)} %get-tuple-element.132) | copy-start | bytes 3145732
  160.2 3.9 %copy-start.41 = (pred[128,128]{0,1:T(8,128)(4,1)S(1)}, pred[128,128]{0,1:T(8,128)(4,1)}, u32[]{:S(2)}) copy-start(pred[128,128]{0,1:T(8,128)(4,1)} %copy-done.40) | copy-start | bytes 49156
  160.2 4.2 %copy-start.3 = (f32[4,4,128,128]{2,3,1,0:T(8,128)S(1)}, f32[4,4,128,128]{2,3,1,0:T(8,128)}, u32[]{:S(2)}) copy-start(f32[4,4,128,128]{2,3,1,0:T(8,128)} %get-tuple-element.130) | copy-start | bytes 3145732
  160.2 4.2 %copy-start.39 = (pred[128,128]{0,1:T(8,128)(4,1)S(1)}, pred[128,128]{0,1:T(8,128)(4,1)}, u32[]{:S(2)}) copy-start(pred[128,128]{0,1:T(8,128)(4,1)} %copy-done.38) | copy-start | bytes 49156
  161.6 3.0 %copy-start.6 = (f32[4,4,128,128]{2,3,1,0:T(8,128)S(1)}, f32[4,4,128,128]{2,3,1,0:T(8,128)}, u32[]{:S(2)}) copy-start(f32[4,4,128,128]{2,3,1,0:T(8,128)} %get-tuple-element.128) | copy-start | bytes 3145732
  161.6 3.0 %copy-start.37 = (pred[128,128]{0,1:T(8,128)(4,1)S(1)}, pred[128,128]{0,1:T(8,128)(4,1)}, u32[]{:S(2)}) copy-start(pred[128,128]{0,1:T(8,128)(4,1)} %get-tuple-element.93) | copy-start | bytes 49156
  162.6 2.3 %copy-start.5 = (f32[4,4,128,128]{2,3,1,0:T(8,128)S(1)}, f32[4,4,128,128]{2,3,1,0:T(8,128)}, u32[]{:S(2)}) copy-start(f32[4,4,128,128]{2,3,1,0:T(8,128)} %get-tuple-element.126) | copy-start | bytes 3145732
  162.6 2.3 %copy-start.36 = (pred[128,128]{0,1:T(8,128)(4,1)S(1)}, pred[128,128]{0,1:T(8,128)(4,1)}, u32[]{:S(2)}) copy-start(pred[128,128]{0,1:T(8,128)(4,1)} %get-tuple-element.94) | copy-start | bytes 49156
  164.8 1.6 copy-start.9
  164.9 1.6 copy-start.32
  178.7 2.6 %copy-start.2 = (f32[1,128,2048]{2,1,0:T(8,128)S(1)}, f32[1,128,2048]{2,1,0:T(8,128)}, u32[]{:S(2)}) copy-start(f32[1,128,2048]{2,1,0:T(8,128)} %param.8) | copy-start | bytes 3145732
  178.7 2.6 %copy-start.75 = (f32[1,1,2048]{2,1,0:T(1,128)S(1)}, f32[1,1,2048]{2,1,0:T(1,128)}, u32[]{:S(2)}) copy-start(f32[1,1,2048]{2,1,0:T(1,128)} %param.15) | copy-start | bytes 24580
  182.7 32.6 %collective-permute-start.15 = (f32[1,128,2048]{2,1,0:T(8,128)S(1)}, f32[1,128,2048]{2,1,0:T(8,128)S(1)}, u32[]{:S(2)}, u32[]{:S(2)}) collective-permute-start(f32[1,128,2048]{2,1,0:T(8,128)S(1)} %add_select_fusion), channel_id=1, source_target_pairs={{752,0},{0,16},{16,32},{32,48},{48,64},{64,80},{80,96},{96,112},{1... | collective-permute-start | bytes 3145736 | tf_op jit(solution)/shard_map/ppermute | solution.py:14
  (46 other events, 55.6 us)

commit v2 on v1

--- a/solution.py
+++ b/solution.py
@@ -97,17 +97,15 @@
     )
     own_block = jnp.concatenate([key_unit, values], axis=1)
 
-    ring_route = [
-        (i, ((i // 2 + (1 if i % 2 == 0 else -1)) % n_ring) * 2 + i % 2) for i in range(n_ctx)
-    ]
+    same_core = [list(range(c, n_ctx, 2)) for c in range(2)]
     partner_route = [(i, i ^ 1) for i in range(n_ctx)]
+    mine = lax.all_gather(own_block, "ctx", axis=0, tiled=True, axis_index_groups=same_core)
+    theirs = lax.ppermute(mine, "ctx", partner_route)
 
-    def origin_pos(origin):
-        return row_positions(origin * tok_rows, tok_rows, resident_tile_order, tok_rows)
-
-    def fold(running, block, origin):
-        return attend_block(
-            running, block, origin_pos(origin), queries, logit_multiplier, query_pos
+    def group_pos(group_core):
+        origins = jnp.arange(n_ring, dtype=jnp.int32) * 2 + group_core
+        return jnp.concatenate(
+            [row_positions(origins[j] * tok_rows, tok_rows, resident_tile_order, tok_rows) for j in range(n_ring)]
         )
 
     running = (
@@ -115,21 +113,8 @@
         jnp.zeros((KEY_VALUE_HEADS, query_groups, tok_rows), jnp.float32),
         jnp.zeros((KEY_VALUE_HEADS, query_groups, tok_rows, ATTN_UNIT_WIDTH), jnp.float32),
     )
-    ring_block = own_block
-    pending = None
-    for step in range(n_ring):
-        ring_origin = ((chip - step * step_dir) % n_ring) * 2 + core
-        partner_origin = ((chip + step * step_dir) % n_ring) * 2 + (1 - core)
-        partner_block = lax.ppermute(ring_block, "ctx", partner_route)
-        next_block = None
-        if step < n_ring - 1:
-            next_block = lax.ppermute(ring_block, "ctx", ring_route)
-        running = fold(running, ring_block, ring_origin)
-        if pending is not None:
-            running = fold(running, *pending)
-        pending = (partner_block, partner_origin)
-        ring_block = next_block
-    running = fold(running, *pending)
+    running = attend_block(running, mine, group_pos(core), queries, logit_multiplier, query_pos)
+    running = attend_block(running, theirs, group_pos(1 - core), queries, logit_multiplier, query_pos)
 
     mixed_out = running[2] / running[1][..., None]
     mixed_rows = jnp.transpose(mixed_out, (2, 0, 1, 3)).reshape(

time: 218 us -> 165 us (0.76)
  starting transfers between devices: 52.1 us -> 9.5 us
  local copies, waits for them, and re-layouts: 68.4 us -> 25.9 us
  waiting for transfers between devices: 30.7 us -> 63.8 us
  between operations: 2.32 us -> 24.4 us
  matrix products: 47.8 us -> 27.6 us
  other arithmetic: 15 us -> 12.7 us
    ppermute x15 -> x1, starting transfers between devices: 50.1 us -> 6.38 us  [local(): theirs = lax.ppermute(mine, 'ctx', partner_route)]
    all_gather x0 -> x1, waiting for transfers between devices: none -> 35 us  [local(): lax.all_gather(own_block, 'ctx', axis=0, tiled=True, axis_index_groups=sa...]
    dot_general x16 -> x2, matrix products: 38.8 us -> 15.2 us  [attend_block(): jnp.einsum('cgqe,sce->cgqs', queries, key_piece, preferred_element_type=j...]
    slice x15 -> x1, local copies, waits for them, and re-layouts: 20.9 us -> 3.09 us  [attend_block(): value_piece = block[:, kvd:].reshape(rows, kv_heads, -1)]
    reshape x16 -> x2, local copies, waits for them, and re-layouts: 16.7 us -> 4.58 us  [attend_block(): value_piece = block[:, kvd:].reshape(rows, kv_heads, -1)]
    reshape x15 -> x2, local copies, waits for them, and re-layouts: 16.5 us -> 4.42 us  [attend_block(): key_piece = block[:, :kvd].reshape(rows, kv_heads, -1)]
    unnamed x157 -> x19, local copies, waits for them, and re-layouts: 5.86 us -> 1.01 us
    slice x0 -> x3, local copies, waits for them, and re-layouts: none -> 4.44 us  [the longest x1 3.07 us: attend_block(): key_piece = block[:, :kvd].reshape(rows, kv_heads, -1)]
  transfers between devices with their start and end apart: 16 -> 3, of which waited for: 1 -> 2; matrix products, arithmetic and copies ran while one was open for 26% -> 13% of each run, Pallas kernels for 0% -> 0%
where the time goes in v2:
time: 165 us; the launch traced here: 164 us
  waiting for transfers between devices  63.8 us (39%)
  matrix products  27.6 us (17%)
  local copies, waits for them, and re-layouts  25.9 us (16%)
  between operations  24.4 us (15%)
  other arithmetic  12.7 us (8%)
  starting transfers between devices  9.5 us (6%)
    all_gather x1, waiting for transfers between devices, local(): lax.all_gather(own_block, 'ctx', axis=0, tiled=True, axis_index_groups=sa...  35 us
    ppermute x1, waiting for transfers between devices, passed_along(): return lax.ppermute(block, axis, route)  28.8 us
    dot_general x2, matrix products, attend_block(): jnp.einsum('cgqe,sce->cgqs', queries, key_piece, preferred_element_type=j...  15.2 us
    dot_general x2, matrix products, attend_block(): jnp.einsum('cgqs,sce->cgqe', weights.astype(jnp.bfloat16), value_piece, p...  8.24 us
    ppermute x1, starting transfers between devices, local(): theirs = lax.ppermute(mine, 'ctx', partner_route)  6.38 us
    reduce_sum x1, other arithmetic, attend_block(): new_sum = running_sum * scale + jnp.sum(weights, axis=-1)  4.94 us
    reshape x2, local copies, waits for them, and re-layouts, attend_block(): value_piece = block[:, kvd:].reshape(rows, kv_heads, -1)  4.58 us
    reshape x2, local copies, waits for them, and re-layouts, attend_block(): key_piece = block[:, :kvd].reshape(rows, kv_heads, -1)  4.42 us
  transfers between devices with their start and end apart: 3, of which 2 were waited for; matrix products, arithmetic and copies ran while one was open for 13% of the time, Pallas kernels for 0%

profile of v2, /device:TPU:1, one launch (start us, length us, event | category | flops | bytes accessed | tf_op | source)
XLA Modules:
  0.0 164.0 jit_solution(12364968406495980037)
XLA Ops:
  6.5 0.0 copy-start
  6.5 0.0 all-gather.2.cloned.1.call-start
  6.6 1.5 multiply_reduce_fusion
  8.1 4.0 %copy.29 = bf16[512,2048]{1,0:T(8,128)(2,1)} copy(bf16[512,2048]{0,1:T(8,128)(2,1)} %bitcast.99) | data formatting | bytes 4194304 | tf_op jit(solution)/shard_map/dot_general | solution.py:82
  12.1 0.0 copy-done
  12.1 1.7 %fusion.29 = bf16[128,512]{1,0:T(8,128)(2,1)S(1)} fusion(bf16[1,1,2048,512]{3,2,1,0:T(8,128)(2,1)S(1)} %copy-done, f32[1,128,2048]{2,1,0:T(8,128)} %param.8, f32[2048]{0:T(1024)} %bitcast.105, f32[128]{0:T(128)S(1)} %add_rsqrt_fusion.2), kind=kOutput, calls=%fused_computation.24 | convolution fusion | flops 269287424 | bytes 3285504 | tf_op jit(solution)/shard_map/dot_general | solution.py:88
  13.8 0.0 copy-done.1
  13.9 0.0 copy-done.4
  13.9 2.4 %multiply_reduce_fusion.1 = (f32[128,4]{0,1:T(4,128)S(1)}, f32[128,4,128]{0,2,1:T(8,128)S(1)}) fusion(bf16[4,128,2048]{2,1,0:T(8,128)(2,1)} %bitcast.97, f32[2048]{0:T(1024)S(1)} %bitcast.106, f32[1,128,2048]{2,1,0:T(8,128)S(1)} %copy-done.1, f32[128]{0:T(128)S(1)} %add_rsqrt_fusion.2), kind=kOutput, calls=%fused_computation.44 | convolution fusion | flops 269352448 | bytes 3418624 | tf_op jit(solution)/shard_map/dot_general | solution.py:82
  16.3 0.1 copy.19
  16.4 0.7 pad_maximum_fusion
  17.2 0.0 all-gather.2.cloned.1.call-update
  17.2 1.7 %squeeze.6 = f32[128,4,4,128]{3,2,1,0:T(4,128)} reshape(f32[1,128,2048]{2,1,0:T(8,128)S(1)} %copy-done.1) | data formatting | bytes 2097152 | tf_op jit(solution)/shard_map/squeeze | solution.py:75
  18.9 0.7 multiply_reduce_fusion.2
  19.6 0.1 div.373
  19.7 0.7 fusion.99
  21.1 0.7 fusion.98
  32.1 0.0 copy-done.6
  32.1 0.2 select_reduce_fusion
  32.6 35.0 %all-gather.2.cloned.1.call-done = bf16[1024,1024]{1,0:T(8,128)(2,1)} async-done(((bf16[128,1024]{1,0:T(8,128)(2,1)}), bf16[1024,1024]{1,0:T(8,128)(2,1)}) %all-gather.2.cloned.1.call-update) | async-done | bytes 2097168 | tf_op jit(solution)/shard_map/all_gather | solution.py:102
  67.5 6.4 %collective-permute-start = (bf16[1024,1024]{1,0:T(8,128)(2,1)}, bf16[1024,1024]{1,0:T(8,128)(2,1)}, u32[]{:S(2)}, u32[]{:S(2)}) collective-permute-start(bf16[1024,1024]{1,0:T(8,128)(2,1)} %all-gather.2.cloned.1.call-done), channel_id=1, source_target_pairs={{0,1},{1,0},{2,3},{3,2},{4,5},{5,4},{6,7},{7,6},{8,9},{9,8},{10,11... | collective-permute-start | bytes 6291464 | tf_op jit(solution)/shard_map/ppermute | solution.py:103
  74.0 2.4 %fusion.32 = (f32[128,4,4]{0,2,1:T(4,128)S(1)}, bf16[128,4,4,128]{3,0,2,1:T(8,128)(2,1)}) fusion(f32[4,4,128]{2,1,0:T(4,128)S(1)} %bitcast.107, f32[128]{0:T(128)S(1)} %add_rsqrt_fusion.2, f32[128,4,4,128]{3,2,1,0:T(4,128)} %squeeze.6), kind=kLoop, calls=%fused_computation.25 | loop fusion | flops 1570816 | bytes 1589760 | tf_op jit(solution)/shard_map/reduce_sum | solution.py:18
  76.4 0.2 broadcast_compare_fusion
  76.6 3.1 %fusion.97 = (bf16[1024,512]{1,0:T(8,128)(2,1)}, bf16[1024,512]{1,0:T(8,128)(2,1)}) fusion(bf16[1024,1024]{1,0:T(8,128)(2,1)} %all-gather.2.cloned.1.call-done), kind=kLoop, calls=%fused_computation.356 | loop fusion | bytes 4194304 | tf_op jit(solution)/shard_map/slice | solution.py:36
  79.7 2.3 %copy.32 = bf16[1024,512]{0,1:T(8,128)(2,1)} copy(bf16[1024,512]{1,0:T(8,128)(2,1)} %get-tuple-element.31) | data formatting | bytes 2097152 | tf_op jit(solution)/shard_map/reshape | solution.py:37
  82.0 2.2 %reshape.1070 = bf16[1024,4,128]{2,1,0:T(4,128)(2,1)} reshape(bf16[1024,512]{1,0:T(8,128)(2,1)} %get-tuple-element.30) | data formatting | bytes 2097152 | tf_op jit(solution)/shard_map/reshape | solution.py:36
  84.2 6.2 %fusion = (f32[4,4,128]{2,1,0:T(4,128)S(1)}, f32[4,4,128,1024]{3,2,1,0:T(8,128)}) fusion(f32[4,4]{1,0:T(4,128)S(1)} %div.373, pred[128,1024]{1,0:T(8,128)(4,1)S(1)} %get-tuple-element.34, bf16[1024,4,128,1]{2,1,0,3:T(4,128)(2,1)} %bitcast.98, bf16[128,4,4,128]{3,0,2,1:T(8,128)(2,1)} %get-tuple-element.27, f32[128,4,4]{0,2,1:T(4,128)S(1)} %add_rsqrt_fusion), kind=kOutput, calls=%fused_computation.4 | convolution fusion | flops 543946752 | bytes 10108992 | tf_op jit(solution)/shard_map/cgqe,sce->cgqs/dot_general | solution.py:40
  90.4 0.0 collective-permute-done
  90.4 3.1 %fusion.96 = (bf16[1024,512]{1,0:T(8,128)(2,1)}, bf16[1024,512]{1,0:T(8,128)(2,1)}) fusion(bf16[1024,1024]{1,0:T(8,128)(2,1)} %collective-permute-done), kind=kLoop, calls=%fused_computation.355 | loop fusion | bytes 4194304 | tf_op jit(solution)/shard_map/slice | solution.py:37
  93.5 2.2 %reshape.1072 = bf16[1024,4,128]{2,1,0:T(4,128)(2,1)} reshape(bf16[1024,512]{1,0:T(8,128)(2,1)} %get-tuple-element.29) | data formatting | bytes 2097152 | tf_op jit(solution)/shard_map/reshape | solution.py:36
  95.7 9.0 %fusion.2 = (f32[4,4,128]{2,1,0:T(4,128)S(1)}, f32[4,4,128]{2,1,0:T(4,128)S(1)}, f32[4,4,128,1024]{3,2,1,0:T(8,128)}) fusion(f32[4,4,128,1024]{3,2,1,0:T(8,128)} %get-tuple-element.54, f32[4,4,128]{2,1,0:T(4,128)S(1)} %broadcast_maximum_fusion, f32[4,4]{1,0:T(4,128)S(1)} %div.373, pred[128,1024]{1,0:T(8,128)(4,1)S(1)} %get-tuple-element.34, ...), kind=kOutput, calls=%fused_computation.6 | convolution fusion | flops 554430464 | bytes 18645056 | tf_op jit(solution)/shard_map/cgqe,sce->cgqs/dot_general | solution.py:40
  104.7 2.3 %copy.35 = bf16[1024,512]{0,1:T(8,128)(2,1)} copy(bf16[1024,512]{1,0:T(8,128)(2,1)} %get-tuple-element.28) | data formatting | bytes 2097152 | tf_op jit(solution)/shard_map/reshape | solution.py:37
  107.0 4.9 %fusion.4 = f32[4,4,128]{2,1,0:T(4,128)S(1)} fusion(f32[4,4,128,1024]{3,2,1,0:T(8,128)} %get-tuple-element.55, f32[4,4,128]{2,1,0:T(4,128)S(1)} %fusion.93, f32[4,4]{1,0:T(4,128)S(1)} %div.373, pred[128,1024]{1,0:T(8,128)(4,1)S(1)} %get-tuple-element.33), kind=kLoop, calls=%fused_computation.8 | loop fusion | flops 10483712 | bytes 8536128 | tf_op jit(solution)/shard_map/reduce_sum | solution.py:47
  112.0 0.0 copy-done.2
  112.0 0.0 slice-start.1
  112.0 0.0 copy-start.3
  112.0 4.9 %fusion.26 = f32[128,4,4,128]{0,3,2,1:T(8,128)S(1)} fusion(bf16[1024,4,128,1]{0,2,3,1:T(8,128)(2,1)S(1)} %bitcast.100, f32[4,4,128,1024]{3,2,1,0:T(8,128)} %get-tuple-element.54, f32[4,4,128]{2,1,0:T(4,128)S(1)} %broadcast_maximum_fusion, f32[4,4]{1,0:T(4,128)S(1)} %div.373, pred[128,1024]{1,0:T(8,128)(4,1)S(1)} %get-tuple-element.34, ...), kind=kOutput, calls=%fused_computation.21 | convolution fusion | flops 547880960 | bytes 10641472 | tf_op jit(solution)/shard_map/cgqs,sce->cgqe/dot_general | solution.py:48
  116.9 0.0 slice-done
  116.9 0.0 slice-done.1
  116.9 0.0 copy-done.3
  117.0 0.0 copy-start.5
  117.0 3.3 %fusion.40 = f32[128,4,4,128]{0,3,2,1:T(8,128)} fusion(f32[128,4,4,128]{0,3,2,1:T(8,128)S(1)} %fusion.26, bf16[1024,4,128,1]{0,2,3,1:T(8,128)(2,1)S(1)} %bitcast.101, f32[4,4,128,1024]{3,2,1,0:T(8,128)S(1)} %bitcast.96, f32[4,4,128]{2,1,0:T(4,128)S(1)} %fusion.93, f32[4,4]{1,0:T(4,128)S(1)} %div.373, pred[128,1024]{1,0:T(8,128)(4,1)S(1)} %get-tuple-element.33, ...), kind=kOutput, calls=%fused_computation.36 | convolution fusion | flops 547880960 | bytes 11681856 | tf_op jit(solution)/shard_map/cgqs,sce->cgqe/dot_general | solution.py:48
  120.3 2.5 %copy.24 = f32[1,128,2048]{2,1,0:T(8,128)} copy(f32[1,128,2048]{1,2,0:T(8,128)} %bitcast.103) | data formatting | bytes 2097152 | tf_op jit(solution)/shard_map/reshape | solution.py:120
  122.9 0.0 copy-done.5
  122.9 1.4 add_select_fusion
  124.2 3.1 %collective-permute-start.1 = (f32[1,128,2048]{2,1,0:T(8,128)S(1)}, f32[1,128,2048]{2,1,0:T(8,128)S(1)}, u32[]{:S(2)}, u32[]{:S(2)}) collective-permute-start(f32[1,128,2048]{2,1,0:T(8,128)S(1)} %add_select_fusion), channel_id=1, source_target_pairs={{752,0},{0,16},{16,32},{32,48},{48,64},{64,80},{80,96},{96,112},{1... | collective-permute-start | bytes 3145736 | tf_op jit(solution)/shard_map/ppermute | solution.py:14
  127.3 28.8 %collective-permute-done.1 = f32[1,128,2048]{2,1,0:T(8,128)S(1)} collective-permute-done((f32[1,128,2048]{2,1,0:T(8,128)S(1)}, f32[1,128,2048]{2,1,0:T(8,128)S(1)}, u32[]{:S(2)}, u32[]{:S(2)}) %collective-permute-start.1) | collective-permute-done | bytes 1048608 | tf_op jit(solution)/shard_map/ppermute | solution.py:14
  156.2 1.0 copy.68
  (50 shorter events, 0.7 us)
Async XLA Ops:
  6.5 5.6 %copy-start = (bf16[1,1,2048,512]{3,2,1,0:T(8,128)(2,1)S(1)}, bf16[1,1,2048,512]{3,2,1,0:T(8,128)(2,1)}, u32[]{:S(2)}) copy-start(bf16[1,1,2048,512]{3,2,1,0:T(8,128)(2,1)} %param.13) | copy-start | bytes 6291460
  6.5 7.3 %copy-start.1 = (f32[1,128,2048]{2,1,0:T(8,128)S(1)}, f32[1,128,2048]{2,1,0:T(8,128)}, u32[]{:S(2)}) copy-start(f32[1,128,2048]{2,1,0:T(8,128)} %param.8) | copy-start | bytes 3145732
  6.5 7.3 %copy-start.4 = (f32[1,1,2048]{2,1,0:T(1,128)S(1)}, f32[1,1,2048]{2,1,0:T(1,128)}, u32[]{:S(2)}) copy-start(f32[1,1,2048]{2,1,0:T(1,128)} %param.11) | copy-start | bytes 24580
  6.5 25.6 %copy-start.6 = (s32[32]{0:T(128)S(1)}, s32[32]{0:T(128)}, u32[]{:S(2)}) copy-start(s32[32]{0:T(128)} %param.10) | copy-start | bytes 388
  6.5 61.0 %all-gather.2.cloned.1.call-start = ((), (), s32[]{:S(2)}) async-start(), calls=%async_computation | async-start | bytes 2359296 | tf_op jit(solution)/shard_map/all_gather | solution.py:102
  67.5 22.9 %collective-permute-start = (bf16[1024,1024]{1,0:T(8,128)(2,1)}, bf16[1024,1024]{1,0:T(8,128)(2,1)}, u32[]{:S(2)}, u32[]{:S(2)}) collective-permute-start(bf16[1024,1024]{1,0:T(8,128)(2,1)} %all-gather.2.cloned.1.call-done), channel_id=1, source_target_pairs={{0,1},{1,0},{2,3},{3,2},{4,5},{5,4},{6,7},{7,6},{8,9},{9,8},{10,11... | collective-permute-start | bytes 6291464 | tf_op jit(solution)/shard_map/ppermute | solution.py:103
  107.0 5.0 %copy-start.2 = (bf16[1024,512]{0,1:T(8,128)(2,1)S(1)}, bf16[1024,512]{0,1:T(8,128)(2,1)}, u32[]{:S(2)}) copy-start(bf16[1024,512]{0,1:T(8,128)(2,1)} %copy.32) | copy-start | bytes 3145732
  107.0 9.9 %slice-start = ((s8[8388608]{0:T(1024)(128)(4,1)}), s8[4194304]{0:T(1024)(128)(4,1)S(1)}, s32[]{:S(2)}) async-start(s8[8388608]{0:T(1024)(128)(4,1)} %bitcast.95), calls=%async_computation.1 | async-start | bytes 8388608
  112.0 4.9 %slice-start.1 = ((s8[8388608]{0:T(1024)(128)(4,1)}), s8[4194304]{0:T(1024)(128)(4,1)S(1)}, s32[]{:S(2)}) async-start(s8[8388608]{0:T(1024)(128)(4,1)} %bitcast.95), calls=%async_computation.2 | async-start | bytes 8388608
  112.0 4.9 %copy-start.3 = (bf16[1024,512]{0,1:T(8,128)(2,1)S(1)}, bf16[1024,512]{0,1:T(8,128)(2,1)}, u32[]{:S(2)}) copy-start(bf16[1024,512]{0,1:T(8,128)(2,1)} %copy.35) | copy-start | bytes 3145732
  117.0 5.9 %copy-start.5 = (f32[1,1,2048]{2,1,0:T(1,128)S(1)}, f32[1,1,2048]{2,1,0:T(1,128)}, u32[]{:S(2)}) copy-start(f32[1,1,2048]{2,1,0:T(1,128)} %param.15) | copy-start | bytes 24580
  124.2 31.9 %collective-permute-start.1 = (f32[1,128,2048]{2,1,0:T(8,128)S(1)}, f32[1,128,2048]{2,1,0:T(8,128)S(1)}, u32[]{:S(2)}, u32[]{:S(2)}) collective-permute-start(f32[1,128,2048]{2,1,0:T(8,128)S(1)} %add_select_fusion), channel_id=1, source_target_pairs={{752,0},{0,16},{16,32},{32,48},{48,64},{64,80},{80,96},{96,112},{1... | collective-permute-start | bytes 3145736 | tf_op jit(solution)/shard_map/ppermute | solution.py:14
Sparse Core Ops, SparseCore 0:
  17.3 50.1 all-gather.1

commit v3 on v2

v3 whole, which is shorter than its diff:
```python
import functools

import jax
import jax.numpy as jnp
from jax import lax
from jax.experimental import pallas as pl
from jax.experimental.pallas import tpu as pltpu
from jax.sharding import PartitionSpec as P

H = 16
KEY_VALUE_HEADS = 4
ATTN_UNIT_WIDTH = 128


def passed_along(block, axis, distance):
    devices = range(lax.axis_size(axis))
    route = [((i - distance) % len(devices), i) for i in devices]
    return lax.ppermute(block, axis, route)


def head_norm(values):
    return values * lax.rsqrt(jnp.mean(values * values, axis=-1, keepdims=True) + 1e-05)


def attention_kernel(
    mult_ref, tiers_ref, qpos_ref, kpos_a_ref, kpos_b_ref, q_ref,
    ka_ref, va_ref, kb_ref, vb_ref, x_ref, w_ref, out_ref,
):
    c = pl.program_id(0)
    group = q_ref.shape[1] // ATTN_UNIT_WIDTH
    qpos = qpos_ref[...]
    allowed_a = kpos_a_ref[...] <= qpos
    allowed_b = kpos_b_ref[...] <= qpos
    ka = ka_ref[...]
    kb = kb_ref[...]
    va = va_ref[...]
    vb = vb_ref[...]
    gate = tiers_ref[0] > 0
    dims = (((1,), (1,)), ((), ()))
    for g in range(group):
        cols = slice(g * ATTN_UNIT_WIDTH, (g + 1) * ATTN_UNIT_WIDTH)
        qh = q_ref[:, cols]
        mult = mult_ref[c * group + g]
        s_a = lax.dot_general(qh, ka, dims, preferred_element_type=jnp.float32) * mult
        s_b = lax.dot_general(qh, kb, dims, preferred_element_type=jnp.float32) * mult
        s_a = jnp.where(allowed_a, s_a, -1e30)
        s_b = jnp.where(allowed_b, s_b, -1e30)
        row_max = jnp.maximum(
            jnp.max(s_a, axis=1, keepdims=True), jnp.max(s_b, axis=1, keepdims=True)
        )
        p_a = jnp.where(allowed_a, jnp.exp(s_a - row_max), 0.0)
        p_b = jnp.where(allowed_b, jnp.exp(s_b - row_max), 0.0)
        total = jnp.sum(p_a, axis=1, keepdims=True) + jnp.sum(p_b, axis=1, keepdims=True)
        mixed = jnp.dot(
            p_a.astype(jnp.bfloat16), va, preferred_element_type=jnp.float32
        ) + jnp.dot(p_b.astype(jnp.bfloat16), vb, preferred_element_type=jnp.float32)
        mixed = mixed / total
        x = x_ref[:, cols]
        out_ref[:, cols] = jnp.where(gate, x + w_ref[:, cols] * mixed, x)


def attend_and_update(mult, tiers, qpos, kpos_a, kpos_b, queries, block_a, block_b, x, w_out):
    rows, width = x.shape
    kv_rows = block_a.shape[0]
    kv_heads = KEY_VALUE_HEADS
    head_cols = width // kv_heads
    smem = pl.BlockSpec(memory_space=pltpu.SMEM)
    whole = lambda shape: pl.BlockSpec(shape, lambda c: (0, 0))
    cols = lambda shape: pl.BlockSpec(shape, lambda c: (0, c))
    values_at = lambda shape: pl.BlockSpec(shape, lambda c: (0, c + kv_heads))
    kv_block = (kv_rows, ATTN_UNIT_WIDTH)
    flops = 4 * rows * 2 * kv_rows * ATTN_UNIT_WIDTH * H
    return pl.pallas_call(
        attention_kernel,
        grid=(kv_heads,),
        in_specs=[
            smem,
            smem,
            whole((rows, 1)),
            whole((1, kv_rows)),
            whole((1, kv_rows)),
            cols((rows, head_cols)),
            cols(kv_block),
            values_at(kv_block),
            cols(kv_block),
            values_at(kv_block),
            cols((rows, head_cols)),
            cols((1, head_cols)),
        ],
        out_specs=cols((rows, head_cols)),
        out_shape=jax.ShapeDtypeStruct((rows, width), jnp.float32),
        cost_estimate=pl.CostEstimate(
            flops=flops,
            transcendentals=rows * 2 * kv_rows * H,
            bytes_accessed=4 * kv_rows * 1024 + rows * width * 10,
        ),
    )(mult, tiers, qpos, kpos_a, kpos_b, queries, block_a, block_a, block_b, block_b, x, w_out)


def local(
    residual_flow,
    tiers_each_segment,
    resident_tile_order,
    normalizer_weight_entries,
    lookup_map_weights,
    content_map_weights,
    softmax_warmth,
    attention_result_weight,
):
    tok_rows = residual_flow.shape[1]
    query_groups = H // KEY_VALUE_HEADS
    n_ctx = lax.axis_size("ctx")
    n_chips = n_ctx // 2
    me = lax.axis_index("ctx")
    core = me % 2
    half_rows = tok_rows // 2
    residual = residual_flow[0]

    all_pos = (
        jnp.repeat(resident_tile_order.astype(jnp.int32), half_rows) * half_rows
        + jnp.tile(jnp.arange(half_rows, dtype=jnp.int32), resident_tile_order.shape[0])
    )
    query_pos = lax.dynamic_slice(all_pos, (me * tok_rows,), (tok_rows,)).reshape(tok_rows, 1)
    by_core = all_pos.reshape(n_chips, 2, tok_rows)
    pos_mine = lax.dynamic_index_in_dim(by_core, core, axis=1, keepdims=False).reshape(1, -1)
    pos_theirs = lax.dynamic_index_in_dim(by_core, 1 - core, axis=1, keepdims=False).reshape(1, -1)

    normed = (
        residual
        * lax.rsqrt(jnp.mean(residual * residual, axis=-1, keepdims=True) + 1e-05)
        * normalizer_weight_entries[0, 0]
    ).astype(jnp.bfloat16)
    keys_raw = jnp.dot(normed, lookup_map_weights[0, 0], preferred_element_type=jnp.float32)
    key_unit = (
        head_norm(keys_raw.reshape(tok_rows, KEY_VALUE_HEADS, ATTN_UNIT_WIDTH))
        .astype(jnp.bfloat16)
        .reshape(tok_rows, KEY_VALUE_HEADS * ATTN_UNIT_WIDTH)
    )
    values = jnp.dot(normed, content_map_weights[0, 0], preferred_element_type=jnp.float32).astype(
        jnp.bfloat16
    )
    queries = (
        head_norm(normed.astype(jnp.float32).reshape(tok_rows, H, ATTN_UNIT_WIDTH))
        .astype(jnp.bfloat16)
        .reshape(tok_rows, H * ATTN_UNIT_WIDTH)
    )
    own_block = jnp.concatenate([key_unit, values], axis=1)

    same_core = [list(range(c, n_ctx, 2)) for c in range(2)]
    partner_route = [(i, i ^ 1) for i in range(n_ctx)]
    mine = lax.all_gather(own_block, "ctx", axis=0, tiled=True, axis_index_groups=same_core)
    theirs = lax.ppermute(mine, "ctx", partner_route)

    mult = softmax_warmth[0, 0] / ATTN_UNIT_WIDTH
    residual = attend_and_update(
        mult,
        tiers_each_segment,
        query_pos,
        pos_mine,
        pos_theirs,
        queries,
        mine,
        theirs,
        residual,
        attention_result_weight[0],
    )
    return passed_along(residual[None], "section", 1)


def solution(mesh):
    in_specs = (
        P("section", "ctx", None),
        P("section"),
        P(),
        P("section", None, None),
        P("section", None, None, None),
        P("section", None, None, None),
        P("section", None, None),
        P("section", None, None),
    )
    out_specs = P("section", "ctx", None)
    return jax.shard_map(local, mesh=mesh, in_specs=in_specs, out_specs=out_specs, check_vma=False)
```

time: 165 us -> 131 us (0.79)
  matrix products: 27.6 us -> 1.28 us
  local copies, waits for them, and re-layouts: 25.9 us -> 8.78 us
  waiting for transfers between devices: 63.8 us -> 79.4 us
  Pallas kernels: 0 us -> 12.9 us
  between operations: 24.4 us -> 14.2 us
  other arithmetic: 12.7 us -> 4.86 us
    dot_general x4 -> x0, matrix products: 23.5 us -> none  [the longest x2 15.2 us: attend_block(): jnp.einsum('cgqe,sce->cgqs', queries, key_piece, preferred_element_type=j...]
    all_gather x1, waiting for transfers between devices: 35 us -> 50.4 us  [local(): lax.all_gather(own_block, 'ctx', axis=0, tiled=True, axis_index_groups=sa...]
    pallas_call x0 -> x1, Pallas kernels: none -> 12.9 us  [attend_and_update(): pl.pallas_call(attention_kernel, grid=(kv_heads,), in_specs=[smem, smem,...]
    reshape x5 -> x2, local copies, waits for them, and re-layouts: 11.5 us -> 0.83 us  [local(): lax.dynamic_slice(all_pos, (me * tok_rows,), (tok_rows,))]
    slice x4 -> x0, local copies, waits for them, and re-layouts: 7.53 us -> none  [the longest x1 3.09 us: attend_block(): value_piece = block[:, kvd:].reshape(rows, kv_heads, -1)]
    reduce_sum x2 -> x0, other arithmetic: 5.1 us -> none  [the longest x1 4.94 us: attend_block(): new_sum = running_sum * scale + jnp.sum(weights, axis=-1)]
    reduce_sum x1, other arithmetic: 2.41 us -> 0.34 us  [head_norm(): jnp.mean(values * values, axis=-1, keepdims=True) + 1e-05]
    squeeze x1 -> x0, local copies, waits for them, and re-layouts: 1.68 us -> none  [local(): residual = residual_flow[0]]
  transfers between devices with their start and end apart: 3 -> 3, of which waited for: 2 -> 2; matrix products, arithmetic and copies ran while one was open for 13% -> 4% of each run, Pallas kernels for 0% -> 0%
where the time goes in v3:
time: 131 us
  waiting for transfers between devices  79.4 us (61%)
  between operations  14.2 us (11%)
  Pallas kernels  12.9 us (10%)
  starting transfers between devices  9.28 us (7%)
  local copies, waits for them, and re-layouts  8.78 us (7%)
  other arithmetic  4.86 us (4%)
    all_gather x1, waiting for transfers between devices, local(): lax.all_gather(own_block, 'ctx', axis=0, tiled=True, axis_index_groups=sa...  50.4 us
    ppermute x1, waiting for transfers between devices, passed_along(): return lax.ppermute(block, axis, route)  29.1 us
    pallas_call x1, Pallas kernels, attend_and_update(): pl.pallas_call(attention_kernel, grid=(kv_heads,), in_specs=[smem, smem,...  12.9 us
    ppermute x1, starting transfers between devices, local(): theirs = lax.ppermute(mine, 'ctx', partner_route)  6.2 us
    dot_general x1, local copies, waits for them, and re-layouts, local(): jnp.dot(normed, lookup_map_weights[0, 0], preferred_element_type=jnp.floa...  4.04 us
    ppermute x1, starting transfers between devices, passed_along(): return lax.ppermute(block, axis, route)  3.08 us
  transfers between devices with their start and end apart: 3, of which 2 were waited for; matrix products, arithmetic and copies ran while one was open for 4% of the time, Pallas kernels for 0%

profile of v3, /device:TPU:1, one launch (start us, length us, event | category | flops | bytes accessed | tf_op | source)
XLA Modules:
  0.0 130.8 jit_solution(4833155592936504502)
XLA Ops:
  6.5 0.0 copy-start
  6.5 0.0 all-gather.2.cloned.1.call-start
  6.5 1.5 %multiply_reduce_fusion.1 = f32[128]{0:T(128)S(1)} fusion(f32[1,128,2048]{2,1,0:T(8,128)} %param.8), kind=kLoop, calls=%fused_computation.11 | loop fusion | flops 524160 | bytes 1049088 | tf_op jit(solution)/shard_map/reduce_sum | solution.py:130
  8.1 0.0 copy-start.1
  8.1 0.0 copy-start.3
  8.1 4.0 %copy.28 = bf16[512,2048]{1,0:T(8,128)(2,1)} copy(bf16[512,2048]{0,1:T(8,128)(2,1)} %bitcast.51) | data formatting | bytes 4194304 | tf_op jit(solution)/shard_map/dot_general | solution.py:133
  12.1 0.0 copy-start.2
  12.1 0.0 copy-done
  12.1 0.0 copy-done.1
  12.1 0.0 copy-done.3
  12.2 0.5 fusion.2
  12.7 1.1 copy-done.2
  13.7 0.0 copy-start.4
  13.7 0.8 multiply_reduce_fusion.2
  14.6 0.1 copy.29
  14.7 0.7 pad_maximum_fusion
  15.4 0.0 all-gather.2.cloned.1.call-update
  15.5 50.4 %all-gather.2.cloned.1.call-done.ka_ref.va_ref = bf16[1024,1024]{1,0:T(8,128)(2,1)} async-done(((bf16[128,1024]{1,0:T(8,128)(2,1)}), bf16[1024,1024]{1,0:T(8,128)(2,1)}) %all-gather.2.cloned.1.call-update) | async-done | bytes 2097168 | tf_op jit(solution)/shard_map/all_gather | solution.py:151
  65.8 6.2 %collective-permute-start = (bf16[1024,1024]{1,0:T(8,128)(2,1)}, bf16[1024,1024]{1,0:T(8,128)(2,1)}, u32[]{:S(2)}, u32[]{:S(2)}) collective-permute-start(bf16[1024,1024]{1,0:T(8,128)(2,1)} %all-gather.2.cloned.1.call-done.ka_ref.va_ref), channel_id=1, source_target_pairs={{0,1},{1,0},{2,3},{3,2},{4,5},{5,4},{6,7},{7,6},{8,9},{9,8},{10,11... | collective-permute-start | bytes 6291464 | tf_op jit(solution)/shard_map/ppermute | solution.py:152
  72.0 0.0 copy-done.4
  72.7 0.1 tile.15
  72.8 0.1 mul.103
  72.9 0.1 broadcast_in_dim.12
  73.0 0.1 mul.104
  73.1 0.1 iota_add_fusion
  73.2 0.1 add.58
  73.2 0.1 dynamic-slice_bitcast_fusion
  73.3 0.8 copy.27.qpos_ref
  74.1 0.0 copy-start.5
  74.1 0.2 copy.30
  74.2 0.2 fusion.7
  74.5 0.3 multiply_reduce_fusion
  74.8 0.1 copy.23
  74.9 0.1 copy.24
  75.0 0.6 constant_dynamic-slice_fusion
  75.6 0.0 copy-done.5
  75.6 0.6 multiply_bitcast_fusion.mult_ref
  76.2 0.3 mul.117
  76.5 1.3 %fusion.5.q_ref = bf16[128,2048]{1,0:T(8,128)(2,1)} fusion(f32[16,8,16,128]{3,2,1,0:T(8,128)S(1)} %bitcast.50, f32[2048]{0:T(1024)S(1)} %bitcast.57, f32[128]{0:T(128)S(1)} %add_rsqrt_fusion.2, f32[1,128,2048]{2,1,0:T(8,128)S(1)} %copy-done.1), kind=kLoop, calls=%fused_computation.4 | loop fusion | flops 1572864 | bytes 2630144 | tf_op jit(solution)/shard_map/convert_element_type | solution.py:144
  77.9 0.0 collective-permute-done.kb_ref.vb_ref
  77.9 12.9 %shard_map.82 = f32[128,2048]{1,0:T(8,128)} custom-call(f32[16]{0:T(128)} %multiply_bitcast_fusion.mult_ref, s32[1]{0:T(128)S(6)} %copy.34.tiers_ref, s32[128,1]{1,0:T(8,128)} %copy.27.qpos_ref, s32[1,1024]{1,0:T(1,128)} %bitcast.59, s32[1,1024]{1,0:T(1,128)} %bitcast.58, bf16[128,2048]{1,0:T(8,128)(2,1)} %fusion.5.q_ref, ...), custom_call_target="tpu_custom_call" | custom-call | flops 2147483648 | bytes 6815744 | tf_op jit(solution)/shard_map/pallas_call | solution.py:73
  90.8 3.1 %collective-permute-start.1 = (f32[1,128,2048]{2,1,0:T(8,128)}, f32[1,128,2048]{2,1,0:T(8,128)S(1)}, u32[]{:S(2)}, u32[]{:S(2)}) collective-permute-start(f32[1,128,2048]{2,1,0:T(8,128)} %bitcast.52), channel_id=1, source_target_pairs={{752,0},{0,16},{16,32},{32,48},{48,64},{64,80},{80,96},{96,112},{1... | collective-permute-start | bytes 3145736 | tf_op jit(solution)/shard_map/ppermute | solution.py:18
  93.9 29.1 %collective-permute-done.1 = f32[1,128,2048]{2,1,0:T(8,128)S(1)} collective-permute-done((f32[1,128,2048]{2,1,0:T(8,128)}, f32[1,128,2048]{2,1,0:T(8,128)S(1)}, u32[]{:S(2)}, u32[]{:S(2)}) %collective-permute-start.1) | collective-permute-done | bytes 1048608 | tf_op jit(solution)/shard_map/ppermute | solution.py:18
  122.9 1.0 copy.35
  (8 shorter events, 0.1 us)
Async XLA Ops:
  6.5 5.6 %copy-start = (bf16[1,1,2048,512]{3,2,1,0:T(8,128)(2,1)S(1)}, bf16[1,1,2048,512]{3,2,1,0:T(8,128)(2,1)}, u32[]{:S(2)}) copy-start(bf16[1,1,2048,512]{3,2,1,0:T(8,128)(2,1)} %param.13) | copy-start | bytes 6291460
  6.5 59.3 %all-gather.2.cloned.1.call-start = ((), (), s32[]{:S(2)}) async-start(), calls=%async_computation | async-start | bytes 2359296 | tf_op jit(solution)/shard_map/all_gather | solution.py:151
  8.1 4.1 %copy-start.1 = (f32[1,128,2048]{2,1,0:T(8,128)S(1)}, f32[1,128,2048]{2,1,0:T(8,128)}, u32[]{:S(2)}) copy-start(f32[1,128,2048]{2,1,0:T(8,128)} %param.8) | copy-start | bytes 3145732
  8.1 4.1 %copy-start.3 = (f32[1,1,2048]{2,1,0:T(1,128)S(1)}, f32[1,1,2048]{2,1,0:T(1,128)}, u32[]{:S(2)}) copy-start(f32[1,1,2048]{2,1,0:T(1,128)} %param.11) | copy-start | bytes 24580
  12.1 1.6 %copy-start.2 = (bf16[512,2048]{1,0:T(8,128)(2,1)S(1)}, bf16[512,2048]{1,0:T(8,128)(2,1)}, u32[]{:S(2)}) copy-start(bf16[512,2048]{1,0:T(8,128)(2,1)} %copy.28) | copy-start | bytes 6291460
  13.7 58.3 %copy-start.4 = (s32[32]{0:T(128)S(1)}, s32[32]{0:T(128)}, u32[]{:S(2)}) copy-start(s32[32]{0:T(128)} %param.10) | copy-start | bytes 388
  65.8 12.1 %collective-permute-start = (bf16[1024,1024]{1,0:T(8,128)(2,1)}, bf16[1024,1024]{1,0:T(8,128)(2,1)}, u32[]{:S(2)}, u32[]{:S(2)}) collective-permute-start(bf16[1024,1024]{1,0:T(8,128)(2,1)} %all-gather.2.cloned.1.call-done.ka_ref.va_ref), channel_id=1, source_target_pairs={{0,1},{1,0},{2,3},{3,2},{4,5},{5,4},{6,7},{7,6},{8,9},{9,8},{10,11... | collective-permute-start | bytes 6291464 | tf_op jit(solution)/shard_map/ppermute | solution.py:152
  74.1 1.6 %copy-start.5 = (f32[1,1,16]{2,1,0:T(1,128)S(1)}, f32[1,1,16]{2,1,0:T(1,128)}, u32[]{:S(2)}) copy-start(f32[1,1,16]{2,1,0:T(1,128)} %param.14) | copy-start | bytes 196
  90.8 32.1 %collective-permute-start.1 = (f32[1,128,2048]{2,1,0:T(8,128)}, f32[1,128,2048]{2,1,0:T(8,128)S(1)}, u32[]{:S(2)}, u32[]{:S(2)}) collective-permute-start(f32[1,128,2048]{2,1,0:T(8,128)} %bitcast.52), channel_id=1, source_target_pairs={{752,0},{0,16},{16,32},{32,48},{48,64},{64,80},{80,96},{96,112},{1... | collective-permute-start | bytes 3145736 | tf_op jit(solution)/shard_map/ppermute | solution.py:18
Sparse Core Ops, SparseCore 0:
  15.6 50.1 all-gather.1

commit v4 on v3

--- a/solution.py
+++ b/solution.py
@@ -41,15 +41,13 @@
         cols = slice(g * ATTN_UNIT_WIDTH, (g + 1) * ATTN_UNIT_WIDTH)
         qh = q_ref[:, cols]
         mult = mult_ref[c * group + g]
-        s_a = lax.dot_general(qh, ka, dims, preferred_element_type=jnp.float32) * mult
-        s_b = lax.dot_general(qh, kb, dims, preferred_element_type=jnp.float32) * mult
-        s_a = jnp.where(allowed_a, s_a, -1e30)
-        s_b = jnp.where(allowed_b, s_b, -1e30)
+        s_a = jnp.where(allowed_a, lax.dot_general(qh, ka, dims, preferred_element_type=jnp.float32), -1e30)
+        s_b = jnp.where(allowed_b, lax.dot_general(qh, kb, dims, preferred_element_type=jnp.float32), -1e30)
         row_max = jnp.maximum(
             jnp.max(s_a, axis=1, keepdims=True), jnp.max(s_b, axis=1, keepdims=True)
-        )
-        p_a = jnp.where(allowed_a, jnp.exp(s_a - row_max), 0.0)
-        p_b = jnp.where(allowed_b, jnp.exp(s_b - row_max), 0.0)
+        ) * mult
+        p_a = jnp.exp(s_a * mult - row_max)
+        p_b = jnp.exp(s_b * mult - row_max)
         total = jnp.sum(p_a, axis=1, keepdims=True) + jnp.sum(p_b, axis=1, keepdims=True)
         mixed = jnp.dot(
             p_a.astype(jnp.bfloat16), va, preferred_element_type=jnp.float32
@@ -57,6 +55,42 @@
         mixed = mixed / total
         x = x_ref[:, cols]
         out_ref[:, cols] = jnp.where(gate, x + w_ref[:, cols] * mixed, x)
+
+
+def prologue_kernel(x_ref, gain_ref, wk_ref, wv_ref, kv_ref, q_ref):
+    x = x_ref[...]
+    normed = (
+        x * lax.rsqrt(jnp.mean(x * x, axis=1, keepdims=True) + 1e-05) * gain_ref[...]
+    ).astype(jnp.bfloat16)
+    keys = jnp.dot(normed, wk_ref[...], preferred_element_type=jnp.float32)
+    kv_cols = keys.shape[1]
+    for c in range(kv_cols // ATTN_UNIT_WIDTH):
+        cols = slice(c * ATTN_UNIT_WIDTH, (c + 1) * ATTN_UNIT_WIDTH)
+        kv_ref[:, cols] = head_norm(keys[:, cols]).astype(jnp.bfloat16)
+    kv_ref[:, kv_cols:] = jnp.dot(
+        normed, wv_ref[...], preferred_element_type=jnp.float32
+    ).astype(jnp.bfloat16)
+    wide = normed.astype(jnp.float32)
+    for h in range(wide.shape[1] // ATTN_UNIT_WIDTH):
+        cols = slice(h * ATTN_UNIT_WIDTH, (h + 1) * ATTN_UNIT_WIDTH)
+        q_ref[:, cols] = head_norm(wide[:, cols]).astype(jnp.bfloat16)
+
+
+def prologue(x, gain, wk, wv):
+    rows, width = x.shape
+    kv_cols = wk.shape[1]
+    return pl.pallas_call(
+        prologue_kernel,
+        out_shape=(
+            jax.ShapeDtypeStruct((rows, 2 * kv_cols), jnp.bfloat16),
+            jax.ShapeDtypeStruct((rows, width), jnp.bfloat16),
+        ),
+        cost_estimate=pl.CostEstimate(
+            flops=4 * rows * width * kv_cols,
+            transcendentals=rows * 24,
+            bytes_accessed=2 * width * kv_cols * 2 + rows * width * 6 + rows * kv_cols * 4,
+        ),
+    )(x, gain, wk, wv)
 
 
 def attend_and_update(mult, tiers, qpos, kpos_a, kpos_b, queries, block_a, block_b, x, w_out):
@@ -108,7 +142,6 @@
     attention_result_weight,
 ):
     tok_rows = residual_flow.shape[1]
-    query_groups = H // KEY_VALUE_HEADS
     n_ctx = lax.axis_size("ctx")
     n_chips = n_ctx // 2
     me = lax.axis_index("ctx")
@@ -125,33 +158,22 @@
     pos_mine = lax.dynamic_index_in_dim(by_core, core, axis=1, keepdims=False).reshape(1, -1)
     pos_theirs = lax.dynamic_index_in_dim(by_core, 1 - core, axis=1, keepdims=False).reshape(1, -1)
 
-    normed = (
-        residual
-        * lax.rsqrt(jnp.mean(residual * residual, axis=-1, keepdims=True) + 1e-05)
-        * normalizer_weight_entries[0, 0]
-    ).astype(jnp.bfloat16)
-    keys_raw = jnp.dot(normed, lookup_map_weights[0, 0], preferred_element_type=jnp.float32)
-    key_unit = (
-        head_norm(keys_raw.reshape(tok_rows, KEY_VALUE_HEADS, ATTN_UNIT_WIDTH))
-        .astype(jnp.bfloat16)
-        .reshape(tok_rows, KEY_VALUE_HEADS * ATTN_UNIT_WIDTH)
-    )
-    values = jnp.dot(normed, content_map_weights[0, 0], preferred_element_type=jnp.float32).astype(
-        jnp.bfloat16
-    )
-    queries = (
-        head_norm(normed.astype(jnp.float32).reshape(tok_rows, H, ATTN_UNIT_WIDTH))
-        .astype(jnp.bfloat16)
-        .reshape(tok_rows, H * ATTN_UNIT_WIDTH)
-    )
-    own_block = jnp.concatenate([key_unit, values], axis=1)
+    own_block, queries = prologue(
+        residual,
+        normalizer_weight_entries[0],
+        lookup_map_weights[0, 0],
+        content_map_weights[0, 0],
+    )
+    mult = softmax_warmth[0, 0] / ATTN_UNIT_WIDTH
+    own_block, queries, query_pos, pos_mine, pos_theirs, mult = lax.optimization_barrier(
+        (own_block, queries, query_pos, pos_mine, pos_theirs, mult)
+    )
 
     same_core = [list(range(c, n_ctx, 2)) for c in range(2)]
     partner_route = [(i, i ^ 1) for i in range(n_ctx)]
     mine = lax.all_gather(own_block, "ctx", axis=0, tiled=True, axis_index_groups=same_core)
     theirs = lax.ppermute(mine, "ctx", partner_route)
 
-    mult = softmax_warmth[0, 0] / ATTN_UNIT_WIDTH
     residual = attend_and_update(
         mult,
         tiers_each_segment,

time: 131 us -> 127 us (0.969)
  local copies, waits for them, and re-layouts: 8.78 us -> 4.1 us
  Pallas kernels: 12.9 us -> 16 us
  other arithmetic: 4.86 us -> 1.93 us
  waiting for transfers between devices: 79.4 us -> 81.7 us
    pallas_call x0 -> x1, Pallas kernels: none -> 4.13 us  [prologue(): pl.pallas_call(prologue_kernel, out_shape=(jax.ShapeDtypeStruct((rows, 2...]
    dot_general x1 -> x0, local copies, waits for them, and re-layouts: 4.04 us -> none  [local(): jnp.dot(normed, lookup_map_weights[0, 0], preferred_element_type=jnp.floa...]
    ppermute x1, waiting for transfers between devices: 0.01 us -> 2.6 us  [local(): theirs = lax.ppermute(mine, 'ctx', partner_route)]
    reduce_sum x2 -> x0, other arithmetic: 1.87 us -> none  [the longest x1 1.53 us: local(): jnp.mean(residual * residual, axis=-1, keepdims=True) + 1e-05]
    convert_element_type x3 -> x0, other arithmetic: 1.58 us -> none  [the longest x1 1.34 us: local(): queries = head_norm(normed.astype(jnp.float32).reshape(tok_rows, H, ATTN_...]
  transfers between devices with their start and end apart: 3 -> 3, of which waited for: 2 -> 3; matrix products, arithmetic and copies ran while one was open for 4% -> 1% of each run, Pallas kernels for 0% -> 0%
where the time goes in v4:
time: 127 us
  waiting for transfers between devices  81.7 us (64%)
  Pallas kernels  16 us (13%)
  between operations  14.1 us (11%)
  starting transfers between devices  9.28 us (7%)
  local copies, waits for them, and re-layouts  4.1 us (3%)
  other arithmetic  1.93 us (2%)
    all_gather x1, waiting for transfers between devices, local(): lax.all_gather(own_block, 'ctx', axis=0, tiled=True, axis_index_groups=sa...  50.4 us
    ppermute x1, waiting for transfers between devices, passed_along(): return lax.ppermute(block, axis, route)  28.8 us
    pallas_call x1, Pallas kernels, attend_and_update(): pl.pallas_call(attention_kernel, grid=(kv_heads,), in_specs=[smem, smem,...  11.9 us
    ppermute x1, starting transfers between devices, local(): theirs = lax.ppermute(mine, 'ctx', partner_route)  6.2 us
    pallas_call x1, Pallas kernels, prologue(): pl.pallas_call(prologue_kernel, out_shape=(jax.ShapeDtypeStruct((rows, 2...  4.13 us
    ppermute x1, starting transfers between devices, passed_along(): return lax.ppermute(block, axis, route)  3.08 us
    ppermute x1, waiting for transfers between devices, local(): theirs = lax.ppermute(mine, 'ctx', partner_route)  2.6 us
  transfers between devices with their start and end apart: 3, of which 3 were waited for; matrix products, arithmetic and copies ran while one was open for 1% of the time, Pallas kernels for 0%

profile of v4, /device:TPU:1, one launch (start us, length us, event | category | flops | bytes accessed | tf_op | source)
XLA Modules:
  0.0 127.2 jit_solution(10883261178242112096)
XLA Ops:
  6.5 0.0 all-gather.2.cloned.1.call-start
  6.5 0.7 broadcast_multiply_fusion
  7.2 0.1 mul.22
  7.3 0.1 iota_add_fusion
  7.4 1.2 multiply_bitcast_fusion.mult_ref
  8.6 0.1 tile.15
  8.7 0.1 broadcast_in_dim.9
  8.7 0.1 mul.23
  8.8 0.1 add.25
  8.9 0.1 dynamic-slice_bitcast_fusion
  9.0 0.6 constant_dynamic-slice_fusion
  9.6 4.1 %shard_map.82 = (bf16[128,1024]{1,0:T(8,128)(2,1)}, bf16[128,2048]{1,0:T(8,128)(2,1)}) custom-call(f32[128,2048]{1,0:T(8,128)} %bitcast.14, f32[1,2048]{1,0:T(1,128)} %bitcast.21, bf16[2048,512]{1,0:T(8,128)(2,1)} %bitcast.16, bf16[2048,512]{1,0:T(8,128)(2,1)} %bitcast.17), custom_call_target="tpu_custom_call" | custom-call | flops 536870912 | bytes 6029312 | tf_op jit(solution)/shard_map/pallas_call | solution.py:82
  13.7 0.0 all-gather.2.cloned.1.call-update
  13.7 50.4 %all-gather.2.cloned.1.call-done.ka_ref.va_ref = bf16[1024,1024]{1,0:T(8,128)(2,1)} async-done(((bf16[128,1024]{1,0:T(8,128)(2,1)}), bf16[1024,1024]{1,0:T(8,128)(2,1)}) %all-gather.2.cloned.1.call-update) | async-done | bytes 2097168 | tf_op jit(solution)/shard_map/all_gather | solution.py:174
  64.1 6.2 %collective-permute-start = (bf16[1024,1024]{1,0:T(8,128)(2,1)}, bf16[1024,1024]{1,0:T(8,128)(2,1)S(1)}, u32[]{:S(2)}, u32[]{:S(2)}) collective-permute-start(bf16[1024,1024]{1,0:T(8,128)(2,1)} %all-gather.2.cloned.1.call-done.ka_ref.va_ref), channel_id=1, source_target_pairs={{0,1},{1,0},{2,3},{3,2},{4,5},{5,4},{6,7},{7,6},{8,9},{9,8},{10,11... | collective-permute-start | bytes 6291464 | tf_op jit(solution)/shard_map/ppermute | solution.py:175
  70.9 0.7 copy.12.qpos_ref
  71.7 2.6 %collective-permute-done.kb_ref.vb_ref = bf16[1024,1024]{1,0:T(8,128)(2,1)S(1)} collective-permute-done((bf16[1024,1024]{1,0:T(8,128)(2,1)}, bf16[1024,1024]{1,0:T(8,128)(2,1)S(1)}, u32[]{:S(2)}, u32[]{:S(2)}) %collective-permute-start) | collective-permute-done | bytes 2097184 | tf_op jit(solution)/shard_map/ppermute | solution.py:175
  74.3 0.0 copy-start
  74.3 1.3 %copy-done = bf16[1024,1024]{1,0:T(8,128)(2,1)} copy-done((bf16[1024,1024]{1,0:T(8,128)(2,1)}, bf16[1024,1024]{1,0:T(8,128)(2,1)S(1)}, u32[]{:S(2)}) %copy-start) | copy-done | bytes 2097176
  75.6 11.9 %shard_map.83 = f32[128,2048]{1,0:T(8,128)} custom-call(f32[16]{0:T(128)} %multiply_bitcast_fusion.mult_ref, s32[1]{0:T(128)S(6)} %copy.14.tiers_ref, s32[128,1]{1,0:T(8,128)} %copy.12.qpos_ref, s32[1,1024]{1,0:T(1,128)} %bitcast.20, s32[1,1024]{1,0:T(1,128)} %bitcast.19, bf16[128,2048]{1,0:T(8,128)(2,1)} %get-tuple-element.19.q_ref, ...), custom_call_target="tpu_custom_call" | custom-call | flops 2147483648 | bytes 6815744 | tf_op jit(solution)/shard_map/pallas_call | solution.py:107
  87.5 3.1 %collective-permute-start.1 = (f32[1,128,2048]{2,1,0:T(8,128)}, f32[1,128,2048]{2,1,0:T(8,128)S(1)}, u32[]{:S(2)}, u32[]{:S(2)}) collective-permute-start(f32[1,128,2048]{2,1,0:T(8,128)} %bitcast.18), channel_id=1, source_target_pairs={{752,0},{0,16},{16,32},{32,48},{48,64},{64,80},{80,96},{96,112},{1... | collective-permute-start | bytes 3145736 | tf_op jit(solution)/shard_map/ppermute | solution.py:18
  90.6 28.8 %collective-permute-done.1 = f32[1,128,2048]{2,1,0:T(8,128)S(1)} collective-permute-done((f32[1,128,2048]{2,1,0:T(8,128)}, f32[1,128,2048]{2,1,0:T(8,128)S(1)}, u32[]{:S(2)}, u32[]{:S(2)}) %collective-permute-start.1) | collective-permute-done | bytes 1048608 | tf_op jit(solution)/shard_map/ppermute | solution.py:18
  119.3 1.0 copy.15
  (3 shorter events, 0.0 us)
Async XLA Ops:
  6.5 57.6 %all-gather.2.cloned.1.call-start = ((), (), s32[]{:S(2)}) async-start(), calls=%async_computation | async-start | bytes 2359296 | tf_op jit(solution)/shard_map/all_gather | solution.py:174
  64.1 10.2 %collective-permute-start = (bf16[1024,1024]{1,0:T(8,128)(2,1)}, bf16[1024,1024]{1,0:T(8,128)(2,1)S(1)}, u32[]{:S(2)}, u32[]{:S(2)}) collective-permute-start(bf16[1024,1024]{1,0:T(8,128)(2,1)} %all-gather.2.cloned.1.call-done.ka_ref.va_ref), channel_id=1, source_target_pairs={{0,1},{1,0},{2,3},{3,2},{4,5},{5,4},{6,7},{7,6},{8,9},{9,8},{10,11... | collective-permute-start | bytes 6291464 | tf_op jit(solution)/shard_map/ppermute | solution.py:175
  74.3 1.3 %copy-start = (bf16[1024,1024]{1,0:T(8,128)(2,1)}, bf16[1024,1024]{1,0:T(8,128)(2,1)S(1)}, u32[]{:S(2)}) copy-start(bf16[1024,1024]{1,0:T(8,128)(2,1)S(1)} %collective-permute-done.kb_ref.vb_ref) | copy-start | bytes 6291460
  87.5 31.8 %collective-permute-start.1 = (f32[1,128,2048]{2,1,0:T(8,128)}, f32[1,128,2048]{2,1,0:T(8,128)S(1)}, u32[]{:S(2)}, u32[]{:S(2)}) collective-permute-start(f32[1,128,2048]{2,1,0:T(8,128)} %bitcast.18), channel_id=1, source_target_pairs={{752,0},{0,16},{16,32},{32,48},{48,64},{64,80},{80,96},{96,112},{1... | collective-permute-start | bytes 3145736 | tf_op jit(solution)/shard_map/ppermute | solution.py:18
Sparse Core Ops, SparseCore 0:
  13.9 50.1 all-gather.1

commit v5 on v4

--- a/solution.py
+++ b/solution.py
@@ -22,36 +22,47 @@
     return values * lax.rsqrt(jnp.mean(values * values, axis=-1, keepdims=True) + 1e-05)
 
 
-def attention_kernel(
-    mult_ref, tiers_ref, qpos_ref, kpos_a_ref, kpos_b_ref, q_ref,
-    ka_ref, va_ref, kb_ref, vb_ref, x_ref, w_ref, out_ref,
+def first_half_kernel(mult_ref, qpos_ref, kpos_ref, q_ref, k_ref, v_ref, m_ref, l_ref, acc_ref):
+    c = pl.program_id(0)
+    group = q_ref.shape[1] // ATTN_UNIT_WIDTH
+    allowed = kpos_ref[...] <= qpos_ref[...]
+    k = k_ref[...]
+    v = v_ref[...]
+    dims = (((1,), (1,)), ((), ()))
+    for g in range(group):
+        cols = slice(g * ATTN_UNIT_WIDTH, (g + 1) * ATTN_UNIT_WIDTH)
+        mult = mult_ref[c * group + g]
+        s = jnp.where(allowed, lax.dot_general(q_ref[:, cols], k, dims, preferred_element_type=jnp.float32), -1e30)
+        row_max = jnp.max(s, axis=1, keepdims=True) * mult
+        p = jnp.exp(s * mult - row_max)
+        m_ref[:, cols] = jnp.broadcast_to(row_max, (row_max.shape[0], ATTN_UNIT_WIDTH))
+        l_ref[:, cols] = jnp.broadcast_to(jnp.sum(p, axis=1, keepdims=True), (p.shape[0], ATTN_UNIT_WIDTH))
+        acc_ref[:, cols] = jnp.dot(p.astype(jnp.bfloat16), v, preferred_element_type=jnp.float32)
+
+
+def second_half_kernel(
+    mult_ref, tiers_ref, qpos_ref, kpos_ref, q_ref, k_ref, v_ref, m_ref, l_ref, acc_ref,
+    x_ref, w_ref, out_ref,
 ):
     c = pl.program_id(0)
     group = q_ref.shape[1] // ATTN_UNIT_WIDTH
-    qpos = qpos_ref[...]
-    allowed_a = kpos_a_ref[...] <= qpos
-    allowed_b = kpos_b_ref[...] <= qpos
-    ka = ka_ref[...]
-    kb = kb_ref[...]
-    va = va_ref[...]
-    vb = vb_ref[...]
+    allowed = kpos_ref[...] <= qpos_ref[...]
+    k = k_ref[...]
+    v = v_ref[...]
     gate = tiers_ref[0] > 0
     dims = (((1,), (1,)), ((), ()))
     for g in range(group):
         cols = slice(g * ATTN_UNIT_WIDTH, (g + 1) * ATTN_UNIT_WIDTH)
-        qh = q_ref[:, cols]
         mult = mult_ref[c * group + g]
-        s_a = jnp.where(allowed_a, lax.dot_general(qh, ka, dims, preferred_element_type=jnp.float32), -1e30)
-        s_b = jnp.where(allowed_b, lax.dot_general(qh, kb, dims, preferred_element_type=jnp.float32), -1e30)
-        row_max = jnp.maximum(
-            jnp.max(s_a, axis=1, keepdims=True), jnp.max(s_b, axis=1, keepdims=True)
-        ) * mult
-        p_a = jnp.exp(s_a * mult - row_max)
-        p_b = jnp.exp(s_b * mult - row_max)
-        total = jnp.sum(p_a, axis=1, keepdims=True) + jnp.sum(p_b, axis=1, keepdims=True)
-        mixed = jnp.dot(
-            p_a.astype(jnp.bfloat16), va, preferred_element_type=jnp.float32
-        ) + jnp.dot(p_b.astype(jnp.bfloat16), vb, preferred_element_type=jnp.float32)
+        s = jnp.where(allowed, lax.dot_general(q_ref[:, cols], k, dims, preferred_element_type=jnp.float32), -1e30)
+        old_max = m_ref[:, cols][:, :1]
+        row_max = jnp.maximum(old_max, jnp.max(s, axis=1, keepdims=True) * mult)
+        p = jnp.exp(s * mult - row_max)
+        scale = jnp.exp(old_max - row_max)
+        total = l_ref[:, cols] * scale + jnp.sum(p, axis=1, keepdims=True)
+        mixed = acc_ref[:, cols] * scale + jnp.dot(
+            p.astype(jnp.bfloat16), v, preferred_element_type=jnp.float32
+        )
         mixed = mixed / total
         x = x_ref[:, cols]
         out_ref[:, cols] = jnp.where(gate, x + w_ref[:, cols] * mixed, x)
@@ -103,32 +114,31 @@
     cols = lambda shape: pl.BlockSpec(shape, lambda c: (0, c))
     values_at = lambda shape: pl.BlockSpec(shape, lambda c: (0, c + kv_heads))
     kv_block = (kv_rows, ATTN_UNIT_WIDTH)
-    flops = 4 * rows * 2 * kv_rows * ATTN_UNIT_WIDTH * H
+    wide = cols((rows, head_cols))
+    state = jax.ShapeDtypeStruct((rows, width), jnp.float32)
+    flops = 4 * rows * kv_rows * ATTN_UNIT_WIDTH * H
+    cost = pl.CostEstimate(
+        flops=flops, transcendentals=rows * kv_rows * H, bytes_accessed=2 * kv_rows * 1024 + rows * width * 16
+    )
+    running = pl.pallas_call(
+        first_half_kernel,
+        grid=(kv_heads,),
+        in_specs=[smem, whole((rows, 1)), whole((1, kv_rows)), wide, cols(kv_block), values_at(kv_block)],
+        out_specs=[wide, wide, wide],
+        out_shape=[state, state, state],
+        cost_estimate=cost,
+    )(mult, qpos, kpos_a, queries, block_a, block_a)
     return pl.pallas_call(
-        attention_kernel,
+        second_half_kernel,
         grid=(kv_heads,),
         in_specs=[
-            smem,
-            smem,
-            whole((rows, 1)),
-            whole((1, kv_rows)),
-            whole((1, kv_rows)),
-            cols((rows, head_cols)),
-            cols(kv_block),
-            values_at(kv_block),
-            cols(kv_block),
-            values_at(kv_block),
-            cols((rows, head_cols)),
-            cols((1, head_cols)),
+            smem, smem, whole((rows, 1)), whole((1, kv_rows)), wide, cols(kv_block), values_at(kv_block),
+            wide, wide, wide, wide, cols((1, head_cols)),
         ],
-        out_specs=cols((rows, head_cols)),
-        out_shape=jax.ShapeDtypeStruct((rows, width), jnp.float32),
-        cost_estimate=pl.CostEstimate(
-            flops=flops,
-            transcendentals=rows * 2 * kv_rows * H,
-            bytes_accessed=4 * kv_rows * 1024 + rows * width * 10,
-        ),
-    )(mult, tiers, qpos, kpos_a, kpos_b, queries, block_a, block_a, block_b, block_b, x, w_out)
+        out_specs=wide,
+        out_shape=state,
+        cost_estimate=cost,
+    )(mult, tiers, qpos, kpos_b, queries, block_b, block_b, *running, x, w_out)
 
 
 def local(

time: 127 us -> 132 us (1.039)
  Pallas kernels: 16 us -> 22.5 us
  waiting for transfers between devices: 81.7 us -> 79.4 us
    pallas_call x1 -> x2, Pallas kernels: 11.9 us -> 18.4 us  [the longest x1 10 us: attend_and_update(): pl.pallas_call(second_half_kernel, grid=(kv_heads,), in_specs=[smem, smem...]
    ppermute x1, waiting for transfers between devices: 2.6 us -> 0.01 us  [local(): theirs = lax.ppermute(mine, 'ctx', partner_route)]
  transfers between devices with their start and end apart: 3 -> 3, of which waited for: 3 -> 2; matrix products, arithmetic and copies ran while one was open for 1% -> 1% of each run, Pallas kernels for 0% -> 6%
where the time goes in v5:
time: 132 us; the launch traced here: 131 us
  waiting for transfers between devices  79.4 us (60%)
  Pallas kernels  22.5 us (17%)
  between operations  14.1 us (11%)
  starting transfers between devices  9.28 us (7%)
  local copies, waits for them, and re-layouts  4.14 us (3%)
  other arithmetic  1.91 us (1%)
    all_gather x1, waiting for transfers between devices, local(): lax.all_gather(own_block, 'ctx', axis=0, tiled=True, axis_index_groups=sa...  50.3 us
    ppermute x1, waiting for transfers between devices, passed_along(): return lax.ppermute(block, axis, route)  29.1 us
    pallas_call x1, Pallas kernels, attend_and_update(): pl.pallas_call(second_half_kernel, grid=(kv_heads,), in_specs=[smem, smem...  10 us
    pallas_call x1, Pallas kernels, attend_and_update(): pl.pallas_call(first_half_kernel, grid=(kv_heads,), in_specs=[smem, whole...  8.33 us
    ppermute x1, starting transfers between devices, local(): theirs = lax.ppermute(mine, 'ctx', partner_route)  6.2 us
    pallas_call x1, Pallas kernels, prologue(): pl.pallas_call(prologue_kernel, out_shape=(jax.ShapeDtypeStruct((rows, 2...  4.14 us
    ppermute x1, starting transfers between devices, passed_along(): return lax.ppermute(block, axis, route)  3.08 us
  transfers between devices with their start and end apart: 3, of which 2 were waited for; matrix products, arithmetic and copies ran while one was open for 1% of the time, Pallas kernels for 6%

profile of v5, /device:TPU:1, one launch (start us, length us, event | category | flops | bytes accessed | tf_op | source)
XLA Modules:
  0.0 131.4 jit_solution(1029317136614870922)
XLA Ops:
  6.5 0.0 all-gather.2.cloned.1.call-start
  6.5 0.7 broadcast_multiply_fusion
  7.2 0.1 mul.22
  7.3 0.1 iota_add_fusion
  7.4 1.2 multiply_bitcast_fusion.mult_ref
  8.6 0.1 tile.15
  8.6 0.1 broadcast_in_dim.9
  8.7 0.1 mul.23
  8.8 0.1 add.25
  8.9 0.1 dynamic-slice_bitcast_fusion
  9.0 0.6 constant_dynamic-slice_fusion
  9.6 4.1 %shard_map.82 = (bf16[128,1024]{1,0:T(8,128)(2,1)}, bf16[128,2048]{1,0:T(8,128)(2,1)}) custom-call(f32[128,2048]{1,0:T(8,128)} %bitcast.14, f32[1,2048]{1,0:T(1,128)} %bitcast.21, bf16[2048,512]{1,0:T(8,128)(2,1)} %bitcast.16, bf16[2048,512]{1,0:T(8,128)(2,1)} %bitcast.17), custom_call_target="tpu_custom_call" | custom-call | flops 536870912 | bytes 6029312 | tf_op jit(solution)/shard_map/pallas_call | solution.py:93
  13.7 0.0 all-gather.2.cloned.1.call-update
  13.7 50.3 %all-gather.2.cloned.1.call-done.k_ref.v_ref = bf16[1024,1024]{1,0:T(8,128)(2,1)} async-done(((bf16[128,1024]{1,0:T(8,128)(2,1)}), bf16[1024,1024]{1,0:T(8,128)(2,1)}) %all-gather.2.cloned.1.call-update) | async-done | bytes 2097168 | tf_op jit(solution)/shard_map/all_gather | solution.py:184
  64.1 6.2 %collective-permute-start = (bf16[1024,1024]{1,0:T(8,128)(2,1)}, bf16[1024,1024]{1,0:T(8,128)(2,1)S(1)}, u32[]{:S(2)}, u32[]{:S(2)}) collective-permute-start(bf16[1024,1024]{1,0:T(8,128)(2,1)} %all-gather.2.cloned.1.call-done.k_ref.v_ref), channel_id=1, source_target_pairs={{0,1},{1,0},{2,3},{3,2},{4,5},{5,4},{6,7},{7,6},{8,9},{9,8},{10,11... | collective-permute-start | bytes 6291464 | tf_op jit(solution)/shard_map/ppermute | solution.py:185
  70.9 0.7 copy.14.qpos_ref
  71.7 8.3 %shard_map.83 = (f32[128,2048]{1,0:T(8,128)}, f32[128,2048]{1,0:T(8,128)}, f32[128,2048]{1,0:T(8,128)}) custom-call(f32[16]{0:T(128)} %multiply_bitcast_fusion.mult_ref, s32[128,1]{1,0:T(8,128)} %copy.14.qpos_ref, s32[1,1024]{1,0:T(1,128)} %bitcast.20, bf16[128,2048]{1,0:T(8,128)(2,1)} %get-tuple-element.21.q_ref, ...), custom_call_target="tpu_custom_call" | custom-call | flops 1073741824 | bytes 6291456 | tf_op jit(solution)/shard_map/pallas_call | solution.py:123
  80.0 0.0 collective-permute-done.k_ref.v_ref
  80.0 0.0 copy-start
  80.0 1.3 %copy-done = bf16[1024,1024]{1,0:T(8,128)(2,1)} copy-done((bf16[1024,1024]{1,0:T(8,128)(2,1)}, bf16[1024,1024]{1,0:T(8,128)(2,1)S(1)}, u32[]{:S(2)}) %copy-start) | copy-done | bytes 2097176
  81.4 10.0 %shard_map.84 = f32[128,2048]{1,0:T(8,128)} custom-call(f32[16]{0:T(128)} %multiply_bitcast_fusion.mult_ref, s32[1]{0:T(128)S(6)} %copy.16.tiers_ref, s32[128,1]{1,0:T(8,128)} %copy.14.qpos_ref, s32[1,1024]{1,0:T(1,128)} %bitcast.19, bf16[128,2048]{1,0:T(8,128)(2,1)} %get-tuple-element.21.q_ref, bf16[1024,1024]{1,0:T(8,128)(2,1)} %copy-done, ...), custom_call_target="tpu_custom_call" | custom-call | flops 1073741824 | bytes 6291456 | tf_op jit(solution)/shard_map/pallas_call | solution.py:131
  91.4 3.1 %collective-permute-start.1 = (f32[1,128,2048]{2,1,0:T(8,128)}, f32[1,128,2048]{2,1,0:T(8,128)S(1)}, u32[]{:S(2)}, u32[]{:S(2)}) collective-permute-start(f32[1,128,2048]{2,1,0:T(8,128)} %bitcast.18), channel_id=1, source_target_pairs={{752,0},{0,16},{16,32},{32,48},{48,64},{64,80},{80,96},{96,112},{1... | collective-permute-start | bytes 3145736 | tf_op jit(solution)/shard_map/ppermute | solution.py:18
  94.5 29.1 %collective-permute-done.1 = f32[1,128,2048]{2,1,0:T(8,128)S(1)} collective-permute-done((f32[1,128,2048]{2,1,0:T(8,128)}, f32[1,128,2048]{2,1,0:T(8,128)S(1)}, u32[]{:S(2)}, u32[]{:S(2)}) %collective-permute-start.1) | collective-permute-done | bytes 1048608 | tf_op jit(solution)/shard_map/ppermute | solution.py:18
  123.6 1.0 copy.17
  (3 shorter events, 0.0 us)
Async XLA Ops:
  6.5 57.5 %all-gather.2.cloned.1.call-start = ((), (), s32[]{:S(2)}) async-start(), calls=%async_computation | async-start | bytes 2359296 | tf_op jit(solution)/shard_map/all_gather | solution.py:184
  64.1 15.9 %collective-permute-start = (bf16[1024,1024]{1,0:T(8,128)(2,1)}, bf16[1024,1024]{1,0:T(8,128)(2,1)S(1)}, u32[]{:S(2)}, u32[]{:S(2)}) collective-permute-start(bf16[1024,1024]{1,0:T(8,128)(2,1)} %all-gather.2.cloned.1.call-done.k_ref.v_ref), channel_id=1, source_target_pairs={{0,1},{1,0},{2,3},{3,2},{4,5},{5,4},{6,7},{7,6},{8,9},{9,8},{10,11... | collective-permute-start | bytes 6291464 | tf_op jit(solution)/shard_map/ppermute | solution.py:185
  80.0 1.3 %copy-start = (bf16[1024,1024]{1,0:T(8,128)(2,1)}, bf16[1024,1024]{1,0:T(8,128)(2,1)S(1)}, u32[]{:S(2)}) copy-start(bf16[1024,1024]{1,0:T(8,128)(2,1)S(1)} %collective-permute-done.k_ref.v_ref) | copy-start | bytes 6291460
  91.4 32.2 %collective-permute-start.1 = (f32[1,128,2048]{2,1,0:T(8,128)}, f32[1,128,2048]{2,1,0:T(8,128)S(1)}, u32[]{:S(2)}, u32[]{:S(2)}) collective-permute-start(f32[1,128,2048]{2,1,0:T(8,128)} %bitcast.18), channel_id=1, source_target_pairs={{752,0},{0,16},{16,32},{32,48},{48,64},{64,80},{80,96},{96,112},{1... | collective-permute-start | bytes 3145736 | tf_op jit(solution)/shard_map/ppermute | solution.py:18
Sparse Core Ops, SparseCore 0:
  13.8 50.1 all-gather.1

commit v6 on v4

--- a/solution.py
+++ b/solution.py
@@ -146,6 +146,7 @@
     n_chips = n_ctx // 2
     me = lax.axis_index("ctx")
     core = me % 2
+    chip = me // 2
     half_rows = tok_rows // 2
     residual = residual_flow[0]
 
@@ -154,9 +155,17 @@
         + jnp.tile(jnp.arange(half_rows, dtype=jnp.int32), resident_tile_order.shape[0])
     )
     query_pos = lax.dynamic_slice(all_pos, (me * tok_rows,), (tok_rows,)).reshape(tok_rows, 1)
-    by_core = all_pos.reshape(n_chips, 2, tok_rows)
-    pos_mine = lax.dynamic_index_in_dim(by_core, core, axis=1, keepdims=False).reshape(1, -1)
-    pos_theirs = lax.dynamic_index_in_dim(by_core, 1 - core, axis=1, keepdims=False).reshape(1, -1)
+    by_part = all_pos.reshape(n_chips, 2, 2, half_rows)
+    behind = (chip - jnp.arange(n_chips, dtype=jnp.int32)) % n_chips
+
+    def key_positions(of_core):
+        rows = lax.dynamic_index_in_dim(by_part, of_core, axis=1, keepdims=False)
+        first = rows[:, 0, :].reshape(-1)
+        second = jnp.take(rows[:, 1, :], behind, axis=0).reshape(-1)
+        return jnp.concatenate([first, second]).reshape(1, -1)
+
+    pos_mine = key_positions(core)
+    pos_theirs = key_positions(1 - core)
 
     own_block, queries = prologue(
         residual,
@@ -171,7 +180,14 @@
 
     same_core = [list(range(c, n_ctx, 2)) for c in range(2)]
     partner_route = [(i, i ^ 1) for i in range(n_ctx)]
-    mine = lax.all_gather(own_block, "ctx", axis=0, tiled=True, axis_index_groups=same_core)
+    first_half = lax.all_gather(
+        own_block[:half_rows], "ctx", axis=0, tiled=True, axis_index_groups=same_core
+    )
+    second_halves = [own_block[half_rows:]]
+    for distance in range(1, n_chips):
+        route = [(i, ((i // 2 + distance) % n_chips) * 2 + i % 2) for i in range(n_ctx)]
+        second_halves.append(lax.ppermute(own_block[half_rows:], "ctx", route))
+    mine = jnp.concatenate([first_half] + second_halves, axis=0)
     theirs = lax.ppermute(mine, "ctx", partner_route)
 
     residual = attend_and_update(

time: 127 us -> 163 us (1.28)
  starting transfers between devices: 9.28 us -> 39.1 us
  local copies, waits for them, and re-layouts: 4.1 us -> 6.52 us
  waiting for transfers between devices: 81.7 us -> 83.4 us
    ppermute x0 -> x7, starting transfers between devices: none -> 24.8 us  [local(): second_halves.append(lax.ppermute(own_block[half_rows:], 'ctx', route))]
    ppermute x1, starting transfers between devices: 6.2 us -> 12 us  [local(): theirs = lax.ppermute(mine, 'ctx', partner_route)]
    ppermute x0 -> x7, waiting for transfers between devices: none -> 5.37 us  [local(): second_halves.append(lax.ppermute(own_block[half_rows:], 'ctx', route))]
    all_gather x1, waiting for transfers between devices: 50.4 us -> 46.7 us  [local(): lax.all_gather(own_block[:half_rows], 'ctx', axis=0, tiled=True, axis_ind...]
    slice x0 -> x3, local copies, waits for them, and re-layouts: none -> 1.67 us  [the longest x1 1.65 us: local(): own_block[:half_rows]]
  transfers between devices with their start and end apart: 3 -> 10, of which waited for: 3 -> 5; matrix products, arithmetic and copies ran while one was open for 1% -> 0% of each run, Pallas kernels for 0% -> 0%
where the time goes in v6:
time: 163 us
  waiting for transfers between devices  83.4 us (51%)
  starting transfers between devices  39.1 us (24%)
  Pallas kernels  16.1 us (10%)
  between operations  14.2 us (9%)
  local copies, waits for them, and re-layouts  6.52 us (4%)
  other arithmetic  3.34 us (2%)
    all_gather x1, waiting for transfers between devices, local(): lax.all_gather(own_block[:half_rows], 'ctx', axis=0, tiled=True, axis_ind...  46.7 us
    ppermute x1, waiting for transfers between devices, passed_along(): return lax.ppermute(block, axis, route)  28.8 us
    ppermute x7, starting transfers between devices, local(): second_halves.append(lax.ppermute(own_block[half_rows:], 'ctx', route))  24.8 us
    ppermute x1, starting transfers between devices, local(): theirs = lax.ppermute(mine, 'ctx', partner_route)  12 us
    pallas_call x1, Pallas kernels, attend_and_update(): pl.pallas_call(attention_kernel, grid=(kv_heads,), in_specs=[smem, smem,...  11.9 us
    ppermute x7, waiting for transfers between devices, local(): second_halves.append(lax.ppermute(own_block[half_rows:], 'ctx', route))  5.37 us
    pallas_call x1, Pallas kernels, prologue(): pl.pallas_call(prologue_kernel, out_shape=(jax.ShapeDtypeStruct((rows, 2...  4.13 us
  transfers between devices with their start and end apart: 10, of which 5 were waited for; matrix products, arithmetic and copies ran while one was open for 0% of the time, Pallas kernels for 0%

profile of v6, /device:TPU:1, one launch (start us, length us, event | category | flops | bytes accessed | tf_op | source)
XLA Modules:
  0.0 162.7 jit_solution(18293488349956928137)
XLA Ops:
  6.5 0.0 all-gather.2.cloned.1.call-start
  6.6 0.7 broadcast_multiply_fusion
  7.2 0.1 mul.19
  7.3 0.1 iota_add_fusion.1
  7.4 1.2 multiply_bitcast_fusion.mult_ref
  8.6 0.1 copy.11
  8.7 0.1 iota_add_fusion
  8.8 0.1 reshape_squeeze.7
  8.9 0.1 reshape_squeeze.6
  9.0 0.6 gather_fusion.1
  9.5 0.6 gather_fusion
  10.1 0.1 broadcast_select_fusion
  10.2 0.1 reshape.40
  10.2 0.1 reshape.38
  10.3 0.1 add.35
  10.4 0.6 pad_add_fusion.1
  11.0 0.6 pad_add_fusion
  11.6 0.1 dynamic-slice_bitcast_fusion.2
  11.7 4.1 %shard_map.82 = (bf16[128,1024]{1,0:T(8,128)(2,1)}, bf16[128,2048]{1,0:T(8,128)(2,1)}) custom-call(f32[128,2048]{1,0:T(8,128)} %bitcast.24, f32[1,2048]{1,0:T(1,128)} %bitcast.31, bf16[2048,512]{1,0:T(8,128)(2,1)} %bitcast.26, bf16[2048,512]{1,0:T(8,128)(2,1)} %bitcast.27), custom_call_target="tpu_custom_call" | custom-call | flops 536870912 | bytes 6029312 | tf_op jit(solution)/shard_map/pallas_call | solution.py:82
  15.8 0.0 copy-start.1
  15.8 1.6 %slice.29 = bf16[64,1024]{1,0:T(8,128)(2,1)} slice(bf16[128,1024]{1,0:T(8,128)(2,1)} %get-tuple-element.21), slice={[0:64], [0:1024]} | slice | bytes 262144 | tf_op jit(solution)/shard_map/slice | solution.py:184
  17.4 0.0 all-gather.2.cloned.1.call-update
  17.5 46.7 %all-gather.2.cloned.1.call-done = bf16[512,1024]{1,0:T(8,128)(2,1)} async-done(((bf16[64,1024]{1,0:T(8,128)(2,1)}), bf16[512,1024]{1,0:T(8,128)(2,1)}) %all-gather.2.cloned.1.call-update) | async-done | bytes 1048592 | tf_op jit(solution)/shard_map/all_gather | solution.py:183
  64.2 1.3 constant_dynamic-update-slice_fusion.8
  65.5 0.0 copy-done.1
  65.5 2.8 %collective-permute-start = (bf16[64,1024]{1,0:T(8,128)(2,1)S(1)}, bf16[64,1024]{1,0:T(8,128)(2,1)S(1)}, u32[]{:S(2)}, u32[]{:S(2)}) collective-permute-start(bf16[64,1024]{1,0:T(8,128)(2,1)S(1)} %get-tuple-element.22), channel_id=1, source_target_pairs={{0,2},{1,3},{2,4},{3,5},{4,6},{5,7},{6,8},{7,9},{8,10},{9,11},{10,... | collective-permute-start | bytes 393224 | tf_op jit(solution)/shard_map/ppermute | solution.py:189
  68.4 3.4 %collective-permute-start.1 = (bf16[64,1024]{1,0:T(8,128)(2,1)S(1)}, bf16[64,1024]{1,0:T(8,128)(2,1)S(1)}, u32[]{:S(2)}, u32[]{:S(2)}) collective-permute-start(bf16[64,1024]{1,0:T(8,128)(2,1)S(1)} %get-tuple-element.22), channel_id=1, source_target_pairs={{0,4},{1,5},{2,6},{3,7},{4,8},{5,9},{6,10},{7,11},{8,12},{9,13},{1... | collective-permute-start | bytes 393224 | tf_op jit(solution)/shard_map/ppermute | solution.py:189
  71.8 3.6 %collective-permute-start.6 = (bf16[64,1024]{1,0:T(8,128)(2,1)S(1)}, bf16[64,1024]{1,0:T(8,128)(2,1)S(1)}, u32[]{:S(2)}, u32[]{:S(2)}) collective-permute-start(bf16[64,1024]{1,0:T(8,128)(2,1)S(1)} %get-tuple-element.22), channel_id=1, source_target_pairs={{0,14},{1,15},{2,0},{3,1},{4,2},{5,3},{6,4},{7,5},{8,6},{9,7},{10,... | collective-permute-start | bytes 393224 | tf_op jit(solution)/shard_map/ppermute | solution.py:189
  75.4 2.8 %collective-permute-start.5 = (bf16[64,1024]{1,0:T(8,128)(2,1)S(1)}, bf16[64,1024]{1,0:T(8,128)(2,1)S(1)}, u32[]{:S(2)}, u32[]{:S(2)}) collective-permute-start(bf16[64,1024]{1,0:T(8,128)(2,1)S(1)} %get-tuple-element.22), channel_id=1, source_target_pairs={{0,12},{1,13},{2,14},{3,15},{4,0},{5,1},{6,2},{7,3},{8,4},{9,5},{1... | collective-permute-start | bytes 393224 | tf_op jit(solution)/shard_map/ppermute | solution.py:189
  78.3 4.4 %collective-permute-start.4 = (bf16[64,1024]{1,0:T(8,128)(2,1)S(1)}, bf16[64,1024]{1,0:T(8,128)(2,1)S(1)}, u32[]{:S(2)}, u32[]{:S(2)}) collective-permute-start(bf16[64,1024]{1,0:T(8,128)(2,1)S(1)} %get-tuple-element.22), channel_id=1, source_target_pairs={{0,10},{1,11},{2,12},{3,13},{4,14},{5,15},{6,0},{7,1},{8,2},{9,3},... | collective-permute-start | bytes 393224 | tf_op jit(solution)/shard_map/ppermute | solution.py:189
  82.6 0.0 collective-permute-done
  82.7 2.7 %collective-permute-start.2 = (bf16[64,1024]{1,0:T(8,128)(2,1)S(1)}, bf16[64,1024]{1,0:T(8,128)(2,1)S(1)}, u32[]{:S(2)}, u32[]{:S(2)}) collective-permute-start(bf16[64,1024]{1,0:T(8,128)(2,1)S(1)} %get-tuple-element.22), channel_id=1, source_target_pairs={{0,6},{1,7},{2,8},{3,9},{4,10},{5,11},{6,12},{7,13},{8,14},{9,15},... | collective-permute-start | bytes 393224 | tf_op jit(solution)/shard_map/ppermute | solution.py:189
  85.4 0.0 collective-permute-done.1
  85.4 5.1 %collective-permute-start.3 = (bf16[64,1024]{1,0:T(8,128)(2,1)S(1)}, bf16[64,1024]{1,0:T(8,128)(2,1)S(1)}, u32[]{:S(2)}, u32[]{:S(2)}) collective-permute-start(bf16[64,1024]{1,0:T(8,128)(2,1)S(1)} %get-tuple-element.22), channel_id=1, source_target_pairs={{0,8},{1,9},{2,10},{3,11},{4,12},{5,13},{6,14},{7,15},{8,0},{9,1},... | collective-permute-start | bytes 393224 | tf_op jit(solution)/shard_map/ppermute | solution.py:189
  90.5 3.2 %collective-permute-done.2 = bf16[64,1024]{1,0:T(8,128)(2,1)S(1)} collective-permute-done((bf16[64,1024]{1,0:T(8,128)(2,1)S(1)}, bf16[64,1024]{1,0:T(8,128)(2,1)S(1)}, u32[]{:S(2)}, u32[]{:S(2)}) %collective-permute-start.2) | collective-permute-done | bytes 131104 | tf_op jit(solution)/shard_map/ppermute | solution.py:189
  93.7 2.1 %collective-permute-done.3 = bf16[64,1024]{1,0:T(8,128)(2,1)S(1)} collective-permute-done((bf16[64,1024]{1,0:T(8,128)(2,1)S(1)}, bf16[64,1024]{1,0:T(8,128)(2,1)S(1)}, u32[]{:S(2)}, u32[]{:S(2)}) %collective-permute-start.3) | collective-permute-done | bytes 131104 | tf_op jit(solution)/shard_map/ppermute | solution.py:189
  95.9 0.0 collective-permute-done.4
  95.9 0.0 collective-permute-done.5
  95.9 0.0 collective-permute-done.6
  96.0 0.0 copy-start
  96.0 12.0 %collective-permute-start.7 = (bf16[1024,1024]{1,0:T(8,128)(2,1)S(1)}, bf16[1024,1024]{1,0:T(8,128)(2,1)}, u32[]{:S(2)}, u32[]{:S(2)}) collective-permute-start(bf16[1024,1024]{1,0:T(8,128)(2,1)S(1)} %constant_dynamic-update-slice_fusion.ka_ref.va_ref), channel_id=1, source_target_pairs={{0,1},{1,0},{2,3},{3,2},{4,5},{5,4},{6,7},{7,6},{8,9},{9,8},{10,11... | collective-permute-start | bytes 6291464 | tf_op jit(solution)/shard_map/ppermute | solution.py:191
  108.7 0.7 copy.12.qpos_ref
  109.4 2.5 %collective-permute-done.7.kb_ref.vb_ref = bf16[1024,1024]{1,0:T(8,128)(2,1)} collective-permute-done((bf16[1024,1024]{1,0:T(8,128)(2,1)S(1)}, bf16[1024,1024]{1,0:T(8,128)(2,1)}, u32[]{:S(2)}, u32[]{:S(2)}) %collective-permute-start.7) | collective-permute-done | bytes 2097184 | tf_op jit(solution)/shard_map/ppermute | solution.py:191
  111.9 0.0 copy-done
  111.9 11.9 %shard_map.83 = f32[128,2048]{1,0:T(8,128)} custom-call(f32[16]{0:T(128)} %multiply_bitcast_fusion.mult_ref, s32[1]{0:T(128)S(6)} %copy.22.tiers_ref, s32[128,1]{1,0:T(8,128)} %copy.12.qpos_ref, s32[1,1024]{1,0:T(1,128)} %bitcast.30, s32[1,1024]{1,0:T(1,128)} %bitcast.29, bf16[128,2048]{1,0:T(8,128)(2,1)} %get-tuple-element.20.q_ref, ...), custom_call_target="tpu_custom_call" | custom-call | flops 2147483648 | bytes 6815744 | tf_op jit(solution)/shard_map/pallas_call | solution.py:107
  123.8 2.3 %collective-permute-start.8 = (f32[1,128,2048]{2,1,0:T(8,128)}, f32[1,128,2048]{2,1,0:T(8,128)S(1)}, u32[]{:S(2)}, u32[]{:S(2)}) collective-permute-start(f32[1,128,2048]{2,1,0:T(8,128)} %bitcast.28), channel_id=1, source_target_pairs={{752,0},{0,16},{16,32},{32,48},{48,64},{64,80},{80,96},{96,112},{1... | collective-permute-start | bytes 3145736 | tf_op jit(solution)/shard_map/ppermute | solution.py:18
  126.1 28.8 %collective-permute-done.8 = f32[1,128,2048]{2,1,0:T(8,128)S(1)} collective-permute-done((f32[1,128,2048]{2,1,0:T(8,128)}, f32[1,128,2048]{2,1,0:T(8,128)S(1)}, u32[]{:S(2)}, u32[]{:S(2)}) %collective-permute-start.8) | collective-permute-done | bytes 1048608 | tf_op jit(solution)/shard_map/ppermute | solution.py:18
  154.9 1.0 copy.23
  (13 shorter events, 0.1 us)
Async XLA Ops:
  6.5 57.7 %all-gather.2.cloned.1.call-start = ((), (), s32[]{:S(2)}) async-start(), calls=%async_computation | async-start | bytes 1179648 | tf_op jit(solution)/shard_map/all_gather | solution.py:183
  15.8 49.7 %copy-start.1 = (bf16[128,1024]{1,0:T(8,128)(2,1)S(1)}, bf16[128,1024]{1,0:T(8,128)(2,1)}, u32[]{:S(2)}) copy-start(bf16[128,1024]{1,0:T(8,128)(2,1)} %get-tuple-element.21) | copy-start | bytes 786436
  65.5 17.1 %collective-permute-start = (bf16[64,1024]{1,0:T(8,128)(2,1)S(1)}, bf16[64,1024]{1,0:T(8,128)(2,1)S(1)}, u32[]{:S(2)}, u32[]{:S(2)}) collective-permute-start(bf16[64,1024]{1,0:T(8,128)(2,1)S(1)} %get-tuple-element.22), channel_id=1, source_target_pairs={{0,2},{1,3},{2,4},{3,5},{4,6},{5,7},{6,8},{7,9},{8,10},{9,11},{10,... | collective-permute-start | bytes 393224 | tf_op jit(solution)/shard_map/ppermute | solution.py:189
  68.4 17.0 %collective-permute-start.1 = (bf16[64,1024]{1,0:T(8,128)(2,1)S(1)}, bf16[64,1024]{1,0:T(8,128)(2,1)S(1)}, u32[]{:S(2)}, u32[]{:S(2)}) collective-permute-start(bf16[64,1024]{1,0:T(8,128)(2,1)S(1)} %get-tuple-element.22), channel_id=1, source_target_pairs={{0,4},{1,5},{2,6},{3,7},{4,8},{5,9},{6,10},{7,11},{8,12},{9,13},{1... | collective-permute-start | bytes 393224 | tf_op jit(solution)/shard_map/ppermute | solution.py:189
  71.8 24.1 %collective-permute-start.6 = (bf16[64,1024]{1,0:T(8,128)(2,1)S(1)}, bf16[64,1024]{1,0:T(8,128)(2,1)S(1)}, u32[]{:S(2)}, u32[]{:S(2)}) collective-permute-start(bf16[64,1024]{1,0:T(8,128)(2,1)S(1)} %get-tuple-element.22), channel_id=1, source_target_pairs={{0,14},{1,15},{2,0},{3,1},{4,2},{5,3},{6,4},{7,5},{8,6},{9,7},{10,... | collective-permute-start | bytes 393224 | tf_op jit(solution)/shard_map/ppermute | solution.py:189
  75.4 20.5 %collective-permute-start.5 = (bf16[64,1024]{1,0:T(8,128)(2,1)S(1)}, bf16[64,1024]{1,0:T(8,128)(2,1)S(1)}, u32[]{:S(2)}, u32[]{:S(2)}) collective-permute-start(bf16[64,1024]{1,0:T(8,128)(2,1)S(1)} %get-tuple-element.22), channel_id=1, source_target_pairs={{0,12},{1,13},{2,14},{3,15},{4,0},{5,1},{6,2},{7,3},{8,4},{9,5},{1... | collective-permute-start | bytes 393224 | tf_op jit(solution)/shard_map/ppermute | solution.py:189
  78.3 17.6 %collective-permute-start.4 = (bf16[64,1024]{1,0:T(8,128)(2,1)S(1)}, bf16[64,1024]{1,0:T(8,128)(2,1)S(1)}, u32[]{:S(2)}, u32[]{:S(2)}) collective-permute-start(bf16[64,1024]{1,0:T(8,128)(2,1)S(1)} %get-tuple-element.22), channel_id=1, source_target_pairs={{0,10},{1,11},{2,12},{3,13},{4,14},{5,15},{6,0},{7,1},{8,2},{9,3},... | collective-permute-start | bytes 393224 | tf_op jit(solution)/shard_map/ppermute | solution.py:189
  82.7 11.1 %collective-permute-start.2 = (bf16[64,1024]{1,0:T(8,128)(2,1)S(1)}, bf16[64,1024]{1,0:T(8,128)(2,1)S(1)}, u32[]{:S(2)}, u32[]{:S(2)}) collective-permute-start(bf16[64,1024]{1,0:T(8,128)(2,1)S(1)} %get-tuple-element.22), channel_id=1, source_target_pairs={{0,6},{1,7},{2,8},{3,9},{4,10},{5,11},{6,12},{7,13},{8,14},{9,15},... | collective-permute-start | bytes 393224 | tf_op jit(solution)/shard_map/ppermute | solution.py:189
  85.4 10.5 %collective-permute-start.3 = (bf16[64,1024]{1,0:T(8,128)(2,1)S(1)}, bf16[64,1024]{1,0:T(8,128)(2,1)S(1)}, u32[]{:S(2)}, u32[]{:S(2)}) collective-permute-start(bf16[64,1024]{1,0:T(8,128)(2,1)S(1)} %get-tuple-element.22), channel_id=1, source_target_pairs={{0,8},{1,9},{2,10},{3,11},{4,12},{5,13},{6,14},{7,15},{8,0},{9,1},... | collective-permute-start | bytes 393224 | tf_op jit(solution)/shard_map/ppermute | solution.py:189
  96.0 15.9 %copy-start = (bf16[1024,1024]{1,0:T(8,128)(2,1)}, bf16[1024,1024]{1,0:T(8,128)(2,1)S(1)}, u32[]{:S(2)}) copy-start(bf16[1024,1024]{1,0:T(8,128)(2,1)S(1)} %constant_dynamic-update-slice_fusion.ka_ref.va_ref) | copy-start | bytes 6291460
  96.0 15.9 %collective-permute-start.7 = (bf16[1024,1024]{1,0:T(8,128)(2,1)S(1)}, bf16[1024,1024]{1,0:T(8,128)(2,1)}, u32[]{:S(2)}, u32[]{:S(2)}) collective-permute-start(bf16[1024,1024]{1,0:T(8,128)(2,1)S(1)} %constant_dynamic-update-slice_fusion.ka_ref.va_ref), channel_id=1, source_target_pairs={{0,1},{1,0},{2,3},{3,2},{4,5},{5,4},{6,7},{7,6},{8,9},{9,8},{10,11... | collective-permute-start | bytes 6291464 | tf_op jit(solution)/shard_map/ppermute | solution.py:191
  123.8 31.1 %collective-permute-start.8 = (f32[1,128,2048]{2,1,0:T(8,128)}, f32[1,128,2048]{2,1,0:T(8,128)S(1)}, u32[]{:S(2)}, u32[]{:S(2)}) collective-permute-start(f32[1,128,2048]{2,1,0:T(8,128)} %bitcast.28), channel_id=1, source_target_pairs={{752,0},{0,16},{16,32},{32,48},{48,64},{64,80},{80,96},{96,112},{1... | collective-permute-start | bytes 3145736 | tf_op jit(solution)/shard_map/ppermute | solution.py:18
Sparse Core Ops, SparseCore 0:
  17.6 46.5 all-gather.1

commit v7 on v4

--- a/solution.py
+++ b/solution.py
@@ -24,7 +24,7 @@
 
 def attention_kernel(
     mult_ref, tiers_ref, qpos_ref, kpos_a_ref, kpos_b_ref, q_ref,
-    ka_ref, va_ref, kb_ref, vb_ref, x_ref, w_ref, out_ref,
+    ka_ref, va_ref, kb_ref, vb_ref, w_ref, out_ref,
 ):
     c = pl.program_id(0)
     group = q_ref.shape[1] // ATTN_UNIT_WIDTH
@@ -53,8 +53,7 @@
             p_a.astype(jnp.bfloat16), va, preferred_element_type=jnp.float32
         ) + jnp.dot(p_b.astype(jnp.bfloat16), vb, preferred_element_type=jnp.float32)
         mixed = mixed / total
-        x = x_ref[:, cols]
-        out_ref[:, cols] = jnp.where(gate, x + w_ref[:, cols] * mixed, x)
+        out_ref[:, cols] = jnp.where(gate, w_ref[:, cols] * mixed, 0.0).astype(out_ref.dtype)
 
 
 def prologue_kernel(x_ref, gain_ref, wk_ref, wv_ref, kv_ref, q_ref):
@@ -93,8 +92,8 @@
     )(x, gain, wk, wv)
 
 
-def attend_and_update(mult, tiers, qpos, kpos_a, kpos_b, queries, block_a, block_b, x, w_out):
-    rows, width = x.shape
+def attend_and_update(mult, tiers, qpos, kpos_a, kpos_b, queries, block_a, block_b, w_out):
+    rows, width = queries.shape
     kv_rows = block_a.shape[0]
     kv_heads = KEY_VALUE_HEADS
     head_cols = width // kv_heads
@@ -118,7 +117,6 @@
             values_at(kv_block),
             cols(kv_block),
             values_at(kv_block),
-            cols((rows, head_cols)),
             cols((1, head_cols)),
         ],
         out_specs=cols((rows, head_cols)),
@@ -128,7 +126,7 @@
             transcendentals=rows * 2 * kv_rows * H,
             bytes_accessed=4 * kv_rows * 1024 + rows * width * 10,
         ),
-    )(mult, tiers, qpos, kpos_a, kpos_b, queries, block_a, block_a, block_b, block_b, x, w_out)
+    )(mult, tiers, qpos, kpos_a, kpos_b, queries, block_a, block_a, block_b, block_b, w_out)
 
 
 def local(
@@ -148,6 +146,7 @@
     core = me % 2
     half_rows = tok_rows // 2
     residual = residual_flow[0]
+    residual_next = passed_along(residual_flow, "section", 1)
 
     all_pos = (
         jnp.repeat(resident_tile_order.astype(jnp.int32), half_rows) * half_rows
@@ -172,9 +171,10 @@
     same_core = [list(range(c, n_ctx, 2)) for c in range(2)]
     partner_route = [(i, i ^ 1) for i in range(n_ctx)]
     mine = lax.all_gather(own_block, "ctx", axis=0, tiled=True, axis_index_groups=same_core)
+    mine, residual_next = lax.optimization_barrier((mine, residual_next))
     theirs = lax.ppermute(mine, "ctx", partner_route)
 
-    residual = attend_and_update(
+    update = attend_and_update(
         mult,
         tiers_each_segment,
         query_pos,
@@ -183,10 +183,10 @@
         queries,
         mine,
         theirs,
-        residual,
         attention_result_weight[0],
     )
-    return passed_along(residual[None], "section", 1)
+    update = update.astype(jnp.float16)
+    return residual_next + passed_along(update[None], "section", 1).astype(jnp.float32)
 
 
 def solution(mesh):

time: 127 us -> 118 us (0.929)
  waiting for transfers between devices: 81.7 us -> 66.6 us
  starting transfers between devices: 9.28 us -> 13.3 us
  other arithmetic: 1.93 us -> 4.28 us
    all_gather x1, waiting for transfers between devices: 50.4 us -> 10.1 us  [local(): lax.all_gather(own_block, 'ctx', axis=0, tiled=True, axis_index_groups=sa...]
    ppermute x1 -> x2, waiting for transfers between devices: 28.8 us -> 53.8 us  [passed_along(): return lax.ppermute(block, axis, route)]
    ppermute x1 -> x2, starting transfers between devices: 3.08 us -> 6.88 us  [passed_along(): return lax.ppermute(block, axis, route)]
    broadcast_in_dim x0 -> x1, other arithmetic: none -> 1.28 us  [local(): update[None]]
  transfers between devices with their start and end apart: 3 -> 4, of which waited for: 3 -> 4; matrix products, arithmetic and copies ran while one was open for 1% -> 1% of each run, Pallas kernels for 0% -> 0%
where the time goes in v7:
time: 118 us; the launch traced here: 117 us
  waiting for transfers between devices  66.6 us (56%)
  Pallas kernels  15.9 us (13%)
  between operations  14.1 us (12%)
  starting transfers between devices  13.3 us (11%)
  other arithmetic  4.28 us (4%)
  local copies, waits for them, and re-layouts  3.14 us (3%)
    ppermute x2, waiting for transfers between devices, passed_along(): return lax.ppermute(block, axis, route)  53.8 us
    pallas_call x1, Pallas kernels, attend_and_update(): pl.pallas_call(attention_kernel, grid=(kv_heads,), in_specs=[smem, smem,...  11.7 us
    all_gather x1, waiting for transfers between devices, local(): lax.all_gather(own_block, 'ctx', axis=0, tiled=True, axis_index_groups=sa...  10.1 us
    ppermute x2, starting transfers between devices, passed_along(): return lax.ppermute(block, axis, route)  6.88 us
    ppermute x1, starting transfers between devices, local(): theirs = lax.ppermute(mine, 'ctx', partner_route)  6.38 us
    pallas_call x1, Pallas kernels, prologue(): pl.pallas_call(prologue_kernel, out_shape=(jax.ShapeDtypeStruct((rows, 2...  4.21 us
    ppermute x1, waiting for transfers between devices, local(): theirs = lax.ppermute(mine, 'ctx', partner_route)  2.6 us
  transfers between devices with their start and end apart: 4, of which 4 were waited for; matrix products, arithmetic and copies ran while one was open for 1% of the time, Pallas kernels for 0%

profile of v7, /device:TPU:1, one launch (start us, length us, event | category | flops | bytes accessed | tf_op | source)
XLA Modules:
  0.0 117.3 jit_solution(18024777036387177938)
XLA Ops:
  6.5 0.0 all-gather.2.cloned.1.call-start
  6.5 0.7 broadcast_multiply_fusion
  7.2 0.1 mul.22
  7.3 0.1 iota_add_fusion
  7.4 1.2 %multiply_bitcast_fusion.mult_ref = f32[16]{0:T(128)} fusion(f32[1,1,16]{2,1,0:T(1,128)} %param.14), kind=kLoop, calls=%fused_computation.4 | loop fusion | flops 16 | bytes 128 | tf_op jit(solution)/shard_map/div | solution.py:166
  8.5 0.1 tile.15
  8.6 0.1 broadcast_in_dim.9
  8.7 0.1 mul.23
  8.8 0.1 add.28
  8.9 0.1 dynamic-slice_bitcast_fusion
  9.0 0.6 constant_dynamic-slice_fusion
  9.6 0.0 copy-start.1
  9.6 4.2 %shard_map.82 = (bf16[128,1024]{1,0:T(8,128)(2,1)}, bf16[128,2048]{1,0:T(8,128)(2,1)}) custom-call(f32[128,2048]{1,0:T(8,128)} %bitcast.17, f32[1,2048]{1,0:T(1,128)} %bitcast.20, bf16[2048,512]{1,0:T(8,128)(2,1)} %bitcast.15, bf16[2048,512]{1,0:T(8,128)(2,1)} %bitcast.16), custom_call_target="tpu_custom_call" | custom-call | flops 536870912 | bytes 6029312 | tf_op jit(solution)/shard_map/pallas_call | solution.py:81
  13.8 0.0 all-gather.2.cloned.1.call-update
  13.8 0.0 copy-done.1
  13.8 4.0 %collective-permute-start = (f32[1,128,2048]{2,1,0:T(8,128)S(1)}, f32[1,128,2048]{2,1,0:T(8,128)S(1)}, u32[]{:S(2)}, u32[]{:S(2)}) collective-permute-start(f32[1,128,2048]{2,1,0:T(8,128)S(1)} %copy-done.1), channel_id=1, source_target_pairs={{752,0},{0,16},{16,32},{32,48},{48,64},{64,80},{80,96},{96,112},{1... | collective-permute-start | bytes 3145736 | tf_op jit(solution)/shard_map/ppermute | solution.py:18
  17.8 36.2 %collective-permute-done = f32[1,128,2048]{2,1,0:T(8,128)S(1)} collective-permute-done((f32[1,128,2048]{2,1,0:T(8,128)S(1)}, f32[1,128,2048]{2,1,0:T(8,128)S(1)}, u32[]{:S(2)}, u32[]{:S(2)}) %collective-permute-start) | collective-permute-done | bytes 1048608 | tf_op jit(solution)/shard_map/ppermute | solution.py:18
  54.0 10.1 %all-gather.2.cloned.1.call-done.ka_ref.va_ref = bf16[1024,1024]{1,0:T(8,128)(2,1)} async-done(((bf16[128,1024]{1,0:T(8,128)(2,1)}), bf16[1024,1024]{1,0:T(8,128)(2,1)}) %all-gather.2.cloned.1.call-update) | async-done | bytes 2097168 | tf_op jit(solution)/shard_map/all_gather | solution.py:173
  64.1 6.4 %collective-permute-start.1 = (bf16[1024,1024]{1,0:T(8,128)(2,1)}, bf16[1024,1024]{1,0:T(8,128)(2,1)S(1)}, u32[]{:S(2)}, u32[]{:S(2)}) collective-permute-start(bf16[1024,1024]{1,0:T(8,128)(2,1)} %all-gather.2.cloned.1.call-done.ka_ref.va_ref), channel_id=1, source_target_pairs={{0,1},{1,0},{2,3},{3,2},{4,5},{5,4},{6,7},{7,6},{8,9},{9,8},{10,11... | collective-permute-start | bytes 6291464 | tf_op jit(solution)/shard_map/ppermute | solution.py:175
  71.2 0.7 copy.12.qpos_ref
  71.9 2.6 %collective-permute-done.1.kb_ref.vb_ref = bf16[1024,1024]{1,0:T(8,128)(2,1)S(1)} collective-permute-done((bf16[1024,1024]{1,0:T(8,128)(2,1)}, bf16[1024,1024]{1,0:T(8,128)(2,1)S(1)}, u32[]{:S(2)}, u32[]{:S(2)}) %collective-permute-start.1) | collective-permute-done | bytes 2097184 | tf_op jit(solution)/shard_map/ppermute | solution.py:175
  74.5 0.0 copy-start
  74.5 1.3 %copy-done = bf16[1024,1024]{1,0:T(8,128)(2,1)} copy-done((bf16[1024,1024]{1,0:T(8,128)(2,1)}, bf16[1024,1024]{1,0:T(8,128)(2,1)S(1)}, u32[]{:S(2)}) %copy-start) | copy-done | bytes 2097176
  75.8 11.7 %shard_map.83 = f32[128,2048]{1,0:T(8,128)} custom-call(f32[16]{0:T(128)} %multiply_bitcast_fusion.mult_ref, s32[1]{0:T(128)S(6)} %copy.13.tiers_ref, s32[128,1]{1,0:T(8,128)} %copy.12.qpos_ref, s32[1,1024]{1,0:T(1,128)} %bitcast.19, s32[1,1024]{1,0:T(1,128)} %bitcast.18, bf16[128,2048]{1,0:T(8,128)(2,1)} %get-tuple-element.23.q_ref, ...), custom_call_target="tpu_custom_call" | custom-call | flops 2147483648 | bytes 6815744 | tf_op jit(solution)/shard_map/pallas_call | solution.py:106
  87.5 1.3 %convert_bitcast_fusion = f16[1,128,2048]{2,1,0:T(8,128)(2,1)S(1)} fusion(f32[128,2048]{1,0:T(8,128)} %shard_map.83), kind=kLoop, calls=%fused_computation.1 | loop fusion | flops 262144 | bytes 1572864 | tf_op jit(solution)/shard_map/broadcast_in_dim | solution.py:189
  88.8 2.9 %collective-permute-start.2 = (f16[1,128,2048]{2,1,0:T(8,128)(2,1)S(1)}, f16[1,128,2048]{2,1,0:T(8,128)(2,1)S(1)}, u32[]{:S(2)}, u32[]{:S(2)}) collective-permute-start(f16[1,128,2048]{2,1,0:T(8,128)(2,1)S(1)} %convert_bitcast_fusion), channel_id=1, source_target_pairs={{752,0},{0,16},{16,32},{32,48},{48,64},{64,80},{80,96},{96,112},{1... | collective-permute-start | bytes 1572872 | tf_op jit(solution)/shard_map/ppermute | solution.py:18
  91.8 17.6 %collective-permute-done.2 = f16[1,128,2048]{2,1,0:T(8,128)(2,1)S(1)} collective-permute-done((f16[1,128,2048]{2,1,0:T(8,128)(2,1)S(1)}, f16[1,128,2048]{2,1,0:T(8,128)(2,1)S(1)}, u32[]{:S(2)}, u32[]{:S(2)}) %collective-permute-start.2) | collective-permute-done | bytes 524320 | tf_op jit(solution)/shard_map/ppermute | solution.py:18
  109.3 1.1 convert_add_fusion
  (3 shorter events, 0.0 us)
Async XLA Ops:
  6.5 57.6 %all-gather.2.cloned.1.call-start = ((), (), s32[]{:S(2)}) async-start(), calls=%async_computation | async-start | bytes 2359296 | tf_op jit(solution)/shard_map/all_gather | solution.py:173
  9.6 4.2 %copy-start.1 = (f32[1,128,2048]{2,1,0:T(8,128)S(1)}, f32[1,128,2048]{2,1,0:T(8,128)}, u32[]{:S(2)}) copy-start(f32[1,128,2048]{2,1,0:T(8,128)} %param.8) | copy-start | bytes 3145732
  13.8 40.2 %collective-permute-start = (f32[1,128,2048]{2,1,0:T(8,128)S(1)}, f32[1,128,2048]{2,1,0:T(8,128)S(1)}, u32[]{:S(2)}, u32[]{:S(2)}) collective-permute-start(f32[1,128,2048]{2,1,0:T(8,128)S(1)} %copy-done.1), channel_id=1, source_target_pairs={{752,0},{0,16},{16,32},{32,48},{48,64},{64,80},{80,96},{96,112},{1... | collective-permute-start | bytes 3145736 | tf_op jit(solution)/shard_map/ppermute | solution.py:18
  64.1 10.4 %collective-permute-start.1 = (bf16[1024,1024]{1,0:T(8,128)(2,1)}, bf16[1024,1024]{1,0:T(8,128)(2,1)S(1)}, u32[]{:S(2)}, u32[]{:S(2)}) collective-permute-start(bf16[1024,1024]{1,0:T(8,128)(2,1)} %all-gather.2.cloned.1.call-done.ka_ref.va_ref), channel_id=1, source_target_pairs={{0,1},{1,0},{2,3},{3,2},{4,5},{5,4},{6,7},{7,6},{8,9},{9,8},{10,11... | collective-permute-start | bytes 6291464 | tf_op jit(solution)/shard_map/ppermute | solution.py:175
  74.5 1.3 %copy-start = (bf16[1024,1024]{1,0:T(8,128)(2,1)}, bf16[1024,1024]{1,0:T(8,128)(2,1)S(1)}, u32[]{:S(2)}) copy-start(bf16[1024,1024]{1,0:T(8,128)(2,1)S(1)} %collective-permute-done.1.kb_ref.vb_ref) | copy-start | bytes 6291460
  88.8 20.5 %collective-permute-start.2 = (f16[1,128,2048]{2,1,0:T(8,128)(2,1)S(1)}, f16[1,128,2048]{2,1,0:T(8,128)(2,1)S(1)}, u32[]{:S(2)}, u32[]{:S(2)}) collective-permute-start(f16[1,128,2048]{2,1,0:T(8,128)(2,1)S(1)} %convert_bitcast_fusion), channel_id=1, source_target_pairs={{752,0},{0,16},{16,32},{32,48},{48,64},{64,80},{80,96},{96,112},{1... | collective-permute-start | bytes 1572872 | tf_op jit(solution)/shard_map/ppermute | solution.py:18
Sparse Core Ops, SparseCore 0:
  13.9 50.1 all-gather.1

commit v8 on v7

--- a/solution.py
+++ b/solution.py
@@ -23,14 +23,33 @@
 
 
 def attention_kernel(
-    mult_ref, tiers_ref, qpos_ref, kpos_a_ref, kpos_b_ref, q_ref,
+    warmth_ref, tiers_ref, order_ref, me_ref, q_ref,
     ka_ref, va_ref, kb_ref, vb_ref, w_ref, out_ref,
 ):
     c = pl.program_id(0)
     group = q_ref.shape[1] // ATTN_UNIT_WIDTH
-    qpos = qpos_ref[...]
-    allowed_a = kpos_a_ref[...] <= qpos
-    allowed_b = kpos_b_ref[...] <= qpos
+    rows = q_ref.shape[0]
+    half = rows // 2
+    kv_rows = ka_ref.shape[0]
+    me = me_ref[0]
+    core = me % 2
+    r = lax.broadcasted_iota(jnp.int32, (rows, 1), 0)
+    qpos = jnp.where(
+        r < half, order_ref[2 * me] * half + r, order_ref[2 * me + 1] * half + r - half
+    )
+    j = lax.broadcasted_iota(jnp.int32, (1, kv_rows), 1)
+    tile = j // half
+    offset = j % half
+
+    def key_positions(of_core):
+        pos = offset
+        for t in range(kv_rows // half):
+            block = 4 * (t // 2) + 2 * of_core + t % 2
+            pos = pos + jnp.where(tile == t, order_ref[block] * half, 0)
+        return pos
+
+    allowed_a = key_positions(core) <= qpos
+    allowed_b = key_positions(1 - core) <= qpos
     ka = ka_ref[...]
     kb = kb_ref[...]
     va = va_ref[...]
@@ -40,7 +59,7 @@
     for g in range(group):
         cols = slice(g * ATTN_UNIT_WIDTH, (g + 1) * ATTN_UNIT_WIDTH)
         qh = q_ref[:, cols]
-        mult = mult_ref[c * group + g]
+        mult = warmth_ref[c * group + g] * (1.0 / ATTN_UNIT_WIDTH)
         s_a = jnp.where(allowed_a, lax.dot_general(qh, ka, dims, preferred_element_type=jnp.float32), -1e30)
         s_b = jnp.where(allowed_b, lax.dot_general(qh, kb, dims, preferred_element_type=jnp.float32), -1e30)
         row_max = jnp.maximum(
@@ -92,7 +111,7 @@
     )(x, gain, wk, wv)
 
 
-def attend_and_update(mult, tiers, qpos, kpos_a, kpos_b, queries, block_a, block_b, w_out):
+def attend_and_update(warmth, tiers, order, me, queries, block_a, block_b, w_out):
     rows, width = queries.shape
     kv_rows = block_a.shape[0]
     kv_heads = KEY_VALUE_HEADS
@@ -109,9 +128,8 @@
         in_specs=[
             smem,
             smem,
-            whole((rows, 1)),
-            whole((1, kv_rows)),
-            whole((1, kv_rows)),
+            smem,
+            smem,
             cols((rows, head_cols)),
             cols(kv_block),
             values_at(kv_block),
@@ -126,7 +144,7 @@
             transcendentals=rows * 2 * kv_rows * H,
             bytes_accessed=4 * kv_rows * 1024 + rows * width * 10,
         ),
-    )(mult, tiers, qpos, kpos_a, kpos_b, queries, block_a, block_a, block_b, block_b, w_out)
+    )(warmth, tiers, order, me, queries, block_a, block_a, block_b, block_b, w_out)
 
 
 def local(
@@ -148,25 +166,13 @@
     residual = residual_flow[0]
     residual_next = passed_along(residual_flow, "section", 1)
 
-    all_pos = (
-        jnp.repeat(resident_tile_order.astype(jnp.int32), half_rows) * half_rows
-        + jnp.tile(jnp.arange(half_rows, dtype=jnp.int32), resident_tile_order.shape[0])
-    )
-    query_pos = lax.dynamic_slice(all_pos, (me * tok_rows,), (tok_rows,)).reshape(tok_rows, 1)
-    by_core = all_pos.reshape(n_chips, 2, tok_rows)
-    pos_mine = lax.dynamic_index_in_dim(by_core, core, axis=1, keepdims=False).reshape(1, -1)
-    pos_theirs = lax.dynamic_index_in_dim(by_core, 1 - core, axis=1, keepdims=False).reshape(1, -1)
-
     own_block, queries = prologue(
         residual,
         normalizer_weight_entries[0],
         lookup_map_weights[0, 0],
         content_map_weights[0, 0],
     )
-    mult = softmax_warmth[0, 0] / ATTN_UNIT_WIDTH
-    own_block, queries, query_pos, pos_mine, pos_theirs, mult = lax.optimization_barrier(
-        (own_block, queries, query_pos, pos_mine, pos_theirs, mult)
-    )
+    own_block, queries = lax.optimization_barrier((own_block, queries))
 
     same_core = [list(range(c, n_ctx, 2)) for c in range(2)]
     partner_route = [(i, i ^ 1) for i in range(n_ctx)]
@@ -175,11 +181,10 @@
     theirs = lax.ppermute(mine, "ctx", partner_route)
 
     update = attend_and_update(
-        mult,
+        softmax_warmth[0, 0],
         tiers_each_segment,
-        query_pos,
-        pos_mine,
-        pos_theirs,
+        resident_tile_order,
+        me.reshape(1).astype(jnp.int32),
         queries,
         mine,
         theirs,

time: 118 us -> 114 us (0.966)
  other arithmetic: 4.28 us -> 2.37 us
  local copies, waits for them, and re-layouts: 3.14 us -> 1.31 us
  transfers between devices with their start and end apart: 4 -> 4, of which waited for: 4 -> 4; matrix products, arithmetic and copies ran while one was open for 1% -> 0% of each run, Pallas kernels for 0% -> 0%
where the time goes in v8:
time: 114 us
  waiting for transfers between devices  67.3 us (59%)
  Pallas kernels  15.9 us (14%)
  between operations  14.1 us (12%)
  starting transfers between devices  13.2 us (12%)
  other arithmetic  2.37 us (2%)
  local copies, waits for them, and re-layouts  1.31 us (1%)
    ppermute x2, waiting for transfers between devices, passed_along(): return lax.ppermute(block, axis, route)  53.8 us
    pallas_call x1, Pallas kernels, attend_and_update(): pl.pallas_call(attention_kernel, grid=(kv_heads,), in_specs=[smem, smem,...  11.7 us
    all_gather x1, waiting for transfers between devices, local(): lax.all_gather(own_block, 'ctx', axis=0, tiled=True, axis_index_groups=sa...  10.1 us
    ppermute x2, starting transfers between devices, passed_along(): return lax.ppermute(block, axis, route)  6.86 us
    ppermute x1, starting transfers between devices, local(): theirs = lax.ppermute(mine, 'ctx', partner_route)  6.38 us
    pallas_call x1, Pallas kernels, prologue(): pl.pallas_call(prologue_kernel, out_shape=(jax.ShapeDtypeStruct((rows, 2...  4.22 us
    ppermute x1, waiting for transfers between devices, local(): theirs = lax.ppermute(mine, 'ctx', partner_route)  3.32 us
  transfers between devices with their start and end apart: 4, of which 4 were waited for; matrix products, arithmetic and copies ran while one was open for 0% of the time, Pallas kernels for 0%

profile of v8, /device:TPU:1, one launch (start us, length us, event | category | flops | bytes accessed | tf_op | source)
XLA Modules:
  0.0 114.2 jit_solution(1031852975592600015)
XLA Ops:
  6.5 0.0 all-gather.2.cloned.1.call-start
  6.5 0.0 copy-start.1
  6.5 4.2 %shard_map.82 = (bf16[128,1024]{1,0:T(8,128)(2,1)}, bf16[128,2048]{1,0:T(8,128)(2,1)}) custom-call(f32[128,2048]{1,0:T(8,128)} %bitcast.11, f32[1,2048]{1,0:T(1,128)} %bitcast.12, bf16[2048,512]{1,0:T(8,128)(2,1)} %bitcast.9, bf16[2048,512]{1,0:T(8,128)(2,1)} %bitcast.10), custom_call_target="tpu_custom_call" | custom-call | flops 536870912 | bytes 6029312 | tf_op jit(solution)/shard_map/pallas_call | solution.py:100
  10.8 0.0 all-gather.2.cloned.1.call-update
  10.8 0.0 copy-done.1
  10.8 4.0 %collective-permute-start = (f32[1,128,2048]{2,1,0:T(8,128)S(1)}, f32[1,128,2048]{2,1,0:T(8,128)S(1)}, u32[]{:S(2)}, u32[]{:S(2)}) collective-permute-start(f32[1,128,2048]{2,1,0:T(8,128)S(1)} %copy-done.1), channel_id=1, source_target_pairs={{752,0},{0,16},{16,32},{32,48},{48,64},{64,80},{80,96},{96,112},{1... | collective-permute-start | bytes 3145736 | tf_op jit(solution)/shard_map/ppermute | solution.py:18
  14.8 36.2 %collective-permute-done = f32[1,128,2048]{2,1,0:T(8,128)S(1)} collective-permute-done((f32[1,128,2048]{2,1,0:T(8,128)S(1)}, f32[1,128,2048]{2,1,0:T(8,128)S(1)}, u32[]{:S(2)}, u32[]{:S(2)}) %collective-permute-start) | collective-permute-done | bytes 1048608 | tf_op jit(solution)/shard_map/ppermute | solution.py:18
  51.0 10.1 %all-gather.2.cloned.1.call-done.ka_ref.va_ref = bf16[1024,1024]{1,0:T(8,128)(2,1)} async-done(((bf16[128,1024]{1,0:T(8,128)(2,1)}), bf16[1024,1024]{1,0:T(8,128)(2,1)}) %all-gather.2.cloned.1.call-update) | async-done | bytes 2097168 | tf_op jit(solution)/shard_map/all_gather | solution.py:179
  61.1 6.4 %collective-permute-start.1 = (bf16[1024,1024]{1,0:T(8,128)(2,1)}, bf16[1024,1024]{1,0:T(8,128)(2,1)S(1)}, u32[]{:S(2)}, u32[]{:S(2)}) collective-permute-start(bf16[1024,1024]{1,0:T(8,128)(2,1)} %all-gather.2.cloned.1.call-done.ka_ref.va_ref), channel_id=1, source_target_pairs={{0,1},{1,0},{2,3},{3,2},{4,5},{5,4},{6,7},{7,6},{8,9},{9,8},{10,11... | collective-permute-start | bytes 6291464 | tf_op jit(solution)/shard_map/ppermute | solution.py:181
  68.2 3.3 %collective-permute-done.1.kb_ref.vb_ref = bf16[1024,1024]{1,0:T(8,128)(2,1)S(1)} collective-permute-done((bf16[1024,1024]{1,0:T(8,128)(2,1)}, bf16[1024,1024]{1,0:T(8,128)(2,1)S(1)}, u32[]{:S(2)}, u32[]{:S(2)}) %collective-permute-start.1) | collective-permute-done | bytes 2097184 | tf_op jit(solution)/shard_map/ppermute | solution.py:181
  71.5 0.0 copy-start
  71.5 1.3 %copy-done = bf16[1024,1024]{1,0:T(8,128)(2,1)} copy-done((bf16[1024,1024]{1,0:T(8,128)(2,1)}, bf16[1024,1024]{1,0:T(8,128)(2,1)S(1)}, u32[]{:S(2)}) %copy-start) | copy-done | bytes 2097176
  72.8 11.7 %shard_map.83 = f32[128,2048]{1,0:T(8,128)} custom-call(f32[16]{0:T(128)} %bitcast.14, s32[1]{0:T(128)S(6)} %copy.9.tiers_ref, s32[32]{0:T(128)} %order_ref.1, s32[1]{0:T(128)} %bitcast.5.me_ref, bf16[128,2048]{1,0:T(8,128)(2,1)} %get-tuple-element.11.q_ref, bf16[1024,1024]{1,0:T(8,128)(2,1)} %all-gather.2.cloned.1.call-done.ka_ref.va_ref, ...), custom_call_target="tpu_custom_call" | custom-call | flops 2147483648 | bytes 6815744 | tf_op jit(solution)/shard_map/pallas_call | solution.py:125
  84.5 1.3 %convert_bitcast_fusion = f16[1,128,2048]{2,1,0:T(8,128)(2,1)S(1)} fusion(f32[128,2048]{1,0:T(8,128)} %shard_map.83), kind=kLoop, calls=%fused_computation.1 | loop fusion | flops 262144 | bytes 1572864 | tf_op jit(solution)/shard_map/broadcast_in_dim | solution.py:194
  85.8 2.9 %collective-permute-start.2 = (f16[1,128,2048]{2,1,0:T(8,128)(2,1)S(1)}, f16[1,128,2048]{2,1,0:T(8,128)(2,1)S(1)}, u32[]{:S(2)}, u32[]{:S(2)}) collective-permute-start(f16[1,128,2048]{2,1,0:T(8,128)(2,1)S(1)} %convert_bitcast_fusion), channel_id=1, source_target_pairs={{752,0},{0,16},{16,32},{32,48},{48,64},{64,80},{80,96},{96,112},{1... | collective-permute-start | bytes 1572872 | tf_op jit(solution)/shard_map/ppermute | solution.py:18
  88.7 17.6 %collective-permute-done.2 = f16[1,128,2048]{2,1,0:T(8,128)(2,1)S(1)} collective-permute-done((f16[1,128,2048]{2,1,0:T(8,128)(2,1)S(1)}, f16[1,128,2048]{2,1,0:T(8,128)(2,1)S(1)}, u32[]{:S(2)}, u32[]{:S(2)}) %collective-permute-start.2) | collective-permute-done | bytes 524320 | tf_op jit(solution)/shard_map/ppermute | solution.py:18
  106.3 1.1 convert_add_fusion
Async XLA Ops:
  6.5 54.6 %all-gather.2.cloned.1.call-start = ((), (), s32[]{:S(2)}) async-start(), calls=%async_computation | async-start | bytes 2359296 | tf_op jit(solution)/shard_map/all_gather | solution.py:179
  6.5 4.2 %copy-start.1 = (f32[1,128,2048]{2,1,0:T(8,128)S(1)}, f32[1,128,2048]{2,1,0:T(8,128)}, u32[]{:S(2)}) copy-start(f32[1,128,2048]{2,1,0:T(8,128)} %param.8) | copy-start | bytes 3145732
  10.8 40.2 %collective-permute-start = (f32[1,128,2048]{2,1,0:T(8,128)S(1)}, f32[1,128,2048]{2,1,0:T(8,128)S(1)}, u32[]{:S(2)}, u32[]{:S(2)}) collective-permute-start(f32[1,128,2048]{2,1,0:T(8,128)S(1)} %copy-done.1), channel_id=1, source_target_pairs={{752,0},{0,16},{16,32},{32,48},{48,64},{64,80},{80,96},{96,112},{1... | collective-permute-start | bytes 3145736 | tf_op jit(solution)/shard_map/ppermute | solution.py:18
  61.1 10.4 %collective-permute-start.1 = (bf16[1024,1024]{1,0:T(8,128)(2,1)}, bf16[1024,1024]{1,0:T(8,128)(2,1)S(1)}, u32[]{:S(2)}, u32[]{:S(2)}) collective-permute-start(bf16[1024,1024]{1,0:T(8,128)(2,1)} %all-gather.2.cloned.1.call-done.ka_ref.va_ref), channel_id=1, source_target_pairs={{0,1},{1,0},{2,3},{3,2},{4,5},{5,4},{6,7},{7,6},{8,9},{9,8},{10,11... | collective-permute-start | bytes 6291464 | tf_op jit(solution)/shard_map/ppermute | solution.py:181
  71.5 1.3 %copy-start = (bf16[1024,1024]{1,0:T(8,128)(2,1)}, bf16[1024,1024]{1,0:T(8,128)(2,1)S(1)}, u32[]{:S(2)}) copy-start(bf16[1024,1024]{1,0:T(8,128)(2,1)S(1)} %collective-permute-done.1.kb_ref.vb_ref) | copy-start | bytes 6291460
  85.8 20.5 %collective-permute-start.2 = (f16[1,128,2048]{2,1,0:T(8,128)(2,1)S(1)}, f16[1,128,2048]{2,1,0:T(8,128)(2,1)S(1)}, u32[]{:S(2)}, u32[]{:S(2)}) collective-permute-start(f16[1,128,2048]{2,1,0:T(8,128)(2,1)S(1)} %convert_bitcast_fusion), channel_id=1, source_target_pairs={{752,0},{0,16},{16,32},{32,48},{48,64},{64,80},{80,96},{96,112},{1... | collective-permute-start | bytes 1572872 | tf_op jit(solution)/shard_map/ppermute | solution.py:18
Sparse Core Ops, SparseCore 0:
  10.9 50.1 all-gather.1

commit v9 on v8

--- a/solution.py
+++ b/solution.py
@@ -75,11 +75,15 @@
         out_ref[:, cols] = jnp.where(gate, w_ref[:, cols] * mixed, 0.0).astype(out_ref.dtype)
 
 
-def prologue_kernel(x_ref, gain_ref, wk_ref, wv_ref, kv_ref, q_ref):
+def normed_rows(x_ref, gain_ref):
     x = x_ref[...]
-    normed = (
+    return (
         x * lax.rsqrt(jnp.mean(x * x, axis=1, keepdims=True) + 1e-05) * gain_ref[...]
     ).astype(jnp.bfloat16)
+
+
+def key_value_kernel(x_ref, gain_ref, wk_ref, wv_ref, kv_ref):
+    normed = normed_rows(x_ref, gain_ref)
     keys = jnp.dot(normed, wk_ref[...], preferred_element_type=jnp.float32)
     kv_cols = keys.shape[1]
     for c in range(kv_cols // ATTN_UNIT_WIDTH):
@@ -88,7 +92,10 @@
     kv_ref[:, kv_cols:] = jnp.dot(
         normed, wv_ref[...], preferred_element_type=jnp.float32
     ).astype(jnp.bfloat16)
-    wide = normed.astype(jnp.float32)
+
+
+def query_kernel(x_ref, gain_ref, q_ref):
+    wide = normed_rows(x_ref, gain_ref).astype(jnp.float32)
     for h in range(wide.shape[1] // ATTN_UNIT_WIDTH):
         cols = slice(h * ATTN_UNIT_WIDTH, (h + 1) * ATTN_UNIT_WIDTH)
         q_ref[:, cols] = head_norm(wide[:, cols]).astype(jnp.bfloat16)
@@ -97,18 +104,23 @@
 def prologue(x, gain, wk, wv):
     rows, width = x.shape
     kv_cols = wk.shape[1]
-    return pl.pallas_call(
-        prologue_kernel,
-        out_shape=(
-            jax.ShapeDtypeStruct((rows, 2 * kv_cols), jnp.bfloat16),
-            jax.ShapeDtypeStruct((rows, width), jnp.bfloat16),
-        ),
+    own_block = pl.pallas_call(
+        key_value_kernel,
+        out_shape=jax.ShapeDtypeStruct((rows, 2 * kv_cols), jnp.bfloat16),
         cost_estimate=pl.CostEstimate(
             flops=4 * rows * width * kv_cols,
-            transcendentals=rows * 24,
-            bytes_accessed=2 * width * kv_cols * 2 + rows * width * 6 + rows * kv_cols * 4,
+            transcendentals=rows * 8,
+            bytes_accessed=2 * width * kv_cols * 2 + rows * width * 4 + rows * kv_cols * 4,
         ),
     )(x, gain, wk, wv)
+    queries = pl.pallas_call(
+        query_kernel,
+        out_shape=jax.ShapeDtypeStruct((rows, width), jnp.bfloat16),
+        cost_estimate=pl.CostEstimate(
+            flops=8 * rows * width, transcendentals=rows * 20, bytes_accessed=rows * width * 6
+        ),
+    )(x, gain)
+    return own_block, queries
 
 
 def attend_and_update(warmth, tiers, order, me, queries, block_a, block_b, w_out):
@@ -172,12 +184,12 @@
         lookup_map_weights[0, 0],
         content_map_weights[0, 0],
     )
-    own_block, queries = lax.optimization_barrier((own_block, queries))
+    own_block = lax.optimization_barrier(own_block)
 
     same_core = [list(range(c, n_ctx, 2)) for c in range(2)]
     partner_route = [(i, i ^ 1) for i in range(n_ctx)]
     mine = lax.all_gather(own_block, "ctx", axis=0, tiled=True, axis_index_groups=same_core)
-    mine, residual_next = lax.optimization_barrier((mine, residual_next))
+    mine, residual_next, queries = lax.optimization_barrier((mine, residual_next, queries))
     theirs = lax.ppermute(mine, "ctx", partner_route)
 
     update = attend_and_update(

time: 114 us -> 114 us (level)
  waiting for transfers between devices: 67.3 us -> 64.8 us
  Pallas kernels: 15.9 us -> 18.4 us
    ppermute x2, waiting for transfers between devices: 53.8 us -> 51.3 us  [passed_along(): return lax.ppermute(block, axis, route)]
    pallas_call x1 -> x2, Pallas kernels: 4.22 us -> 6.7 us  [the longest x1 4.16 us: prologue(): pl.pallas_call(key_value_kernel, out_shape=jax.ShapeDtypeStruct((rows, 2...]
  transfers between devices with their start and end apart: 4 -> 4, of which waited for: 4 -> 4; matrix products, arithmetic and copies ran while one was open for 0% -> 0% of each run, Pallas kernels for 0% -> 2%
where the time goes in v9:
time: 114 us
  waiting for transfers between devices  64.8 us (57%)
  Pallas kernels  18.4 us (16%)
  between operations  14.1 us (12%)
  starting transfers between devices  13.2 us (12%)
  other arithmetic  2.37 us (2%)
  local copies, waits for them, and re-layouts  1.31 us (1%)
    ppermute x2, waiting for transfers between devices, passed_along(): return lax.ppermute(block, axis, route)  51.3 us
    pallas_call x1, Pallas kernels, attend_and_update(): pl.pallas_call(attention_kernel, grid=(kv_heads,), in_specs=[smem, smem,...  11.7 us
    all_gather x1, waiting for transfers between devices, local(): lax.all_gather(own_block, 'ctx', axis=0, tiled=True, axis_index_groups=sa...  10.2 us
    ppermute x2, starting transfers between devices, passed_along(): return lax.ppermute(block, axis, route)  6.86 us
    ppermute x1, starting transfers between devices, local(): theirs = lax.ppermute(mine, 'ctx', partner_route)  6.38 us
    pallas_call x1, Pallas kernels, prologue(): pl.pallas_call(key_value_kernel, out_shape=jax.ShapeDtypeStruct((rows, 2...  4.16 us
    ppermute x1, waiting for transfers between devices, local(): theirs = lax.ppermute(mine, 'ctx', partner_route)  3.32 us
    pallas_call x1, Pallas kernels, prologue(): pl.pallas_call(query_kernel, out_shape=jax.ShapeDtypeStruct((rows, width)...  2.53 us
  transfers between devices with their start and end apart: 4, of which 4 were waited for; matrix products, arithmetic and copies ran while one was open for 0% of the time, Pallas kernels for 2%

profile of v9, /device:TPU:1, one launch (start us, length us, event | category | flops | bytes accessed | tf_op | source)
XLA Modules:
  0.0 114.2 jit_solution(16542769611118254493)
XLA Ops:
  6.5 0.0 all-gather.2.cloned.1.call-start
  6.5 0.0 copy-start.1
  6.5 4.2 %shard_map.82 = bf16[128,1024]{1,0:T(8,128)(2,1)} custom-call(f32[128,2048]{1,0:T(8,128)} %bitcast.9, f32[1,2048]{1,0:T(1,128)} %bitcast.13, bf16[2048,512]{1,0:T(8,128)(2,1)} %bitcast.11, bf16[2048,512]{1,0:T(8,128)(2,1)} %bitcast.12), custom_call_target="tpu_custom_call" | custom-call | flops 536870912 | bytes 5505024 | tf_op jit(solution)/shard_map/pallas_call | solution.py:107
  10.7 0.0 all-gather.2.cloned.1.call-update
  10.7 0.0 copy-done.1
  10.7 4.0 %collective-permute-start = (f32[1,128,2048]{2,1,0:T(8,128)S(1)}, f32[1,128,2048]{2,1,0:T(8,128)S(1)}, u32[]{:S(2)}, u32[]{:S(2)}) collective-permute-start(f32[1,128,2048]{2,1,0:T(8,128)S(1)} %copy-done.1), channel_id=1, source_target_pairs={{752,0},{0,16},{16,32},{32,48},{48,64},{64,80},{80,96},{96,112},{1... | collective-permute-start | bytes 3145736 | tf_op jit(solution)/shard_map/ppermute | solution.py:18
  14.7 2.5 %shard_map.83.q_ref = bf16[128,2048]{1,0:T(8,128)(2,1)} custom-call(f32[128,2048]{1,0:T(8,128)} %bitcast.10, f32[1,2048]{1,0:T(1,128)} %bitcast.14), custom_call_target="tpu_custom_call" | custom-call | flops 2097152 | bytes 1572864 | tf_op jit(solution)/shard_map/pallas_call | solution.py:116
  17.2 33.7 %collective-permute-done = f32[1,128,2048]{2,1,0:T(8,128)S(1)} collective-permute-done((f32[1,128,2048]{2,1,0:T(8,128)S(1)}, f32[1,128,2048]{2,1,0:T(8,128)S(1)}, u32[]{:S(2)}, u32[]{:S(2)}) %collective-permute-start) | collective-permute-done | bytes 1048608 | tf_op jit(solution)/shard_map/ppermute | solution.py:18
  50.9 10.2 %all-gather.2.cloned.1.call-done.ka_ref.va_ref = bf16[1024,1024]{1,0:T(8,128)(2,1)} async-done(((bf16[128,1024]{1,0:T(8,128)(2,1)}), bf16[1024,1024]{1,0:T(8,128)(2,1)}) %all-gather.2.cloned.1.call-update) | async-done | bytes 2097168 | tf_op jit(solution)/shard_map/all_gather | solution.py:191
  61.1 6.4 %collective-permute-start.1 = (bf16[1024,1024]{1,0:T(8,128)(2,1)}, bf16[1024,1024]{1,0:T(8,128)(2,1)S(1)}, u32[]{:S(2)}, u32[]{:S(2)}) collective-permute-start(bf16[1024,1024]{1,0:T(8,128)(2,1)} %all-gather.2.cloned.1.call-done.ka_ref.va_ref), channel_id=1, source_target_pairs={{0,1},{1,0},{2,3},{3,2},{4,5},{5,4},{6,7},{7,6},{8,9},{9,8},{10,11... | collective-permute-start | bytes 6291464 | tf_op jit(solution)/shard_map/ppermute | solution.py:193
  68.1 3.3 %collective-permute-done.1.kb_ref.vb_ref = bf16[1024,1024]{1,0:T(8,128)(2,1)S(1)} collective-permute-done((bf16[1024,1024]{1,0:T(8,128)(2,1)}, bf16[1024,1024]{1,0:T(8,128)(2,1)S(1)}, u32[]{:S(2)}, u32[]{:S(2)}) %collective-permute-start.1) | collective-permute-done | bytes 2097184 | tf_op jit(solution)/shard_map/ppermute | solution.py:193
  71.4 0.0 copy-start
  71.5 1.3 %copy-done = bf16[1024,1024]{1,0:T(8,128)(2,1)} copy-done((bf16[1024,1024]{1,0:T(8,128)(2,1)}, bf16[1024,1024]{1,0:T(8,128)(2,1)S(1)}, u32[]{:S(2)}) %copy-start) | copy-done | bytes 2097176
  72.8 11.7 %shard_map.84 = f32[128,2048]{1,0:T(8,128)} custom-call(f32[16]{0:T(128)} %bitcast.16, s32[1]{0:T(128)S(6)} %copy.9.tiers_ref, s32[32]{0:T(128)} %order_ref.1, s32[1]{0:T(128)} %bitcast.5.me_ref, bf16[128,2048]{1,0:T(8,128)(2,1)} %shard_map.83.q_ref, bf16[1024,1024]{1,0:T(8,128)(2,1)} %all-gather.2.cloned.1.call-done.ka_ref.va_ref, ...), custom_call_target="tpu_custom_call" | custom-call | flops 2147483648 | bytes 6815744 | tf_op jit(solution)/shard_map/pallas_call | solution.py:137
  84.5 1.3 %convert_bitcast_fusion = f16[1,128,2048]{2,1,0:T(8,128)(2,1)S(1)} fusion(f32[128,2048]{1,0:T(8,128)} %shard_map.84), kind=kLoop, calls=%fused_computation.1 | loop fusion | flops 262144 | bytes 1572864 | tf_op jit(solution)/shard_map/broadcast_in_dim | solution.py:206
  85.8 2.9 %collective-permute-start.2 = (f16[1,128,2048]{2,1,0:T(8,128)(2,1)S(1)}, f16[1,128,2048]{2,1,0:T(8,128)(2,1)S(1)}, u32[]{:S(2)}, u32[]{:S(2)}) collective-permute-start(f16[1,128,2048]{2,1,0:T(8,128)(2,1)S(1)} %convert_bitcast_fusion), channel_id=1, source_target_pairs={{752,0},{0,16},{16,32},{32,48},{48,64},{64,80},{80,96},{96,112},{1... | collective-permute-start | bytes 1572872 | tf_op jit(solution)/shard_map/ppermute | solution.py:18
  88.7 17.6 %collective-permute-done.2 = f16[1,128,2048]{2,1,0:T(8,128)(2,1)S(1)} collective-permute-done((f16[1,128,2048]{2,1,0:T(8,128)(2,1)S(1)}, f16[1,128,2048]{2,1,0:T(8,128)(2,1)S(1)}, u32[]{:S(2)}, u32[]{:S(2)}) %collective-permute-start.2) | collective-permute-done | bytes 524320 | tf_op jit(solution)/shard_map/ppermute | solution.py:18
  106.3 1.1 convert_add_fusion
Async XLA Ops:
  6.5 54.5 %all-gather.2.cloned.1.call-start = ((), (), s32[]{:S(2)}) async-start(), calls=%async_computation | async-start | bytes 2359296 | tf_op jit(solution)/shard_map/all_gather | solution.py:191
  6.5 4.2 %copy-start.1 = (f32[1,128,2048]{2,1,0:T(8,128)S(1)}, f32[1,128,2048]{2,1,0:T(8,128)}, u32[]{:S(2)}) copy-start(f32[1,128,2048]{2,1,0:T(8,128)} %param.8) | copy-start | bytes 3145732
  10.7 40.2 %collective-permute-start = (f32[1,128,2048]{2,1,0:T(8,128)S(1)}, f32[1,128,2048]{2,1,0:T(8,128)S(1)}, u32[]{:S(2)}, u32[]{:S(2)}) collective-permute-start(f32[1,128,2048]{2,1,0:T(8,128)S(1)} %copy-done.1), channel_id=1, source_target_pairs={{752,0},{0,16},{16,32},{32,48},{48,64},{64,80},{80,96},{96,112},{1... | collective-permute-start | bytes 3145736 | tf_op jit(solution)/shard_map/ppermute | solution.py:18
  61.1 10.4 %collective-permute-start.1 = (bf16[1024,1024]{1,0:T(8,128)(2,1)}, bf16[1024,1024]{1,0:T(8,128)(2,1)S(1)}, u32[]{:S(2)}, u32[]{:S(2)}) collective-permute-start(bf16[1024,1024]{1,0:T(8,128)(2,1)} %all-gather.2.cloned.1.call-done.ka_ref.va_ref), channel_id=1, source_target_pairs={{0,1},{1,0},{2,3},{3,2},{4,5},{5,4},{6,7},{7,6},{8,9},{9,8},{10,11... | collective-permute-start | bytes 6291464 | tf_op jit(solution)/shard_map/ppermute | solution.py:193
  71.4 1.3 %copy-start = (bf16[1024,1024]{1,0:T(8,128)(2,1)}, bf16[1024,1024]{1,0:T(8,128)(2,1)S(1)}, u32[]{:S(2)}) copy-start(bf16[1024,1024]{1,0:T(8,128)(2,1)S(1)} %collective-permute-done.1.kb_ref.vb_ref) | copy-start | bytes 6291460
  85.8 20.5 %collective-permute-start.2 = (f16[1,128,2048]{2,1,0:T(8,128)(2,1)S(1)}, f16[1,128,2048]{2,1,0:T(8,128)(2,1)S(1)}, u32[]{:S(2)}, u32[]{:S(2)}) collective-permute-start(f16[1,128,2048]{2,1,0:T(8,128)(2,1)S(1)} %convert_bitcast_fusion), channel_id=1, source_target_pairs={{752,0},{0,16},{16,32},{32,48},{48,64},{64,80},{80,96},{96,112},{1... | collective-permute-start | bytes 1572872 | tf_op jit(solution)/shard_map/ppermute | solution.py:18
Sparse Core Ops, SparseCore 0:
  10.8 50.1 all-gather.1

commit v10 on v9

--- a/solution.py
+++ b/solution.py
@@ -32,7 +32,6 @@
     half = rows // 2
     kv_rows = ka_ref.shape[0]
     me = me_ref[0]
-    core = me % 2
     r = lax.broadcasted_iota(jnp.int32, (rows, 1), 0)
     qpos = jnp.where(
         r < half, order_ref[2 * me] * half + r, order_ref[2 * me + 1] * half + r - half
@@ -41,15 +40,14 @@
     tile = j // half
     offset = j % half
 
-    def key_positions(of_core):
+    def key_positions(first_block):
         pos = offset
         for t in range(kv_rows // half):
-            block = 4 * (t // 2) + 2 * of_core + t % 2
-            pos = pos + jnp.where(tile == t, order_ref[block] * half, 0)
+            pos = pos + jnp.where(tile == t, order_ref[first_block + t] * half, 0)
         return pos
 
-    allowed_a = key_positions(core) <= qpos
-    allowed_b = key_positions(1 - core) <= qpos
+    allowed_a = key_positions(0) <= qpos
+    allowed_b = key_positions(kv_rows // half) <= qpos
     ka = ka_ref[...]
     kb = kb_ref[...]
     va = va_ref[...]
@@ -186,11 +184,9 @@
     )
     own_block = lax.optimization_barrier(own_block)
 
-    same_core = [list(range(c, n_ctx, 2)) for c in range(2)]
-    partner_route = [(i, i ^ 1) for i in range(n_ctx)]
-    mine = lax.all_gather(own_block, "ctx", axis=0, tiled=True, axis_index_groups=same_core)
-    mine, residual_next, queries = lax.optimization_barrier((mine, residual_next, queries))
-    theirs = lax.ppermute(mine, "ctx", partner_route)
+    gathered = lax.all_gather(own_block, "ctx", axis=0, tiled=True)
+    gathered, residual_next, queries = lax.optimization_barrier((gathered, residual_next, queries))
+    split = gathered.shape[0] // 2
 
     update = attend_and_update(
         softmax_warmth[0, 0],
@@ -198,8 +194,8 @@
         resident_tile_order,
         me.reshape(1).astype(jnp.int32),
         queries,
-        mine,
-        theirs,
+        gathered[:split],
+        gathered[split:],
         attention_result_weight[0],
     )
     update = update.astype(jnp.float16)

time: 114 us -> 113 us (level)
  starting transfers between devices: 13.2 us -> 6.87 us
  local copies, waits for them, and re-layouts: 1.31 us -> 4.64 us
  waiting for transfers between devices: 64.8 us -> 66.2 us
    ppermute x1 -> x0, starting transfers between devices: 6.38 us -> none  [local(): theirs = lax.ppermute(mine, 'ctx', partner_route)]
    all_gather x1, waiting for transfers between devices: 10.2 us -> 15.4 us  [local(): gathered = lax.all_gather(own_block, 'ctx', axis=0, tiled=True)]
    slice x0 -> x1, local copies, waits for them, and re-layouts: none -> 4.63 us  [local(): gathered[split:]]
    ppermute x1 -> x0, waiting for transfers between devices: 3.32 us -> none  [local(): theirs = lax.ppermute(mine, 'ctx', partner_route)]
    unnamed x4 -> x2, local copies, waits for them, and re-layouts: 1.31 us -> 0.01 us
  transfers between devices with their start and end apart: 4 -> 3, of which waited for: 4 -> 3; matrix products, arithmetic and copies ran while one was open for 0% -> 0% of each run, Pallas kernels for 2% -> 2%
where the time goes in v10:
time: 113 us
  waiting for transfers between devices  66.2 us (59%)
  Pallas kernels  18.4 us (16%)
  between operations  14.1 us (12%)
  starting transfers between devices  6.87 us (6%)
  local copies, waits for them, and re-layouts  4.64 us (4%)
  other arithmetic  2.37 us (2%)
    ppermute x2, waiting for transfers between devices, passed_along(): return lax.ppermute(block, axis, route)  50.7 us
    all_gather x1, waiting for transfers between devices, local(): gathered = lax.all_gather(own_block, 'ctx', axis=0, tiled=True)  15.4 us
    pallas_call x1, Pallas kernels, attend_and_update(): pl.pallas_call(attention_kernel, grid=(kv_heads,), in_specs=[smem, smem,...  11.7 us
    ppermute x2, starting transfers between devices, passed_along(): return lax.ppermute(block, axis, route)  6.87 us
    slice x1, local copies, waits for them, and re-layouts, local(): gathered[split:]  4.63 us
    pallas_call x1, Pallas kernels, prologue(): pl.pallas_call(key_value_kernel, out_shape=jax.ShapeDtypeStruct((rows, 2...  4.16 us
    pallas_call x1, Pallas kernels, prologue(): pl.pallas_call(query_kernel, out_shape=jax.ShapeDtypeStruct((rows, width)...  2.57 us
  transfers between devices with their start and end apart: 3, of which 3 were waited for; matrix products, arithmetic and copies ran while one was open for 0% of the time, Pallas kernels for 2%

profile of v10, /device:TPU:1, one launch (start us, length us, event | category | flops | bytes accessed | tf_op | source)
XLA Modules:
  0.0 112.5 jit_solution(8954938692167818450)
XLA Ops:
  6.5 0.0 all-gather.2.cloned.1.call-start
  6.5 0.0 copy-start
  6.5 4.2 %shard_map.82 = bf16[128,1024]{1,0:T(8,128)(2,1)} custom-call(f32[128,2048]{1,0:T(8,128)} %bitcast.9, f32[1,2048]{1,0:T(1,128)} %bitcast.13, bf16[2048,512]{1,0:T(8,128)(2,1)} %bitcast.11, bf16[2048,512]{1,0:T(8,128)(2,1)} %bitcast.12), custom_call_target="tpu_custom_call" | custom-call | flops 536870912 | bytes 5505024 | tf_op jit(solution)/shard_map/pallas_call | solution.py:105
  10.7 0.0 all-gather.2.cloned.1.call-update
  10.7 0.0 copy-done
  10.7 4.0 %collective-permute-start = (f32[1,128,2048]{2,1,0:T(8,128)S(1)}, f32[1,128,2048]{2,1,0:T(8,128)S(1)}, u32[]{:S(2)}, u32[]{:S(2)}) collective-permute-start(f32[1,128,2048]{2,1,0:T(8,128)S(1)} %copy-done), channel_id=1, source_target_pairs={{752,0},{0,16},{16,32},{32,48},{48,64},{64,80},{80,96},{96,112},{1... | collective-permute-start | bytes 3145736 | tf_op jit(solution)/shard_map/ppermute | solution.py:18
  15.4 2.6 %shard_map.83.q_ref = bf16[128,2048]{1,0:T(8,128)(2,1)} custom-call(f32[128,2048]{1,0:T(8,128)} %bitcast.10, f32[1,2048]{1,0:T(1,128)} %bitcast.14), custom_call_target="tpu_custom_call" | custom-call | flops 2097152 | bytes 1572864 | tf_op jit(solution)/shard_map/pallas_call | solution.py:114
  17.9 33.0 %collective-permute-done = f32[1,128,2048]{2,1,0:T(8,128)S(1)} collective-permute-done((f32[1,128,2048]{2,1,0:T(8,128)S(1)}, f32[1,128,2048]{2,1,0:T(8,128)S(1)}, u32[]{:S(2)}, u32[]{:S(2)}) %collective-permute-start) | collective-permute-done | bytes 1048608 | tf_op jit(solution)/shard_map/ppermute | solution.py:18
  50.9 15.4 %all-gather.2.cloned.1.call-done = bf16[2048,1024]{1,0:T(8,128)(2,1)} async-done(((bf16[128,1024]{1,0:T(8,128)(2,1)}), bf16[2048,1024]{1,0:T(8,128)(2,1)}) %all-gather.2.cloned.1.call-update) | async-done | bytes 4194320 | tf_op jit(solution)/shard_map/all_gather | solution.py:187
  66.3 4.6 %fusion = (bf16[1024,1024]{1,0:T(8,128)(2,1)}, bf16[1024,1024]{1,0:T(8,128)(2,1)}) fusion(bf16[2048,1024]{1,0:T(8,128)(2,1)} %all-gather.2.cloned.1.call-done), kind=kLoop, calls=%fused_computation.2 | loop fusion | bytes 8388608 | tf_op jit(solution)/shard_map/slice | solution.py:198
  71.0 11.7 %shard_map.84 = f32[128,2048]{1,0:T(8,128)} custom-call(f32[16]{0:T(128)} %bitcast.16, s32[1]{0:T(128)S(6)} %copy.9.tiers_ref, s32[32]{0:T(128)} %order_ref.1, s32[1]{0:T(128)} %bitcast.5.me_ref, bf16[128,2048]{1,0:T(8,128)(2,1)} %shard_map.83.q_ref, bf16[1024,1024]{1,0:T(8,128)(2,1)} %get-tuple-element.12.ka_ref.va_ref, ...), custom_call_target="tpu_custom_call" | custom-call | flops 2147483648 | bytes 6815744 | tf_op jit(solution)/shard_map/pallas_call | solution.py:135
  82.7 1.3 %convert_bitcast_fusion = f16[1,128,2048]{2,1,0:T(8,128)(2,1)S(1)} fusion(f32[128,2048]{1,0:T(8,128)} %shard_map.84), kind=kLoop, calls=%fused_computation.1 | loop fusion | flops 262144 | bytes 1572864 | tf_op jit(solution)/shard_map/broadcast_in_dim | solution.py:202
  84.0 2.9 %collective-permute-start.1 = (f16[1,128,2048]{2,1,0:T(8,128)(2,1)S(1)}, f16[1,128,2048]{2,1,0:T(8,128)(2,1)S(1)}, u32[]{:S(2)}, u32[]{:S(2)}) collective-permute-start(f16[1,128,2048]{2,1,0:T(8,128)(2,1)S(1)} %convert_bitcast_fusion), channel_id=1, source_target_pairs={{752,0},{0,16},{16,32},{32,48},{48,64},{64,80},{80,96},{96,112},{1... | collective-permute-start | bytes 1572872 | tf_op jit(solution)/shard_map/ppermute | solution.py:18
  86.9 17.7 %collective-permute-done.1 = f16[1,128,2048]{2,1,0:T(8,128)(2,1)S(1)} collective-permute-done((f16[1,128,2048]{2,1,0:T(8,128)(2,1)S(1)}, f16[1,128,2048]{2,1,0:T(8,128)(2,1)S(1)}, u32[]{:S(2)}, u32[]{:S(2)}) %collective-permute-start.1) | collective-permute-done | bytes 524320 | tf_op jit(solution)/shard_map/ppermute | solution.py:18
  104.6 1.1 convert_add_fusion
Async XLA Ops:
  6.5 59.8 %all-gather.2.cloned.1.call-start = ((), (), s32[]{:S(2)}) async-start(), calls=%async_computation | async-start | bytes 4456448 | tf_op jit(solution)/shard_map/all_gather | solution.py:187
  6.5 4.2 %copy-start = (f32[1,128,2048]{2,1,0:T(8,128)S(1)}, f32[1,128,2048]{2,1,0:T(8,128)}, u32[]{:S(2)}) copy-start(f32[1,128,2048]{2,1,0:T(8,128)} %param.8) | copy-start | bytes 3145732
  10.7 40.2 %collective-permute-start = (f32[1,128,2048]{2,1,0:T(8,128)S(1)}, f32[1,128,2048]{2,1,0:T(8,128)S(1)}, u32[]{:S(2)}, u32[]{:S(2)}) collective-permute-start(f32[1,128,2048]{2,1,0:T(8,128)S(1)} %copy-done), channel_id=1, source_target_pairs={{752,0},{0,16},{16,32},{32,48},{48,64},{64,80},{80,96},{96,112},{1... | collective-permute-start | bytes 3145736 | tf_op jit(solution)/shard_map/ppermute | solution.py:18
  84.0 20.6 %collective-permute-start.1 = (f16[1,128,2048]{2,1,0:T(8,128)(2,1)S(1)}, f16[1,128,2048]{2,1,0:T(8,128)(2,1)S(1)}, u32[]{:S(2)}, u32[]{:S(2)}) collective-permute-start(f16[1,128,2048]{2,1,0:T(8,128)(2,1)S(1)} %convert_bitcast_fusion), channel_id=1, source_target_pairs={{752,0},{0,16},{16,32},{32,48},{48,64},{64,80},{80,96},{96,112},{1... | collective-permute-start | bytes 1572872 | tf_op jit(solution)/shard_map/ppermute | solution.py:18
Sparse Core Ops, SparseCore 0:
  10.8 55.4 all-gather.1

commit v11 on v10

--- a/solution.py
+++ b/solution.py
@@ -121,15 +121,17 @@
     return own_block, queries
 
 
-def attend_and_update(warmth, tiers, order, me, queries, block_a, block_b, w_out):
+def attend_and_update(warmth, tiers, order, me, queries, gathered, w_out):
     rows, width = queries.shape
-    kv_rows = block_a.shape[0]
+    kv_rows = gathered.shape[0] // 2
     kv_heads = KEY_VALUE_HEADS
     head_cols = width // kv_heads
     smem = pl.BlockSpec(memory_space=pltpu.SMEM)
     whole = lambda shape: pl.BlockSpec(shape, lambda c: (0, 0))
     cols = lambda shape: pl.BlockSpec(shape, lambda c: (0, c))
     values_at = lambda shape: pl.BlockSpec(shape, lambda c: (0, c + kv_heads))
+    late_keys = lambda shape: pl.BlockSpec(shape, lambda c: (1, c))
+    late_values = lambda shape: pl.BlockSpec(shape, lambda c: (1, c + kv_heads))
     kv_block = (kv_rows, ATTN_UNIT_WIDTH)
     flops = 4 * rows * 2 * kv_rows * ATTN_UNIT_WIDTH * H
     return pl.pallas_call(
@@ -143,8 +145,8 @@
             cols((rows, head_cols)),
             cols(kv_block),
             values_at(kv_block),
-            cols(kv_block),
-            values_at(kv_block),
+            late_keys(kv_block),
+            late_values(kv_block),
             cols((1, head_cols)),
         ],
         out_specs=cols((rows, head_cols)),
@@ -154,7 +156,7 @@
             transcendentals=rows * 2 * kv_rows * H,
             bytes_accessed=4 * kv_rows * 1024 + rows * width * 10,
         ),
-    )(warmth, tiers, order, me, queries, block_a, block_a, block_b, block_b, w_out)
+    )(warmth, tiers, order, me, queries, gathered, gathered, gathered, gathered, w_out)
 
 
 def local(
@@ -186,7 +188,6 @@
 
     gathered = lax.all_gather(own_block, "ctx", axis=0, tiled=True)
     gathered, residual_next, queries = lax.optimization_barrier((gathered, residual_next, queries))
-    split = gathered.shape[0] // 2
 
     update = attend_and_update(
         softmax_warmth[0, 0],
@@ -194,8 +195,7 @@
         resident_tile_order,
         me.reshape(1).astype(jnp.int32),
         queries,
-        gathered[:split],
-        gathered[split:],
+        gathered,
         attention_result_weight[0],
     )
     update = update.astype(jnp.float16)

time: 113 us -> 108 us (0.956)
  local copies, waits for them, and re-layouts: 4.64 us -> 0.01 us
    slice x1 -> x0, local copies, waits for them, and re-layouts: 4.63 us -> none  [local(): gathered[split:]]
where the time goes in v11:
time: 108 us
  waiting for transfers between devices  66.2 us (61%)
  Pallas kernels  18.4 us (17%)
  between operations  14.1 us (13%)
  starting transfers between devices  6.87 us (6%)
  other arithmetic  2.37 us (2%)
    ppermute x2, waiting for transfers between devices, passed_along(): return lax.ppermute(block, axis, route)  50.7 us
    all_gather x1, waiting for transfers between devices, local(): gathered = lax.all_gather(own_block, 'ctx', axis=0, tiled=True)  15.4 us
    pallas_call x1, Pallas kernels, attend_and_update(): pl.pallas_call(attention_kernel, grid=(kv_heads,), in_specs=[smem, smem,...  11.7 us
    ppermute x2, starting transfers between devices, passed_along(): return lax.ppermute(block, axis, route)  6.87 us
    pallas_call x1, Pallas kernels, prologue(): pl.pallas_call(key_value_kernel, out_shape=jax.ShapeDtypeStruct((rows, 2...  4.16 us
    pallas_call x1, Pallas kernels, prologue(): pl.pallas_call(query_kernel, out_shape=jax.ShapeDtypeStruct((rows, width)...  2.54 us
  transfers between devices with their start and end apart: 3, of which 3 were waited for; matrix products, arithmetic and copies ran while one was open for 0% of the time, Pallas kernels for 2%

profile of v11, /device:TPU:1, one launch (start us, length us, event | category | flops | bytes accessed | tf_op | source)
XLA Modules:
  0.0 107.9 jit_solution(3293462518188347325)
XLA Ops:
  6.5 0.0 all-gather.2.cloned.1.call-start
  6.5 0.0 copy-start
  6.5 4.2 %shard_map.82 = bf16[128,1024]{1,0:T(8,128)(2,1)} custom-call(f32[128,2048]{1,0:T(8,128)} %bitcast.9, f32[1,2048]{1,0:T(1,128)} %bitcast.13, bf16[2048,512]{1,0:T(8,128)(2,1)} %bitcast.11, bf16[2048,512]{1,0:T(8,128)(2,1)} %bitcast.12), custom_call_target="tpu_custom_call" | custom-call | flops 536870912 | bytes 5505024 | tf_op jit(solution)/shard_map/pallas_call | solution.py:105
  10.7 0.0 all-gather.2.cloned.1.call-update
  10.7 0.0 copy-done
  10.7 4.0 %collective-permute-start = (f32[1,128,2048]{2,1,0:T(8,128)S(1)}, f32[1,128,2048]{2,1,0:T(8,128)S(1)}, u32[]{:S(2)}, u32[]{:S(2)}) collective-permute-start(f32[1,128,2048]{2,1,0:T(8,128)S(1)} %copy-done), channel_id=1, source_target_pairs={{752,0},{0,16},{16,32},{32,48},{48,64},{64,80},{80,96},{96,112},{1... | collective-permute-start | bytes 3145736 | tf_op jit(solution)/shard_map/ppermute | solution.py:18
  15.4 2.5 %shard_map.83.q_ref = bf16[128,2048]{1,0:T(8,128)(2,1)} custom-call(f32[128,2048]{1,0:T(8,128)} %bitcast.10, f32[1,2048]{1,0:T(1,128)} %bitcast.14), custom_call_target="tpu_custom_call" | custom-call | flops 2097152 | bytes 1572864 | tf_op jit(solution)/shard_map/pallas_call | solution.py:114
  17.9 33.0 %collective-permute-done = f32[1,128,2048]{2,1,0:T(8,128)S(1)} collective-permute-done((f32[1,128,2048]{2,1,0:T(8,128)S(1)}, f32[1,128,2048]{2,1,0:T(8,128)S(1)}, u32[]{:S(2)}, u32[]{:S(2)}) %collective-permute-start) | collective-permute-done | bytes 1048608 | tf_op jit(solution)/shard_map/ppermute | solution.py:18
  50.9 15.4 %all-gather.2.cloned.1.call-done.ka_ref.va_ref.kb_ref.vb_ref = bf16[2048,1024]{1,0:T(8,128)(2,1)} async-done(((bf16[128,1024]{1,0:T(8,128)(2,1)}), bf16[2048,1024]{1,0:T(8,128)(2,1)}) %all-gather.2.cloned.1.call-update) | async-done | bytes 4194320 | tf_op jit(solution)/shard_map/all_gather | solution.py:189
  66.3 11.7 %shard_map.84 = f32[128,2048]{1,0:T(8,128)} custom-call(f32[16]{0:T(128)} %bitcast.16, s32[1]{0:T(128)S(6)} %copy.9.tiers_ref, s32[32]{0:T(128)} %order_ref.1, s32[1]{0:T(128)} %bitcast.5.me_ref, bf16[128,2048]{1,0:T(8,128)(2,1)} %shard_map.83.q_ref, bf16[2048,1024]{1,0:T(8,128)(2,1)} %all-gather.2.cloned.1.call-done.ka_ref.va_ref.kb_ref.vb_ref, ...), custom_call_target="tpu_custom_call" | custom-call | flops 2147483648 | bytes 6815744 | tf_op jit(solution)/shard_map/pallas_call | solution.py:137
  78.1 1.3 %convert_bitcast_fusion = f16[1,128,2048]{2,1,0:T(8,128)(2,1)S(1)} fusion(f32[128,2048]{1,0:T(8,128)} %shard_map.84), kind=kLoop, calls=%fused_computation.1 | loop fusion | flops 262144 | bytes 1572864 | tf_op jit(solution)/shard_map/broadcast_in_dim | solution.py:202
  79.4 2.9 %collective-permute-start.1 = (f16[1,128,2048]{2,1,0:T(8,128)(2,1)S(1)}, f16[1,128,2048]{2,1,0:T(8,128)(2,1)S(1)}, u32[]{:S(2)}, u32[]{:S(2)}) collective-permute-start(f16[1,128,2048]{2,1,0:T(8,128)(2,1)S(1)} %convert_bitcast_fusion), channel_id=1, source_target_pairs={{752,0},{0,16},{16,32},{32,48},{48,64},{64,80},{80,96},{96,112},{1... | collective-permute-start | bytes 1572872 | tf_op jit(solution)/shard_map/ppermute | solution.py:18
  82.3 17.7 %collective-permute-done.1 = f16[1,128,2048]{2,1,0:T(8,128)(2,1)S(1)} collective-permute-done((f16[1,128,2048]{2,1,0:T(8,128)(2,1)S(1)}, f16[1,128,2048]{2,1,0:T(8,128)(2,1)S(1)}, u32[]{:S(2)}, u32[]{:S(2)}) %collective-permute-start.1) | collective-permute-done | bytes 524320 | tf_op jit(solution)/shard_map/ppermute | solution.py:18
  100.0 1.1 %convert_add_fusion = f32[1,128,2048]{2,1,0:T(8,128)} fusion(f32[1,128,2048]{2,1,0:T(8,128)S(1)} %collective-permute-done, f16[1,128,2048]{2,1,0:T(8,128)(2,1)S(1)} %collective-permute-done.1), kind=kLoop, calls=%fused_computation | loop fusion | flops 524288 | bytes 2621440 | tf_op jit(solution)/shard_map/add | solution.py:202
Async XLA Ops:
  6.5 59.8 %all-gather.2.cloned.1.call-start = ((), (), s32[]{:S(2)}) async-start(), calls=%async_computation | async-start | bytes 4456448 | tf_op jit(solution)/shard_map/all_gather | solution.py:189
  6.5 4.2 %copy-start = (f32[1,128,2048]{2,1,0:T(8,128)S(1)}, f32[1,128,2048]{2,1,0:T(8,128)}, u32[]{:S(2)}) copy-start(f32[1,128,2048]{2,1,0:T(8,128)} %param.8) | copy-start | bytes 3145732
  10.7 40.2 %collective-permute-start = (f32[1,128,2048]{2,1,0:T(8,128)S(1)}, f32[1,128,2048]{2,1,0:T(8,128)S(1)}, u32[]{:S(2)}, u32[]{:S(2)}) collective-permute-start(f32[1,128,2048]{2,1,0:T(8,128)S(1)} %copy-done), channel_id=1, source_target_pairs={{752,0},{0,16},{16,32},{32,48},{48,64},{64,80},{80,96},{96,112},{1... | collective-permute-start | bytes 3145736 | tf_op jit(solution)/shard_map/ppermute | solution.py:18
  79.4 20.6 %collective-permute-start.1 = (f16[1,128,2048]{2,1,0:T(8,128)(2,1)S(1)}, f16[1,128,2048]{2,1,0:T(8,128)(2,1)S(1)}, u32[]{:S(2)}, u32[]{:S(2)}) collective-permute-start(f16[1,128,2048]{2,1,0:T(8,128)(2,1)S(1)} %convert_bitcast_fusion), channel_id=1, source_target_pairs={{752,0},{0,16},{16,32},{32,48},{48,64},{64,80},{80,96},{96,112},{1... | collective-permute-start | bytes 1572872 | tf_op jit(solution)/shard_map/ppermute | solution.py:18
Sparse Core Ops, SparseCore 0:
  10.8 55.4 all-gather.1

commit v12 on v11

--- a/solution.py
+++ b/solution.py
@@ -80,16 +80,31 @@
     ).astype(jnp.bfloat16)
 
 
-def key_value_kernel(x_ref, gain_ref, wk_ref, wv_ref, kv_ref):
-    normed = normed_rows(x_ref, gain_ref)
-    keys = jnp.dot(normed, wk_ref[...], preferred_element_type=jnp.float32)
-    kv_cols = keys.shape[1]
-    for c in range(kv_cols // ATTN_UNIT_WIDTH):
-        cols = slice(c * ATTN_UNIT_WIDTH, (c + 1) * ATTN_UNIT_WIDTH)
-        kv_ref[:, cols] = head_norm(keys[:, cols]).astype(jnp.bfloat16)
-    kv_ref[:, kv_cols:] = jnp.dot(
-        normed, wv_ref[...], preferred_element_type=jnp.float32
-    ).astype(jnp.bfloat16)
+def key_value_kernel(x_ref, gain_ref, wk_ref, wv_ref, kv_ref, normed_ref, k_acc, v_acc):
+    i = pl.program_id(0)
+    chunks = normed_ref.shape[0]
+    chunk = normed_ref.shape[2]
+
+    @pl.when(i == 0)
+    def _():
+        normed = normed_rows(x_ref, gain_ref)
+        for part in range(chunks):
+            normed_ref[part] = normed[:, part * chunk:(part + 1) * chunk]
+        k_acc[...] = jnp.zeros_like(k_acc)
+        v_acc[...] = jnp.zeros_like(v_acc)
+
+    piece = normed_ref[i]
+    k_acc[...] += jnp.dot(piece, wk_ref[...], preferred_element_type=jnp.float32)
+    v_acc[...] += jnp.dot(piece, wv_ref[...], preferred_element_type=jnp.float32)
+
+    @pl.when(i == chunks - 1)
+    def _():
+        keys = k_acc[...]
+        kv_cols = keys.shape[1]
+        for c in range(kv_cols // ATTN_UNIT_WIDTH):
+            cols = slice(c * ATTN_UNIT_WIDTH, (c + 1) * ATTN_UNIT_WIDTH)
+            kv_ref[:, cols] = head_norm(keys[:, cols]).astype(jnp.bfloat16)
+        kv_ref[:, kv_cols:] = v_acc[...].astype(jnp.bfloat16)
 
 
 def query_kernel(x_ref, gain_ref, q_ref):
@@ -102,8 +117,23 @@
 def prologue(x, gain, wk, wv):
     rows, width = x.shape
     kv_cols = wk.shape[1]
+    chunks = 4
+    chunk = width // chunks
     own_block = pl.pallas_call(
         key_value_kernel,
+        grid=(chunks,),
+        in_specs=[
+            pl.BlockSpec((rows, width), lambda i: (0, 0)),
+            pl.BlockSpec((1, width), lambda i: (0, 0)),
+            pl.BlockSpec((chunk, kv_cols), lambda i: (i, 0)),
+            pl.BlockSpec((chunk, kv_cols), lambda i: (i, 0)),
+        ],
+        out_specs=pl.BlockSpec((rows, 2 * kv_cols), lambda i: (0, 0)),
+        scratch_shapes=[
+            pltpu.VMEM((chunks, rows, chunk), jnp.bfloat16),
+            pltpu.VMEM((rows, kv_cols), jnp.float32),
+            pltpu.VMEM((rows, kv_cols), jnp.float32),
+        ],
         out_shape=jax.ShapeDtypeStruct((rows, 2 * kv_cols), jnp.bfloat16),
         cost_estimate=pl.CostEstimate(
             flops=4 * rows * width * kv_cols,

time: 108 us -> 109 us (level)
  no operation moved by 1% of the time
where the time goes in v12:
time: 109 us
  waiting for transfers between devices  66.2 us (61%)
  Pallas kernels  19.2 us (18%)
  between operations  14.1 us (13%)
  starting transfers between devices  6.88 us (6%)
  other arithmetic  2.37 us (2%)
    ppermute x2, waiting for transfers between devices, passed_along(): return lax.ppermute(block, axis, route)  50.8 us
    all_gather x1, waiting for transfers between devices, local(): gathered = lax.all_gather(own_block, 'ctx', axis=0, tiled=True)  15.4 us
    pallas_call x1, Pallas kernels, attend_and_update(): pl.pallas_call(attention_kernel, grid=(kv_heads,), in_specs=[smem, smem,...  11.7 us
    ppermute x2, starting transfers between devices, passed_along(): return lax.ppermute(block, axis, route)  6.88 us
    pallas_call x1, Pallas kernels, prologue(): pl.pallas_call(key_value_kernel, grid=(chunks,), in_specs=[pl.BlockSpec((...  4.95 us
    pallas_call x1, Pallas kernels, prologue(): pl.pallas_call(query_kernel, out_shape=jax.ShapeDtypeStruct((rows, width)...  2.54 us
  transfers between devices with their start and end apart: 3, of which 3 were waited for; matrix products, arithmetic and copies ran while one was open for 0% of the time, Pallas kernels for 2%

profile of v12, /device:TPU:1, one launch (start us, length us, event | category | flops | bytes accessed | tf_op | source)
XLA Modules:
  0.0 108.7 jit_solution(7387843419872938108)
XLA Ops:
  6.5 0.0 all-gather.2.cloned.1.call-start
  6.5 0.0 copy-start
  6.5 4.9 %shard_map.82 = bf16[128,1024]{1,0:T(8,128)(2,1)} custom-call(f32[128,2048]{1,0:T(8,128)} %bitcast.9, f32[1,2048]{1,0:T(1,128)} %bitcast.13, bf16[2048,512]{1,0:T(8,128)(2,1)} %bitcast.11, bf16[2048,512]{1,0:T(8,128)(2,1)} %bitcast.12), custom_call_target="tpu_custom_call" | custom-call | flops 536870912 | bytes 5505024 | tf_op jit(solution)/shard_map/pallas_call | solution.py:122
  11.5 0.0 all-gather.2.cloned.1.call-update
  11.5 0.0 copy-done
  11.5 4.0 %collective-permute-start = (f32[1,128,2048]{2,1,0:T(8,128)S(1)}, f32[1,128,2048]{2,1,0:T(8,128)S(1)}, u32[]{:S(2)}, u32[]{:S(2)}) collective-permute-start(f32[1,128,2048]{2,1,0:T(8,128)S(1)} %copy-done), channel_id=1, source_target_pairs={{752,0},{0,16},{16,32},{32,48},{48,64},{64,80},{80,96},{96,112},{1... | collective-permute-start | bytes 3145736 | tf_op jit(solution)/shard_map/ppermute | solution.py:18
  16.1 2.5 %shard_map.83.q_ref = bf16[128,2048]{1,0:T(8,128)(2,1)} custom-call(f32[128,2048]{1,0:T(8,128)} %bitcast.10, f32[1,2048]{1,0:T(1,128)} %bitcast.14), custom_call_target="tpu_custom_call" | custom-call | flops 2097152 | bytes 1572864 | tf_op jit(solution)/shard_map/pallas_call | solution.py:144
  18.7 33.0 %collective-permute-done = f32[1,128,2048]{2,1,0:T(8,128)S(1)} collective-permute-done((f32[1,128,2048]{2,1,0:T(8,128)S(1)}, f32[1,128,2048]{2,1,0:T(8,128)S(1)}, u32[]{:S(2)}, u32[]{:S(2)}) %collective-permute-start) | collective-permute-done | bytes 1048608 | tf_op jit(solution)/shard_map/ppermute | solution.py:18
  51.7 15.4 %all-gather.2.cloned.1.call-done.ka_ref.va_ref.kb_ref.vb_ref = bf16[2048,1024]{1,0:T(8,128)(2,1)} async-done(((bf16[128,1024]{1,0:T(8,128)(2,1)}), bf16[2048,1024]{1,0:T(8,128)(2,1)}) %all-gather.2.cloned.1.call-update) | async-done | bytes 4194320 | tf_op jit(solution)/shard_map/all_gather | solution.py:219
  67.1 11.7 %shard_map.84 = f32[128,2048]{1,0:T(8,128)} custom-call(f32[16]{0:T(128)} %bitcast.16, s32[1]{0:T(128)S(6)} %copy.9.tiers_ref, s32[32]{0:T(128)} %order_ref.1, s32[1]{0:T(128)} %bitcast.5.me_ref, bf16[128,2048]{1,0:T(8,128)(2,1)} %shard_map.83.q_ref, bf16[2048,1024]{1,0:T(8,128)(2,1)} %all-gather.2.cloned.1.call-done.ka_ref.va_ref.kb_ref.vb_ref, ...), custom_call_target="tpu_custom_call" | custom-call | flops 2147483648 | bytes 6815744 | tf_op jit(solution)/shard_map/pallas_call | solution.py:167
  78.9 1.3 %convert_bitcast_fusion = f16[1,128,2048]{2,1,0:T(8,128)(2,1)S(1)} fusion(f32[128,2048]{1,0:T(8,128)} %shard_map.84), kind=kLoop, calls=%fused_computation.1 | loop fusion | flops 262144 | bytes 1572864 | tf_op jit(solution)/shard_map/broadcast_in_dim | solution.py:232
  80.1 2.9 %collective-permute-start.1 = (f16[1,128,2048]{2,1,0:T(8,128)(2,1)S(1)}, f16[1,128,2048]{2,1,0:T(8,128)(2,1)S(1)}, u32[]{:S(2)}, u32[]{:S(2)}) collective-permute-start(f16[1,128,2048]{2,1,0:T(8,128)(2,1)S(1)} %convert_bitcast_fusion), channel_id=1, source_target_pairs={{752,0},{0,16},{16,32},{32,48},{48,64},{64,80},{80,96},{96,112},{1... | collective-permute-start | bytes 1572872 | tf_op jit(solution)/shard_map/ppermute | solution.py:18
  83.1 17.7 %collective-permute-done.1 = f16[1,128,2048]{2,1,0:T(8,128)(2,1)S(1)} collective-permute-done((f16[1,128,2048]{2,1,0:T(8,128)(2,1)S(1)}, f16[1,128,2048]{2,1,0:T(8,128)(2,1)S(1)}, u32[]{:S(2)}, u32[]{:S(2)}) %collective-permute-start.1) | collective-permute-done | bytes 524320 | tf_op jit(solution)/shard_map/ppermute | solution.py:18
  100.8 1.1 %convert_add_fusion = f32[1,128,2048]{2,1,0:T(8,128)} fusion(f32[1,128,2048]{2,1,0:T(8,128)S(1)} %collective-permute-done, f16[1,128,2048]{2,1,0:T(8,128)(2,1)S(1)} %collective-permute-done.1), kind=kLoop, calls=%fused_computation | loop fusion | flops 524288 | bytes 2621440 | tf_op jit(solution)/shard_map/add | solution.py:232
Async XLA Ops:
  6.5 60.6 %all-gather.2.cloned.1.call-start = ((), (), s32[]{:S(2)}) async-start(), calls=%async_computation | async-start | bytes 4456448 | tf_op jit(solution)/shard_map/all_gather | solution.py:219
  6.5 5.0 %copy-start = (f32[1,128,2048]{2,1,0:T(8,128)S(1)}, f32[1,128,2048]{2,1,0:T(8,128)}, u32[]{:S(2)}) copy-start(f32[1,128,2048]{2,1,0:T(8,128)} %param.8) | copy-start | bytes 3145732
  11.5 40.2 %collective-permute-start = (f32[1,128,2048]{2,1,0:T(8,128)S(1)}, f32[1,128,2048]{2,1,0:T(8,128)S(1)}, u32[]{:S(2)}, u32[]{:S(2)}) collective-permute-start(f32[1,128,2048]{2,1,0:T(8,128)S(1)} %copy-done), channel_id=1, source_target_pairs={{752,0},{0,16},{16,32},{32,48},{48,64},{64,80},{80,96},{96,112},{1... | collective-permute-start | bytes 3145736 | tf_op jit(solution)/shard_map/ppermute | solution.py:18
  80.1 20.6 %collective-permute-start.1 = (f16[1,128,2048]{2,1,0:T(8,128)(2,1)S(1)}, f16[1,128,2048]{2,1,0:T(8,128)(2,1)S(1)}, u32[]{:S(2)}, u32[]{:S(2)}) collective-permute-start(f16[1,128,2048]{2,1,0:T(8,128)(2,1)S(1)} %convert_bitcast_fusion), channel_id=1, source_target_pairs={{752,0},{0,16},{16,32},{32,48},{48,64},{64,80},{80,96},{96,112},{1... | collective-permute-start | bytes 1572872 | tf_op jit(solution)/shard_map/ppermute | solution.py:18
Sparse Core Ops, SparseCore 0:
  11.6 55.4 all-gather.1

commit v13 on v11

--- a/solution.py
+++ b/solution.py
@@ -69,7 +69,7 @@
         mixed = jnp.dot(
             p_a.astype(jnp.bfloat16), va, preferred_element_type=jnp.float32
         ) + jnp.dot(p_b.astype(jnp.bfloat16), vb, preferred_element_type=jnp.float32)
-        mixed = mixed / total
+        mixed = mixed * (1.0 / total)
         out_ref[:, cols] = jnp.where(gate, w_ref[:, cols] * mixed, 0.0).astype(out_ref.dtype)
 
 

time: 108 us -> 108 us (level)
  no operation moved by 1% of the time
where the time goes in v13:
time: 108 us
  waiting for transfers between devices  66.2 us (61%)
  Pallas kernels  18.4 us (17%)
  between operations  14.1 us (13%)
  starting transfers between devices  6.87 us (6%)
  other arithmetic  2.37 us (2%)
    ppermute x2, waiting for transfers between devices, passed_along(): return lax.ppermute(block, axis, route)  50.7 us
    all_gather x1, waiting for transfers between devices, local(): gathered = lax.all_gather(own_block, 'ctx', axis=0, tiled=True)  15.4 us
    pallas_call x1, Pallas kernels, attend_and_update(): pl.pallas_call(attention_kernel, grid=(kv_heads,), in_specs=[smem, smem,...  11.7 us
    ppermute x2, starting transfers between devices, passed_along(): return lax.ppermute(block, axis, route)  6.87 us
    pallas_call x1, Pallas kernels, prologue(): pl.pallas_call(key_value_kernel, out_shape=jax.ShapeDtypeStruct((rows, 2...  4.16 us
    pallas_call x1, Pallas kernels, prologue(): pl.pallas_call(query_kernel, out_shape=jax.ShapeDtypeStruct((rows, width)...  2.54 us
  transfers between devices with their start and end apart: 3, of which 3 were waited for; matrix products, arithmetic and copies ran while one was open for 0% of the time, Pallas kernels for 2%

profile of v13, /device:TPU:1, one launch (start us, length us, event | category | flops | bytes accessed | tf_op | source)
XLA Modules:
  0.0 107.9 jit_solution(3293462518188347325)
XLA Ops:
  6.5 0.0 all-gather.2.cloned.1.call-start
  6.5 0.0 copy-start
  6.5 4.2 %shard_map.82 = bf16[128,1024]{1,0:T(8,128)(2,1)} custom-call(f32[128,2048]{1,0:T(8,128)} %bitcast.9, f32[1,2048]{1,0:T(1,128)} %bitcast.13, bf16[2048,512]{1,0:T(8,128)(2,1)} %bitcast.11, bf16[2048,512]{1,0:T(8,128)(2,1)} %bitcast.12), custom_call_target="tpu_custom_call" | custom-call | flops 536870912 | bytes 5505024 | tf_op jit(solution)/shard_map/pallas_call | solution.py:105
  10.7 0.0 all-gather.2.cloned.1.call-update
  10.7 0.0 copy-done
  10.7 4.0 %collective-permute-start = (f32[1,128,2048]{2,1,0:T(8,128)S(1)}, f32[1,128,2048]{2,1,0:T(8,128)S(1)}, u32[]{:S(2)}, u32[]{:S(2)}) collective-permute-start(f32[1,128,2048]{2,1,0:T(8,128)S(1)} %copy-done), channel_id=1, source_target_pairs={{752,0},{0,16},{16,32},{32,48},{48,64},{64,80},{80,96},{96,112},{1... | collective-permute-start | bytes 3145736 | tf_op jit(solution)/shard_map/ppermute | solution.py:18
  15.4 2.5 %shard_map.83.q_ref = bf16[128,2048]{1,0:T(8,128)(2,1)} custom-call(f32[128,2048]{1,0:T(8,128)} %bitcast.10, f32[1,2048]{1,0:T(1,128)} %bitcast.14), custom_call_target="tpu_custom_call" | custom-call | flops 2097152 | bytes 1572864 | tf_op jit(solution)/shard_map/pallas_call | solution.py:114
  17.9 33.0 %collective-permute-done = f32[1,128,2048]{2,1,0:T(8,128)S(1)} collective-permute-done((f32[1,128,2048]{2,1,0:T(8,128)S(1)}, f32[1,128,2048]{2,1,0:T(8,128)S(1)}, u32[]{:S(2)}, u32[]{:S(2)}) %collective-permute-start) | collective-permute-done | bytes 1048608 | tf_op jit(solution)/shard_map/ppermute | solution.py:18
  50.9 15.4 %all-gather.2.cloned.1.call-done.ka_ref.va_ref.kb_ref.vb_ref = bf16[2048,1024]{1,0:T(8,128)(2,1)} async-done(((bf16[128,1024]{1,0:T(8,128)(2,1)}), bf16[2048,1024]{1,0:T(8,128)(2,1)}) %all-gather.2.cloned.1.call-update) | async-done | bytes 4194320 | tf_op jit(solution)/shard_map/all_gather | solution.py:189
  66.3 11.7 %shard_map.84 = f32[128,2048]{1,0:T(8,128)} custom-call(f32[16]{0:T(128)} %bitcast.16, s32[1]{0:T(128)S(6)} %copy.9.tiers_ref, s32[32]{0:T(128)} %order_ref.1, s32[1]{0:T(128)} %bitcast.5.me_ref, bf16[128,2048]{1,0:T(8,128)(2,1)} %shard_map.83.q_ref, bf16[2048,1024]{1,0:T(8,128)(2,1)} %all-gather.2.cloned.1.call-done.ka_ref.va_ref.kb_ref.vb_ref, ...), custom_call_target="tpu_custom_call" | custom-call | flops 2147483648 | bytes 6815744 | tf_op jit(solution)/shard_map/pallas_call | solution.py:137
  78.1 1.3 %convert_bitcast_fusion = f16[1,128,2048]{2,1,0:T(8,128)(2,1)S(1)} fusion(f32[128,2048]{1,0:T(8,128)} %shard_map.84), kind=kLoop, calls=%fused_computation.1 | loop fusion | flops 262144 | bytes 1572864 | tf_op jit(solution)/shard_map/broadcast_in_dim | solution.py:202
  79.4 2.9 %collective-permute-start.1 = (f16[1,128,2048]{2,1,0:T(8,128)(2,1)S(1)}, f16[1,128,2048]{2,1,0:T(8,128)(2,1)S(1)}, u32[]{:S(2)}, u32[]{:S(2)}) collective-permute-start(f16[1,128,2048]{2,1,0:T(8,128)(2,1)S(1)} %convert_bitcast_fusion), channel_id=1, source_target_pairs={{752,0},{0,16},{16,32},{32,48},{48,64},{64,80},{80,96},{96,112},{1... | collective-permute-start | bytes 1572872 | tf_op jit(solution)/shard_map/ppermute | solution.py:18
  82.3 17.7 %collective-permute-done.1 = f16[1,128,2048]{2,1,0:T(8,128)(2,1)S(1)} collective-permute-done((f16[1,128,2048]{2,1,0:T(8,128)(2,1)S(1)}, f16[1,128,2048]{2,1,0:T(8,128)(2,1)S(1)}, u32[]{:S(2)}, u32[]{:S(2)}) %collective-permute-start.1) | collective-permute-done | bytes 524320 | tf_op jit(solution)/shard_map/ppermute | solution.py:18
  100.0 1.1 %convert_add_fusion = f32[1,128,2048]{2,1,0:T(8,128)} fusion(f32[1,128,2048]{2,1,0:T(8,128)S(1)} %collective-permute-done, f16[1,128,2048]{2,1,0:T(8,128)(2,1)S(1)} %collective-permute-done.1), kind=kLoop, calls=%fused_computation | loop fusion | flops 524288 | bytes 2621440 | tf_op jit(solution)/shard_map/add | solution.py:202
Async XLA Ops:
  6.5 59.8 %all-gather.2.cloned.1.call-start = ((), (), s32[]{:S(2)}) async-start(), calls=%async_computation | async-start | bytes 4456448 | tf_op jit(solution)/shard_map/all_gather | solution.py:189
  6.5 4.2 %copy-start = (f32[1,128,2048]{2,1,0:T(8,128)S(1)}, f32[1,128,2048]{2,1,0:T(8,128)}, u32[]{:S(2)}) copy-start(f32[1,128,2048]{2,1,0:T(8,128)} %param.8) | copy-start | bytes 3145732
  10.7 40.2 %collective-permute-start = (f32[1,128,2048]{2,1,0:T(8,128)S(1)}, f32[1,128,2048]{2,1,0:T(8,128)S(1)}, u32[]{:S(2)}, u32[]{:S(2)}) collective-permute-start(f32[1,128,2048]{2,1,0:T(8,128)S(1)} %copy-done), channel_id=1, source_target_pairs={{752,0},{0,16},{16,32},{32,48},{48,64},{64,80},{80,96},{96,112},{1... | collective-permute-start | bytes 3145736 | tf_op jit(solution)/shard_map/ppermute | solution.py:18
  79.4 20.6 %collective-permute-start.1 = (f16[1,128,2048]{2,1,0:T(8,128)(2,1)S(1)}, f16[1,128,2048]{2,1,0:T(8,128)(2,1)S(1)}, u32[]{:S(2)}, u32[]{:S(2)}) collective-permute-start(f16[1,128,2048]{2,1,0:T(8,128)(2,1)S(1)} %convert_bitcast_fusion), channel_id=1, source_target_pairs={{752,0},{0,16},{16,32},{32,48},{48,64},{64,80},{80,96},{96,112},{1... | collective-permute-start | bytes 1572872 | tf_op jit(solution)/shard_map/ppermute | solution.py:18
Sparse Core Ops, SparseCore 0:
  10.8 55.4 all-gather.1
